TPU v7x, 256 devices: a whole 4x4x8 slice. The times are simulated.
256 devices in a mesh: tile: 64 (over x, z, core), row: 4 (over y).
Axes of the slice: x: 4, y: 4, z: 8, core: 2. Of those that a mesh axis runs over, the one named last changes fastest.
Arguments:
- amplitudes: float32 [576, 64, 256], P('tile'), may hold values from -6 to 6
- integrals: float32 [4, 4096, 128, 256], P('row', 'tile'), may hold values from -0.0390625 to 0.0390625
- slot_ab: int32 [4, 4096], P('row', 'tile'), may hold values from 0 to 17
- slot_cd: int32 [4, 4096], P('row', 'tile'), may hold values from 0 to 575, as said below
- live_count: int32 [4, 64], P('row', 'tile'), may hold values from 1 to 64, as said below
- pair_list: int32 [64, 2], replicated, may hold values from 0 to 127, as said below
Outputs:
- symmetrized: float32 [64, 96, 96], P('tile', 'row')
Inputs may be any that keep to these rules, and one draw needn't show every extreme that they name: `slot_cd`: slot s of row index r belongs to tile index k = s // 64; its cd tile is held in amplitudes by tile index k - 1, k or k + 1, taken cyclically over the tile axis (cd tile c is held by tile index c // 9). `live_count`: slots at or after a device's count are unused. In every row index some device uses all 64 slots. `pair_list`: the rows are distinct pairs (i, j) with i != j, and for every row the reversed pair (j, i) is also a row.
All inputs are finite; a program needn't handle non-finite values.
Results may differ from a plain program's by a relative error of at most 0.0003.
Values sent between devices are 32-bit elements; how exact they have to be, the bound alone decides.
No kernel may reach another device: no remote copies, remote signals or barrier semaphores. Data moves between devices by JAX's collectives and lax.ppermute only.
A program may use at most 64 MiB of HBM per device.

v0:
```python
import jax
import jax.numpy as jnp
from jax import lax
from jax.sharding import PartitionSpec as P

TS = 16
ATS = 8
SLAB = 96


def padded(x, sides, width):
    for axis, dim in sides:
        size, length = (lax.axis_size(axis), x.shape[dim])
        up = [(i, (i + 1) % size) for i in range(size)]
        down = [(j, i) for i, j in up]
        last = lax.slice_in_dim(x, length - width, length, axis=dim)
        first = lax.slice_in_dim(x, 0, width, axis=dim)
        before = lax.ppermute(last, axis, up)
        after = lax.ppermute(first, axis, down)
        x = jnp.concatenate([before, x, after], axis=dim)
    return x


def find_mirror(pair_list):
    first_orb = pair_list[:, 0]
    second = pair_list[:, 1]
    matches = (first_orb[:, None] == second[None, :]) & (second[:, None] == first_orb[None, :])
    columns = jnp.arange(pair_list.shape[0], dtype=jnp.int32)
    return jnp.sum(jnp.where(matches, columns[None, :], 0), axis=1)


def to_grid(totals, a_tiles, b_tiles):
    pair_count = totals.shape[1]
    shaped = totals.reshape(a_tiles, b_tiles, pair_count, ATS, TS)
    return jnp.transpose(shaped, (2, 0, 3, 1, 4)).reshape(pair_count, a_tiles * ATS, b_tiles * TS)


def shards(amplitudes, integrals, slot_ab, slot_cd, live_count, pair_list):
    highest = lax.Precision.HIGHEST
    tile_size = lax.axis_size("tile")
    row_size = lax.axis_size("row")
    tile_index = lax.axis_index("tile")
    shard_tiles = amplitudes.shape[0]
    pair_count = amplitudes.shape[1]
    extended = padded(amplitudes, (("tile", 0),), shard_tiles)
    blocks_all = integrals[0]
    ab_local = slot_ab[0]
    cd_global = slot_cd[0]
    owner_tile = cd_global // shard_tiles
    offset = (owner_tile - tile_index + 1 + tile_size) % tile_size
    ext_index = offset * shard_tiles + cd_global % shard_tiles
    live_total = live_count[0, 0]
    a_tiles = SLAB // (row_size * ATS)
    b_tiles = SLAB // TS
    tiles_ab = a_tiles * b_tiles
    block_width = integrals.shape[2]
    group_size = 8

    def block_step(block_index, totals):
        first_slot = block_index * group_size
        picked = lax.dynamic_slice_in_dim(ext_index, first_slot, group_size)
        ab_tiles = lax.dynamic_slice_in_dim(ab_local, first_slot, group_size)
        blocks = lax.dynamic_slice_in_dim(blocks_all, first_slot, group_size, 0)
        live_mask = (first_slot + jnp.arange(group_size, dtype=jnp.int32) < live_total).astype(
            jnp.float32
        )
        amp_tiles = jnp.take(extended, picked, axis=0)
        products = jnp.einsum(
            "spw,sbw->spb", amp_tiles, blocks, precision=highest, preferred_element_type=jnp.float32
        )
        one_hot = (ab_tiles[:, None] == jnp.arange(tiles_ab, dtype=jnp.int32)[None, :]).astype(
            jnp.float32
        ) * live_mask[:, None]
        return totals + jnp.einsum(
            "se,spb->epb", one_hot, products, precision=highest, preferred_element_type=jnp.float32
        )

    turn_count = (live_total + group_size - 1) // group_size
    start_totals = jnp.zeros((tiles_ab, pair_count, block_width), jnp.float32)
    totals = lax.fori_loop(0, turn_count, block_step, start_totals)
    whole_term = to_grid(totals, a_tiles, b_tiles)
    mirror = find_mirror(pair_list)
    reduced = lax.psum_scatter(whole_term, "tile", scatter_dimension=0, tiled=True)
    exchanged = lax.all_to_all(reduced, "row", split_axis=2, concat_axis=1, tiled=True)
    turned = jnp.transpose(exchanged, (0, 2, 1))
    everyone = lax.all_gather(turned, "tile", axis=0, tiled=True)
    local_pairs = reduced.shape[0]
    wanted = lax.dynamic_slice_in_dim(mirror, tile_index * local_pairs, local_pairs)
    return reduced + jnp.take(everyone, wanted, axis=0)


def solution(mesh):
    return jax.shard_map(
        shards,
        mesh=mesh,
        in_specs=(
            P("tile", None, None),
            P("row", "tile", None, None),
            P("row", "tile"),
            P("row", "tile"),
            P("row", "tile"),
            P(),
        ),
        out_specs=P("tile", "row", None),
        check_vma=False,
    )
```

profile of v0, /device:TPU:32, one launch (start us, length us, event | category | flops | bytes accessed | tf_op | source)
XLA Modules:
  0.0 265.3 jit_solution(6142205821760800485)
XLA Ops:
  6.5 1.7 collective-permute-start.1
  9.0 0.7 fusion.16
  9.6 6.4 %collective-permute-done = f32[9,64,256]{2,1,0:T(8,128)S(1)} collective-permute-done((f32[9,64,256]{2,1,0:T(8,128)}, f32[9,64,256]{2,1,0:T(8,128)S(1)}, u32[]{:S(2)}, u32[]{:S(2)}) %collective-permute-start) | collective-permute-done | bytes 589856 | tf_op jit(solution)/shard_map/ppermute | solution.py:18
  16.1 1.2 pad_maximum_fusion
  17.4 9.9 %while.11 = (s32[]{:T(128)}, f32[18,64,128]{2,0,1:T(8,128)S(1)}, s32[]{:T(128)}, s32[64]{0:T(128)S(1)}, s32[]{:T(128)}, /*index=5*/s32[64]{0:T(128)S(1)}, f32[27...) while((s32[]{:T(128)}, f32[18,64,128]{2,0,1:T(8,128)S(1)}, ...), condition=%wide.region_1.2_spmd, body=%wide.region_0.1_spmd.sunk | while | flops 215762288 | bytes 4329959 | solution.py:80
  17.4 0.7 compare_and_fusion.2
  18.1 0.6 gather_fusion
  18.7 2.5 fusion.28
  21.3 1.0 convolution_add_fusion.2
  22.3 0.7 compare_and_fusion.2
  23.1 0.6 gather_fusion
  23.7 2.5 fusion.28
  26.3 1.0 convolution_add_fusion.2
  27.8 1.2 copy.29
  29.1 165.2 %reduce-scatter.4.cloned.1.call-done = f32[1,24,96]{2,1,0:T(8,128)} async-done(((f32[64,24,96]{2,1,0:T(8,128)}), f32[1,24,96]{2,1,0:T(8,128)}) %reduce-scatter.4.cloned.1.call-update) | async-done | bytes 9232
  194.3 0.8 copy.30
  195.6 0.7 reduce
  196.3 0.7 reshape.79
  197.0 4.2 %all-to-all-start = ((f32[4,1,576]{2,1,0:T(1,128)}), f32[4,1,576]{2,1,0:T(1,128)S(1)}, u32[]{:S(2)}, u32[]{:S(2)}) async-start(f32[4,1,576]{2,1,0:T(1,128)} %reshape.79), calls=%async_computation | async-start | bytes 20480 | tf_op jit(solution)/shard_map/all_to_all | solution.py:84
  201.4 0.7 dynamic_slice.12
  204.0 2.6 all-to-all-done
  206.6 0.6 reduce.1
  207.6 49.5 %all_gather.3 = f32[64,24,96]{2,1,0:T(8,128)S(1)} all-gather(f32[1,24,96]{2,1,0:T(8,128)S(1)} %bitcast.48), channel_id=1, replica_groups=mesh['tile'=64,'row'=4] {'tile'}, dimensions={0}, use_global_device_ids=true | all-gather | bytes 599040 | tf_op jit(solution)/shard_map/all_gather | solution.py:86
  257.1 1.3 fusion.14
  (22 shorter events, 1.9 us)
Async XLA Ops:
  6.5 187.8 %reduce-scatter.4.cloned.1.call-start = ((), (), s32[]{:S(2)}) async-start(), calls=%async_computation.2 | async-start | bytes 798720
  6.5 9.5 %collective-permute-start = (f32[9,64,256]{2,1,0:T(8,128)}, f32[9,64,256]{2,1,0:T(8,128)S(1)}, u32[]{:S(2)}, u32[]{:S(2)}) collective-permute-start(f32[9,64,256]{2,1,0:T(8,128)} %param.8), channel_id=1, source_target_pairs={{0,4},{4,8},{8,12},{12,16},{16,20},{20,24},{24,28},{28,32},{32,36}... | collective-permute-start | bytes 1769480 | tf_op jit(solution)/shard_map/ppermute | solution.py:18
  6.5 9.5 %collective-permute-start.1 = (f32[9,64,256]{2,1,0:T(8,128)}, f32[9,64,256]{2,1,0:T(8,128)S(1)}, u32[]{:S(2)}, u32[]{:S(2)}) collective-permute-start(f32[9,64,256]{2,1,0:T(8,128)} %param.8), channel_id=1, source_target_pairs={{4,0},{8,4},{12,8},{16,12},{20,16},{24,20},{28,24},{32,28},{36,32}... | collective-permute-start | bytes 1769480 | tf_op jit(solution)/shard_map/ppermute | solution.py:19
  9.6 7.7 %copy-start.1 = (s32[1,64]{1,0:T(1,128)S(1)}, s32[1,64]{1,0:T(1,128)}, u32[]{:S(2)}) copy-start(s32[1,64]{1,0:T(1,128)} %param.10) | copy-start | bytes 772
  27.8 1.3 copy-start
  197.0 9.6 %all-to-all-start = ((f32[4,1,576]{2,1,0:T(1,128)}), f32[4,1,576]{2,1,0:T(1,128)S(1)}, u32[]{:S(2)}, u32[]{:S(2)}) async-start(f32[4,1,576]{2,1,0:T(1,128)} %reshape.79), calls=%async_computation | async-start | bytes 20480 | tf_op jit(solution)/shard_map/all_to_all | solution.py:84
Sparse Core Ops, SparseCore 0:
  29.2 165.0 reduce-scatter.3
where the time goes:
time: 268 us; the launch traced here: 265 us
  waiting for transfers between devices  174 us (65%)
  blocking collectives  49.5 us (18%)
  between operations  16.1 us (6%)
  matrix products  7.07 us (3%)
  local copies, waits for them, and re-layouts  6.21 us (2%)
  other arithmetic  6.12 us (2%)
  starting transfers between devices  5.98 us (2%)
    unnamed x2, waiting for transfers between devices  165 us
    all_gather x1, blocking collectives, shards(): everyone = lax.all_gather(turned, 'tile', axis=0, tiled=True)  49.5 us
    ppermute x1, waiting for transfers between devices, padded(): before = lax.ppermute(last, axis, up)  6.41 us
  transfers between devices with their start and end apart: 4, of which 3 were waited for; matrix products, arithmetic and copies ran while one was open for 1% of the time, Pallas kernels for 0%

commit v1 on v0

--- a/solution.py
+++ b/solution.py
@@ -1,7 +1,7 @@
 import jax
 import jax.numpy as jnp
 from jax import lax
-from jax.sharding import PartitionSpec as P
+from jax.sharding import Mesh, PartitionSpec as P
 
 TS = 16
 ATS = 8
@@ -37,12 +37,12 @@
 
 def shards(amplitudes, integrals, slot_ab, slot_cd, live_count, pair_list):
     highest = lax.Precision.HIGHEST
-    tile_size = lax.axis_size("tile")
+    tile_size = lax.axis_size(TILE)
     row_size = lax.axis_size("row")
-    tile_index = lax.axis_index("tile")
+    tile_index = lax.axis_index(TILE)
     shard_tiles = amplitudes.shape[0]
     pair_count = amplitudes.shape[1]
-    extended = padded(amplitudes, (("tile", 0),), shard_tiles)
+    extended = padded(amplitudes, ((TILE, 0),), shard_tiles)
     blocks_all = integrals[0]
     ab_local = slot_ab[0]
     cd_global = slot_cd[0]
@@ -80,27 +80,49 @@
     totals = lax.fori_loop(0, turn_count, block_step, start_totals)
     whole_term = to_grid(totals, a_tiles, b_tiles)
     mirror = find_mirror(pair_list)
-    reduced = lax.psum_scatter(whole_term, "tile", scatter_dimension=0, tiled=True)
-    exchanged = lax.all_to_all(reduced, "row", split_axis=2, concat_axis=1, tiled=True)
+    mirrored = jnp.take(whole_term, mirror, axis=0)
+    both = jnp.stack([whole_term, mirrored], axis=1)
+    reduced = reduce_over_tile(both)
+    own = reduced[:, 0]
+    exchanged = lax.all_to_all(reduced[:, 1], "row", split_axis=2, concat_axis=1, tiled=True)
     turned = jnp.transpose(exchanged, (0, 2, 1))
-    everyone = lax.all_gather(turned, "tile", axis=0, tiled=True)
-    local_pairs = reduced.shape[0]
-    wanted = lax.dynamic_slice_in_dim(mirror, tile_index * local_pairs, local_pairs)
-    return reduced + jnp.take(everyone, wanted, axis=0)
+    return own + turned
+
+
+def reduce_over_tile(x):
+    chips = lax.axis_size(CHIPS)
+    cores = lax.axis_size("c")
+    shaped = x.reshape((chips, cores) + x.shape[1:])
+    core = lax.axis_index("c")
+    mine = jnp.take(shaped, core, axis=1)
+    other = jnp.take(shaped, 1 - core, axis=1)
+    summed = mine + lax.ppermute(other, "c", [(0, 1), (1, 0)])
+    spread = lax.all_to_all(summed, CHIPS, 0, 0, tiled=True)
+    return jnp.sum(spread, axis=0, keepdims=True)
+
+
+CHIPS = ("x", "z")
+TILE = ("x", "z", "c")
 
 
 def solution(mesh):
+    tile_size = mesh.shape["tile"]
+    row_size = mesh.shape["row"]
+    cores = 2
+    split = Mesh(
+        mesh.devices.reshape(4, tile_size // (4 * cores), cores, row_size), ("x", "z", "c", "row")
+    )
     return jax.shard_map(
         shards,
-        mesh=mesh,
+        mesh=split,
         in_specs=(
-            P("tile", None, None),
-            P("row", "tile", None, None),
-            P("row", "tile"),
-            P("row", "tile"),
-            P("row", "tile"),
+            P(TILE, None, None),
+            P("row", TILE, None, None),
+            P("row", TILE),
+            P("row", TILE),
+            P("row", TILE),
             P(),
         ),
-        out_specs=P("tile", "row", None),
+        out_specs=P(TILE, "row", None),
         check_vma=False,
     )

time: 268 us -> 114 us (0.43)
  waiting for transfers between devices: 174 us -> 7.21 us
  blocking collectives: 49.5 us -> 68.2 us
  between operations: 16.1 us -> 0.87 us
  local copies, waits for them, and re-layouts: 6.21 us -> 15.4 us
  matrix products: 7.07 us -> 10.6 us
    unnamed x2 -> x0, waiting for transfers between devices: 165 us -> none
    all_to_all x0 -> x2, blocking collectives: none -> 68.2 us  [the longest x1 58.3 us: reduce_over_tile(): spread = lax.all_to_all(summed, CHIPS, 0, 0, tiled=True)]
    all_gather x1 -> x0, blocking collectives: 49.5 us -> none  [shards(): everyone = lax.all_gather(turned, 'tile', axis=0, tiled=True)]
    transpose x1 -> x2, local copies, waits for them, and re-layouts: 0.14 us -> 6.02 us  [to_grid(): jnp.transpose(shaped, (2, 0, 3, 1, 4))]
    all_to_all x1 -> x0, starting transfers between devices: 4.23 us -> none  [shards(): lax.all_to_all(reduced, 'row', split_axis=2, concat_axis=1, tiled=True)]
    another operation x0 -> x1, local copies, waits for them, and re-layouts: none -> 4.06 us  [shards(): both = jnp.stack([whole_term, mirrored], axis=1)]
    dot_general x2 -> x3, matrix products: 5.06 us -> 7.57 us  [block_step(): jnp.einsum('spw,sbw->spb', amp_tiles, blocks, precision=highest, preferre...]
  transfers between devices with their start and end apart: 4 -> 3, of which waited for: 3 -> 2; matrix products, arithmetic and copies ran while one was open for 1% -> 2% of each run, Pallas kernels for 0% -> 0%
where the time goes in v1:
time: 114 us; the launch traced here: 113 us
  blocking collectives  68.2 us (60%)
  local copies, waits for them, and re-layouts  15.4 us (14%)
  matrix products  10.6 us (9%)
  waiting for transfers between devices  7.21 us (6%)
  other arithmetic  6.72 us (6%)
  starting transfers between devices  3.86 us (3%)
    all_to_all x1, blocking collectives, reduce_over_tile(): spread = lax.all_to_all(summed, CHIPS, 0, 0, tiled=True)  58.3 us
    all_to_all x1, blocking collectives, shards(): lax.all_to_all(reduced[:, 1], 'row', split_axis=2, concat_axis=1, tiled=T...  9.86 us
    dot_general x3, matrix products, block_step(): jnp.einsum('spw,sbw->spb', amp_tiles, blocks, precision=highest, preferre...  7.57 us
    transpose x2, local copies, waits for them, and re-layouts, to_grid(): jnp.transpose(shaped, (2, 0, 3, 1, 4))  6.02 us
    ppermute x1, waiting for transfers between devices, padded(): before = lax.ppermute(last, axis, up)  5.3 us
    another operation x1, local copies, waits for them, and re-layouts, shards(): both = jnp.stack([whole_term, mirrored], axis=1)  4.06 us
    dot_general x3, matrix products, block_step(): jnp.einsum('se,spb->epb', one_hot, products, precision=highest, preferred...  3 us
  transfers between devices with their start and end apart: 3, of which 2 were waited for; matrix products, arithmetic and copies ran while one was open for 2% of the time, Pallas kernels for 0%

profile of v1, /device:TPU:32, one launch (start us, length us, event | category | flops | bytes accessed | tf_op | source)
XLA Modules:
  0.0 112.9 jit_solution(6461695093040221904)
XLA Ops:
  0.0 1.7 %collective-permute-start.1 = (f32[9,64,256]{2,1,0:T(8,128)}, f32[9,64,256]{2,1,0:T(8,128)S(1)}, u32[]{:S(2)}, u32[]{:S(2)}) collective-permute-start(f32[9,64,256]{2,1,0:T(8,128)} %param.10), channel_id=1, source_target_pairs={{4,0},{8,4},{12,8},{16,12},{20,16},{24,20},{28,24},{32,28},{36,32}... | collective-permute-start | bytes 1769480 | tf_op jit(solution)/shard_map/ppermute | solution.py:19
  1.7 0.8 slice_bitcast_fusion.2
  3.5 0.7 fusion.24
  4.2 5.3 %collective-permute-done = f32[9,64,256]{2,1,0:T(8,128)S(1)} collective-permute-done((f32[9,64,256]{2,1,0:T(8,128)}, f32[9,64,256]{2,1,0:T(8,128)S(1)}, u32[]{:S(2)}, u32[]{:S(2)}) %collective-permute-start) | collective-permute-done | bytes 589856 | tf_op jit(solution)/shard_map/ppermute | solution.py:18
  9.5 1.2 %pad_maximum_fusion = f32[27,64,256]{2,1,0:T(8,128)S(1)} fusion(f32[9,64,256]{2,1,0:T(8,128)S(1)} %collective-permute-done.1, f32[9,64,256]{2,1,0:T(8,128)} %param.10, f32[9,64,256]{2,1,0:T(8,128)S(1)} %collective-permute-done), kind=kLoop, calls=%fused_computation.26 | loop fusion | flops 884736 | bytes 3538944 | tf_op jit(solution)/shard_map/concatenate | solution.py:20
  10.8 14.9 %while.11 = (s32[]{:T(128)}, f32[18,64,128]{2,0,1:T(8,128)S(1)}, s32[]{:T(128)}, s32[64]{0:T(128)S(1)}, s32[]{:T(128)}, /*index=5*/s32[64]{0:T(128)S(1)}, f32[27...) while((s32[]{:T(128)}, f32[18,64,128]{2,0,1:T(8,128)S(1)}, ...), condition=%wide.region_1.2_spmd, body=%wide.region_0.1_spmd.sunk | while | flops 215762288 | bytes 4329959 | solution.py:80
  10.8 0.7 compare_and_fusion.3
  12.2 2.5 %fusion.37 = f32[8,64,128]{2,1,0:T(8,128)S(1)} fusion(f32[64,128,256]{2,1,0:T(8,128)} %get-tuple-element.169, s32[]{:T(128)S(6)} %select_n.124, f32[8,64,256]{2,1,0:T(8,128)S(1)} %gather_fusion, pred[8]{0:T(512)(128)(4,1)S(1)} %get-tuple-element.136), kind=kOutput, calls=%fused_computation.3.clone.1 | convolution fusion | flops 201457664 | bytes 1835020 | tf_op jit(solution)/shard_map/while/body/spw,sbw->spb/dot_general | solution.py:68
  14.8 1.0 convolution_add_fusion.2
  15.8 0.7 compare_and_fusion.3
  17.1 2.5 %fusion.37 = f32[8,64,128]{2,1,0:T(8,128)S(1)} fusion(f32[64,128,256]{2,1,0:T(8,128)} %get-tuple-element.169, s32[]{:T(128)S(6)} %select_n.124, f32[8,64,256]{2,1,0:T(8,128)S(1)} %gather_fusion, pred[8]{0:T(512)(128)(4,1)S(1)} %get-tuple-element.136), kind=kOutput, calls=%fused_computation.3.clone.1 | convolution fusion | flops 201457664 | bytes 1835020 | tf_op jit(solution)/shard_map/while/body/spw,sbw->spb/dot_general | solution.py:68
  19.7 1.0 convolution_add_fusion.2
  20.8 0.7 compare_and_fusion.3
  22.1 2.5 %fusion.37 = f32[8,64,128]{2,1,0:T(8,128)S(1)} fusion(f32[64,128,256]{2,1,0:T(8,128)} %get-tuple-element.169, s32[]{:T(128)S(6)} %select_n.124, f32[8,64,256]{2,1,0:T(8,128)S(1)} %gather_fusion, pred[8]{0:T(512)(128)(4,1)S(1)} %get-tuple-element.136), kind=kOutput, calls=%fused_computation.3.clone.1 | convolution fusion | flops 201457664 | bytes 1835020 | tf_op jit(solution)/shard_map/while/body/spw,sbw->spb/dot_general | solution.py:68
  24.7 1.0 convolution_add_fusion.2
  26.2 5.9 %copy.43 = f32[64,3,8,6,16]{4,3,2,1,0:T(8,128)} copy(f32[64,3,8,6,16]{0,4,2,3,1:T(8,128)S(1)} %bitcast.69) | data formatting | bytes 1179648 | tf_op jit(solution)/shard_map/transpose | solution.py:35
  32.5 4.1 %stack.6 = f32[32,2,1,24,96]{4,3,1,0,2:T(8,128)S(1)} reshape(f32[64,3,8,6,16]{4,3,2,1,0:T(8,128)} %copy.43) | data formatting | bytes 1179648 | tf_op jit(solution)/shard_map/stack | solution.py:84
  36.6 0.6 gather_fusion.1
  37.5 2.1 %collective-permute-start.2 = (f32[32,2,24,96]{3,2,0,1:T(8,128)S(1)}, f32[32,2,24,96]{3,2,0,1:T(8,128)S(1)}, u32[]{:S(2)}, u32[]{:S(2)}) collective-permute-start(f32[32,2,24,96]{3,2,0,1:T(8,128)S(1)} %fusion.16), channel_id=1, source_target_pairs={{0,4},{4,0},{1,5},{5,1},{2,6},{6,2},{3,7},{7,3},{8,12},{12,8},{9,1... | collective-permute-start | bytes 1769480 | tf_op jit(solution)/shard_map/ppermute | solution.py:99
  39.6 1.9 %collective-permute-done.2 = f32[32,2,24,96]{3,2,0,1:T(8,128)S(1)} collective-permute-done((f32[32,2,24,96]{3,2,0,1:T(8,128)S(1)}, f32[32,2,24,96]{3,2,0,1:T(8,128)S(1)}, u32[]{:S(2)}, u32[]{:S(2)}) %collective-permute-start.2) | collective-permute-done | bytes 589856 | tf_op jit(solution)/shard_map/ppermute | solution.py:99
  41.6 58.3 %all_to_all.23 = f32[32,2,24,96]{3,2,1,0:T(8,128)S(1)} all-to-all(f32[32,2,24,96]{3,2,1,0:T(8,128)S(1)} %copy.47), channel_id=1, replica_groups=mesh['x'=4,'z'=8,'c'=2,'row'=4] {'x','z'}, dimensions={0} | all-to-all | bytes 1179648 | tf_op jit(solution)/shard_map/all_to_all | solution.py:100
  100.6 0.8 reduce
  101.5 9.9 %all_to_all.24 = f32[4,1,576]{2,1,0:T(1,128)S(1)} all-to-all(f32[4,1,576]{2,1,0:T(1,128)S(1)} %reshape.144), channel_id=1, replica_groups=mesh['x'=4,'z'=8,'c'=2,'row'=4] {'row'}, dimensions={0} | all-to-all | bytes 18432 | tf_op jit(solution)/shard_map/all_to_all | solution.py:87
  111.4 0.7 reduce.1
  (35 shorter events, 5.3 us)
Async XLA Ops:
  0.0 9.5 %collective-permute-start = (f32[9,64,256]{2,1,0:T(8,128)}, f32[9,64,256]{2,1,0:T(8,128)S(1)}, u32[]{:S(2)}, u32[]{:S(2)}) collective-permute-start(f32[9,64,256]{2,1,0:T(8,128)} %param.10), channel_id=1, source_target_pairs={{0,4},{4,8},{8,12},{12,16},{16,20},{20,24},{24,28},{28,32},{32,36}... | collective-permute-start | bytes 1769480 | tf_op jit(solution)/shard_map/ppermute | solution.py:18
  0.0 9.5 %collective-permute-start.1 = (f32[9,64,256]{2,1,0:T(8,128)}, f32[9,64,256]{2,1,0:T(8,128)S(1)}, u32[]{:S(2)}, u32[]{:S(2)}) collective-permute-start(f32[9,64,256]{2,1,0:T(8,128)} %param.10), channel_id=1, source_target_pairs={{4,0},{8,4},{12,8},{16,12},{20,16},{24,20},{28,24},{32,28},{36,32}... | collective-permute-start | bytes 1769480 | tf_op jit(solution)/shard_map/ppermute | solution.py:19
  4.2 6.6 %copy-start = (s32[1,64]{1,0:T(1,128)S(1)}, s32[1,64]{1,0:T(1,128)}, u32[]{:S(2)}) copy-start(s32[1,64]{1,0:T(1,128)} %param.12) | copy-start | bytes 772
  37.5 4.0 %collective-permute-start.2 = (f32[32,2,24,96]{3,2,0,1:T(8,128)S(1)}, f32[32,2,24,96]{3,2,0,1:T(8,128)S(1)}, u32[]{:S(2)}, u32[]{:S(2)}) collective-permute-start(f32[32,2,24,96]{3,2,0,1:T(8,128)S(1)} %fusion.16), channel_id=1, source_target_pairs={{0,4},{4,0},{1,5},{5,1},{2,6},{6,2},{3,7},{7,3},{8,12},{12,8},{9,1... | collective-permute-start | bytes 1769480 | tf_op jit(solution)/shard_map/ppermute | solution.py:99

commit v2 on v0

v2 whole, which is shorter than its diff:
```python
import functools

import jax
import jax.numpy as jnp
from jax import lax
from jax.experimental import pallas as pl
from jax.experimental.pallas import tpu as pltpu
from jax.sharding import Mesh, PartitionSpec as P

TS = 16
ATS = 8
SLAB = 96
GROUP = 8
CHIPS = ("x", "z")
TILE = ("x", "z", "c")


def padded(x, sides, width):
    for axis, dim in sides:
        size, length = (lax.axis_size(axis), x.shape[dim])
        up = [(i, (i + 1) % size) for i in range(size)]
        down = [(j, i) for i, j in up]
        last = lax.slice_in_dim(x, length - width, length, axis=dim)
        first = lax.slice_in_dim(x, 0, width, axis=dim)
        before = lax.ppermute(last, axis, up)
        after = lax.ppermute(first, axis, down)
        x = jnp.concatenate([before, x, after], axis=dim)
    return x


def find_mirror(pair_list):
    first_orb = pair_list[:, 0]
    second = pair_list[:, 1]
    matches = (first_orb[:, None] == second[None, :]) & (second[:, None] == first_orb[None, :])
    columns = jnp.arange(pair_list.shape[0], dtype=jnp.int32)
    return jnp.sum(jnp.where(matches, columns[None, :], 0), axis=1)


def to_grid(totals, a_tiles, b_tiles):
    pair_count = totals.shape[1]
    shaped = totals.reshape(a_tiles, b_tiles, pair_count, ATS, TS)
    return jnp.transpose(shaped, (2, 0, 3, 1, 4)).reshape(pair_count, a_tiles * ATS, b_tiles * TS)


def slot_kernel(picked_ref, ab_ref, live_ref, amp_ref, block_ref, out_ref):
    step = pl.program_id(0)

    @pl.when(step == 0)
    def _():
        out_ref[...] = jnp.zeros_like(out_ref)

    for j in range(GROUP):
        slot = step * GROUP + j

        @pl.when(slot < live_ref[0])
        def _():
            amp = amp_ref[picked_ref[slot]]
            product = lax.dot_general(
                amp,
                block_ref[j],
                (((1,), (1,)), ((), ())),
                precision=lax.Precision.HIGHEST,
                preferred_element_type=jnp.float32,
            )
            target = ab_ref[slot]
            out_ref[target] = out_ref[target] + product


def slot_products(picked, ab_local, live, amps, blocks, tiles_ab):
    slots, block_width, width = blocks.shape
    rows = amps.shape[1]
    steps = slots // GROUP

    def block_map(i, picked_ref, ab_ref, live_ref):
        last = jnp.maximum(live_ref[0] - 1, 0) // GROUP
        return (jnp.minimum(i, last), 0, 0)

    grid_spec = pltpu.PrefetchScalarGridSpec(
        num_scalar_prefetch=3,
        grid=(steps,),
        in_specs=[
            pl.BlockSpec(amps.shape, lambda i, *_: (0, 0, 0)),
            pl.BlockSpec((GROUP, block_width, width), block_map),
        ],
        out_specs=pl.BlockSpec((tiles_ab, rows, block_width), lambda i, *_: (0, 0, 0)),
    )
    return pl.pallas_call(
        slot_kernel,
        grid_spec=grid_spec,
        out_shape=jax.ShapeDtypeStruct((tiles_ab, rows, block_width), jnp.float32),
        compiler_params=pltpu.CompilerParams(
            dimension_semantics=("arbitrary",), vmem_limit_bytes=48 * 1024 * 1024
        ),
        cost_estimate=pl.CostEstimate(
            flops=2 * slots * rows * width * block_width * 6,
            bytes_accessed=4 * (slots * block_width * width + amps.size + tiles_ab * rows * block_width),
            transcendentals=0,
        ),
    )(picked, ab_local, live, amps, blocks)


def reduce_over_tile(x):
    chips = lax.axis_size(CHIPS)
    cores = lax.axis_size("c")
    shaped = x.reshape(x.shape[:2] + (chips, cores) + x.shape[3:])
    core = lax.axis_index("c")
    mine = jnp.take(shaped, core, axis=3)
    other = jnp.take(shaped, 1 - core, axis=3)
    summed = mine + lax.ppermute(other, "c", [(0, 1), (1, 0)])
    spread = lax.all_to_all(summed, CHIPS, 2, 2, tiled=True)
    return jnp.sum(spread, axis=2)


def shards(amplitudes, integrals, slot_ab, slot_cd, live_count, pair_list):
    tile_size = lax.axis_size(TILE)
    row_size = lax.axis_size("row")
    tile_index = lax.axis_index(TILE)
    shard_tiles = amplitudes.shape[0]
    extended = padded(amplitudes, ((TILE, 0),), shard_tiles)
    mirror = find_mirror(pair_list)
    both = jnp.concatenate([extended, jnp.take(extended, mirror, axis=1)], axis=1)
    cd_global = slot_cd[0]
    owner_tile = cd_global // shard_tiles
    offset = (owner_tile - tile_index + 1 + tile_size) % tile_size
    ext_index = offset * shard_tiles + cd_global % shard_tiles
    a_tiles = SLAB // (row_size * ATS)
    b_tiles = SLAB // TS
    tiles_ab = a_tiles * b_tiles
    totals = slot_products(
        ext_index.astype(jnp.int32),
        slot_ab[0],
        live_count[0],
        both,
        integrals[0],
        tiles_ab,
    )
    pair_count = amplitudes.shape[1]
    halves = totals.reshape(tiles_ab, 2, pair_count, totals.shape[2])
    reduced = reduce_over_tile(halves)
    own = to_grid(reduced[:, 0][:, None], a_tiles, b_tiles)
    mirrored = to_grid(reduced[:, 1][:, None], a_tiles, b_tiles)
    exchanged = lax.all_to_all(mirrored, "row", split_axis=2, concat_axis=1, tiled=True)
    turned = jnp.transpose(exchanged, (0, 2, 1))
    return own + turned


def solution(mesh):
    tile_size = mesh.shape["tile"]
    row_size = mesh.shape["row"]
    cores = 2
    split = Mesh(
        mesh.devices.reshape(4, tile_size // (4 * cores), cores, row_size), ("x", "z", "c", "row")
    )
    return jax.shard_map(
        shards,
        mesh=split,
        in_specs=(
            P(TILE, None, None),
            P("row", TILE, None, None),
            P("row", TILE),
            P("row", TILE),
            P("row", TILE),
            P(),
        ),
        out_specs=P(TILE, "row", None),
        check_vma=False,
    )
```

time: 268 us -> 88.6 us (0.33)
  waiting for transfers between devices: 174 us -> 12.6 us
  between operations: 16.1 us -> 0.85 us
  blocking collectives: 49.5 us -> 38.1 us
  Pallas kernels: 0 us -> 11 us
  matrix products: 7.07 us -> 0 us
  local copies, waits for them, and re-layouts: 6.21 us -> 11.8 us
    unnamed x2 -> x0, waiting for transfers between devices: 165 us -> none
    all_gather x1 -> x0, blocking collectives: 49.5 us -> none  [shards(): everyone = lax.all_gather(turned, 'tile', axis=0, tiled=True)]
    all_to_all x0 -> x1, blocking collectives: none -> 38.1 us  [reduce_over_tile(): spread = lax.all_to_all(summed, CHIPS, 2, 2, tiled=True)]
    pallas_call x0 -> x1, Pallas kernels: none -> 11 us  [slot_products(): pl.pallas_call(slot_kernel, grid_spec=grid_spec, out_shape=jax.ShapeDtype...]
    dot_general x4 -> x0, matrix products: 7.07 us -> none  [the longest x2 5.06 us: block_step(): jnp.einsum('spw,sbw->spb', amp_tiles, blocks, precision=highest, preferre...]
    select_n x0 -> x3, other arithmetic: none -> 3.27 us  [the longest x2 2.73 us: shards(): jnp.take(extended, mirror, axis=1)]
  transfers between devices with their start and end apart: 4 -> 4, of which waited for: 3 -> 3; matrix products, arithmetic and copies ran while one was open for 1% -> 3% of each run, Pallas kernels for 0% -> 0%
where the time goes in v2:
time: 88.6 us; the launch traced here: 87.9 us
  blocking collectives  38.1 us (43%)
  waiting for transfers between devices  12.6 us (14%)
  local copies, waits for them, and re-layouts  11.8 us (13%)
  Pallas kernels  11 us (12%)
  other arithmetic  7.31 us (8%)
  starting transfers between devices  6.22 us (7%)
    all_to_all x1, blocking collectives, reduce_over_tile(): spread = lax.all_to_all(summed, CHIPS, 2, 2, tiled=True)  38.1 us
    pallas_call x1, Pallas kernels, slot_products(): pl.pallas_call(slot_kernel, grid_spec=grid_spec, out_shape=jax.ShapeDtype...  11 us
    ppermute x1, waiting for transfers between devices, padded(): before = lax.ppermute(last, axis, up)  5.46 us
    all_to_all x1, waiting for transfers between devices, shards(): lax.all_to_all(mirrored, 'row', split_axis=2, concat_axis=1, tiled=True)  5.12 us
    all_to_all x1, starting transfers between devices, shards(): lax.all_to_all(mirrored, 'row', split_axis=2, concat_axis=1, tiled=True)  4.39 us
    gather x1, local copies, waits for them, and re-layouts, shards(): jnp.take(extended, mirror, axis=1)  3.56 us
    unnamed x7, local copies, waits for them, and re-layouts  2.99 us
    select_n x2, other arithmetic, shards(): jnp.take(extended, mirror, axis=1)  2.73 us
  transfers between devices with their start and end apart: 4, of which 3 were waited for; matrix products, arithmetic and copies ran while one was open for 3% of the time, Pallas kernels for 0%

profile of v2, /device:TPU:32, one launch (start us, length us, event | category | flops | bytes accessed | tf_op | source)
XLA Modules:
  0.0 87.9 jit_solution(2751794651805998283)
XLA Ops:
  0.0 1.7 %collective-permute-start.1 = (f32[9,64,256]{2,1,0:T(8,128)}, f32[9,64,256]{2,1,0:T(8,128)S(1)}, u32[]{:S(2)}, u32[]{:S(2)}) collective-permute-start(f32[9,64,256]{2,1,0:T(8,128)} %param.8), channel_id=1, source_target_pairs={{4,0},{8,4},{12,8},{16,12},{20,16},{24,20},{28,24},{32,28},{36,32}... | collective-permute-start | bytes 1769480 | tf_op jit(solution)/shard_map/ppermute | solution.py:26
  1.7 0.8 slice_bitcast_fusion
  3.4 0.7 fusion.5.picked_ref
  4.1 5.5 %collective-permute-done = f32[9,64,256]{2,1,0:T(8,128)S(1)} collective-permute-done((f32[9,64,256]{2,1,0:T(8,128)}, f32[9,64,256]{2,1,0:T(8,128)S(1)}, u32[]{:S(2)}, u32[]{:S(2)}) %collective-permute-start) | collective-permute-done | bytes 589856 | tf_op jit(solution)/shard_map/ppermute | solution.py:25
  9.6 1.1 %constant_dynamic-update-slice_fusion.1 = f32[27,64,256]{2,1,0:T(8,128)S(1)} fusion(f32[27,64,256]{2,1,0:T(8,128)S(1)} %constant_dynamic-update-slice_fusion.2, f32[9,64,256]{2,1,0:T(8,128)} %param.8), kind=kLoop, calls=%fused_computation.14 | loop fusion | bytes 1179648
  10.7 2.4 %copy.28 = f32[27,64,256]{2,0,1:T(8,128)} copy(f32[27,64,256]{2,1,0:T(8,128)S(1)} %constant_dynamic-update-slice_fusion) | data formatting | bytes 3538944 | tf_op jit(solution)/shard_map/concatenate | solution.py:27
  13.1 3.6 %gather_fusion = f32[64,27,256]{2,1,0:T(8,128)} fusion(f32[27,64,256]{2,0,1:T(8,128)} %copy.28, s32[1024]{0:T(1024)S(1)} %pad_clamp_fusion), kind=kCustom, calls=%fused_computation | custom fusion | bytes 3539200 | tf_op jit(solution)/shard_map/jit(_take)/gather | solution.py:121
  16.7 2.7 %fusion = f32[27,64,256]{2,1,0:T(8,128)S(1)} fusion(f32[64,27,256]{2,1,0:T(8,128)} %gather_fusion, pred[64]{0:T(512)(128)(4,1)S(1)} %compare_and_fusion), kind=kLoop, calls=%fused_computation.3 | loop fusion | flops 442368 | bytes 3539008 | tf_op jit(solution)/shard_map/jit(_take)/select_n | solution.py:121
  19.4 0.2 pad_maximum_fusion.amp_ref
  19.7 0.4 copy-done
  20.1 11.0 %shard_map.64 = f32[18,128,128]{2,1,0:T(8,128)S(1)} custom-call(s32[64]{0:T(128)S(1)} %fusion.5.picked_ref, s32[64]{0:T(128)S(1)} %bitcast.47, s32[1]{0:T(128)} %bitcast.45.live_ref, f32[27,128,256]{2,1,0:T(8,128)S(1)} %pad_maximum_fusion.amp_ref, f32[64,128,256]{2,1,0:T(8,128)} %bitcast.48), custom_call_target="tpu_custom_call" | custom-call | flops 3221225472 | bytes 13107200 | tf_op jit(solution)/shard_map/pallas_call | solution.py:87
  31.1 1.2 %constant_dynamic-slice_fusion = (f32[18,2,32,1,128]{4,3,2,1,0:T(1,128)S(1)}, f32[18,2,32,1,128]{4,3,2,1,0:T(1,128)S(1)}) fusion(f32[18,2,32,2,128]{4,3,2,1,0:T(2,128)S(1)} %bitcast.46, s32[]{:T(128)S(6)} %select_n.59, s32[]{:T(128)S(6)} %select_n.61), kind=kLoop, calls=%fused_computation.32 | loop fusion | bytes 2359304 | tf_op jit(solution)/shard_map/jit(_take) | solution.py:107
  32.4 0.5 fusion.1
  33.0 2.0 %collective-permute-done.2 = f32[18,2,32,128]{3,1,0,2:T(2,128)S(1)} collective-permute-done((f32[18,2,32,128]{3,1,0,2:T(2,128)S(1)}, f32[18,2,32,128]{3,1,0,2:T(2,128)S(1)}, u32[]{:S(2)}, u32[]{:S(2)}) %collective-permute-start.2) | collective-permute-done | bytes 589856 | tf_op jit(solution)/shard_map/ppermute | solution.py:109
  35.0 0.6 fusion.3
  35.6 38.1 %all_to_all.23 = f32[18,2,32,128]{3,1,0,2:T(2,128)S(1)} all-to-all(f32[18,2,32,128]{3,1,0,2:T(2,128)S(1)} %fusion.3), channel_id=1, replica_groups=mesh['x'=4,'z'=8,'c'=2,'row'=4] {'x','z'}, dimensions={2} | all-to-all | bytes 1179648 | tf_op jit(solution)/shard_map/all_to_all | solution.py:110
  73.7 0.2 reduce_sum.22
  74.3 0.6 broadcast.94
  74.9 0.8 reduce.4
  75.7 0.7 reshape.107
  76.4 4.4 %all-to-all-start.1 = ((f32[4,1,576]{2,1,0:T(1,128)}), f32[4,1,576]{2,1,0:T(1,128)S(1)}, u32[]{:S(2)}, u32[]{:S(2)}) async-start(f32[4,1,576]{2,1,0:T(1,128)} %reshape.107), calls=%async_computation.1 | async-start | bytes 20480 | tf_op jit(solution)/shard_map/all_to_all | solution.py:142
  81.0 5.1 %all-to-all-done.1 = f32[4,1,576]{2,1,0:T(1,128)S(1)} async-done(((f32[4,1,576]{2,1,0:T(1,128)}), f32[4,1,576]{2,1,0:T(1,128)S(1)}, u32[]{:S(2)}, u32[]{:S(2)}) %all-to-all-start.1) | async-done | bytes 9248 | tf_op jit(solution)/shard_map/all_to_all | solution.py:142
  86.1 0.7 reduce.5
  87.3 0.6 bitcast_add_fusion
  (22 shorter events, 1.3 us)
Async XLA Ops:
  0.0 9.5 %collective-permute-start = (f32[9,64,256]{2,1,0:T(8,128)}, f32[9,64,256]{2,1,0:T(8,128)S(1)}, u32[]{:S(2)}, u32[]{:S(2)}) collective-permute-start(f32[9,64,256]{2,1,0:T(8,128)} %param.8), channel_id=1, source_target_pairs={{0,4},{4,8},{8,12},{12,16},{16,20},{20,24},{24,28},{28,32},{32,36}... | collective-permute-start | bytes 1769480 | tf_op jit(solution)/shard_map/ppermute | solution.py:25
  0.0 10.7 %collective-permute-start.1 = (f32[9,64,256]{2,1,0:T(8,128)}, f32[9,64,256]{2,1,0:T(8,128)S(1)}, u32[]{:S(2)}, u32[]{:S(2)}) collective-permute-start(f32[9,64,256]{2,1,0:T(8,128)} %param.8), channel_id=1, source_target_pairs={{4,0},{8,4},{12,8},{16,12},{20,16},{24,20},{28,24},{32,28},{36,32}... | collective-permute-start | bytes 1769480 | tf_op jit(solution)/shard_map/ppermute | solution.py:26
  19.4 0.7 copy-start
  32.9 2.1 %collective-permute-start.2 = (f32[18,2,32,128]{3,1,0,2:T(2,128)S(1)}, f32[18,2,32,128]{3,1,0,2:T(2,128)S(1)}, u32[]{:S(2)}, u32[]{:S(2)}) collective-permute-start(f32[18,2,32,128]{3,1,0,2:T(2,128)S(1)} %fusion.1), channel_id=1, source_target_pairs={{0,4},{4,0},{1,5},{5,1},{2,6},{6,2},{3,7},{7,3},{8,12},{12,8},{9,1... | collective-permute-start | bytes 1769480 | tf_op jit(solution)/shard_map/ppermute | solution.py:109
  76.4 9.7 %all-to-all-start.1 = ((f32[4,1,576]{2,1,0:T(1,128)}), f32[4,1,576]{2,1,0:T(1,128)S(1)}, u32[]{:S(2)}, u32[]{:S(2)}) async-start(f32[4,1,576]{2,1,0:T(1,128)} %reshape.107), calls=%async_computation.1 | async-start | bytes 20480 | tf_op jit(solution)/shard_map/all_to_all | solution.py:142

commit v3 on v2

v3 whole, which is shorter than its diff:
```python
import functools

import jax
import jax.numpy as jnp
from jax import lax
from jax.experimental import pallas as pl
from jax.experimental.pallas import tpu as pltpu
from jax.sharding import Mesh, PartitionSpec as P

TS = 16
ATS = 8
SLAB = 96
GROUP = 8
CHIPS = ("x", "z")
TILE = ("x", "z", "c")


def padded(x, sides, width):
    for axis, dim in sides:
        size, length = (lax.axis_size(axis), x.shape[dim])
        up = [(i, (i + 1) % size) for i in range(size)]
        down = [(j, i) for i, j in up]
        last = lax.slice_in_dim(x, length - width, length, axis=dim)
        first = lax.slice_in_dim(x, 0, width, axis=dim)
        before = lax.ppermute(last, axis, up)
        after = lax.ppermute(first, axis, down)
        x = jnp.concatenate([before, x, after], axis=dim)
    return x


def find_mirror(pair_list):
    first_orb = pair_list[:, 0]
    second = pair_list[:, 1]
    matches = (first_orb[:, None] == second[None, :]) & (second[:, None] == first_orb[None, :])
    columns = jnp.arange(pair_list.shape[0], dtype=jnp.int32)
    return jnp.sum(jnp.where(matches, columns[None, :], 0), axis=1)


def to_grid(totals, a_tiles, b_tiles):
    pair_count = totals.shape[1]
    shaped = totals.reshape(a_tiles, b_tiles, pair_count, ATS, TS)
    return jnp.transpose(shaped, (2, 0, 3, 1, 4)).reshape(pair_count, a_tiles * ATS, b_tiles * TS)


def slot_kernel(offset_ref, local_ref, ab_ref, live_ref, before_ref, own_ref, after_ref,
                block_ref, perm_ref, mine_ref, other_ref, acc_ref):
    step = pl.program_id(0)

    @pl.when(step == 0)
    def _():
        acc_ref[...] = jnp.zeros_like(acc_ref)

    for j in range(GROUP):
        slot = step * GROUP + j
        for side, amp_ref in enumerate((before_ref, own_ref, after_ref)):

            @pl.when((slot < live_ref[0]) & (offset_ref[slot] == side))
            def _():
                product = lax.dot_general(
                    amp_ref[local_ref[slot]],
                    block_ref[j],
                    (((1,), (1,)), ((), ())),
                    precision=lax.Precision.HIGHEST,
                    preferred_element_type=jnp.float32,
                )
                target = ab_ref[slot]
                acc_ref[target] = acc_ref[target] + product

    @pl.when(step == pl.num_programs(0) - 1)
    def _():
        half = mine_ref.shape[1]
        for e in range(acc_ref.shape[0]):
            placed = jnp.dot(
                perm_ref[...], acc_ref[e], precision=lax.Precision.HIGHEST,
                preferred_element_type=jnp.float32,
            )
            mine_ref[e] = placed[:half]
            other_ref[e] = placed[half:]


def slot_products(offset, local, ab_local, live, before, own, after, blocks, perm, tiles_ab):
    slots, block_width, width = blocks.shape
    pairs = own.shape[1]
    steps = slots // GROUP

    def block_map(i, *refs):
        last = jnp.maximum(refs[3][0] - 1, 0) // GROUP
        return (jnp.minimum(i, last), 0, 0)

    whole = lambda shape: pl.BlockSpec(shape, lambda i, *_: (0,) * len(shape))
    out_shape = (tiles_ab, perm.shape[0] // 2, block_width)
    grid_spec = pltpu.PrefetchScalarGridSpec(
        num_scalar_prefetch=4,
        grid=(steps,),
        in_specs=[
            whole(before.shape),
            whole(own.shape),
            whole(after.shape),
            pl.BlockSpec((GROUP, block_width, width), block_map),
            whole(perm.shape),
        ],
        out_specs=[whole(out_shape), whole(out_shape)],
        scratch_shapes=[pltpu.VMEM((tiles_ab, pairs, block_width), jnp.float32)],
    )
    return pl.pallas_call(
        slot_kernel,
        grid_spec=grid_spec,
        out_shape=[jax.ShapeDtypeStruct(out_shape, jnp.float32)] * 2,
        compiler_params=pltpu.CompilerParams(
            dimension_semantics=("arbitrary",), vmem_limit_bytes=48 * 1024 * 1024
        ),
        cost_estimate=pl.CostEstimate(
            flops=2 * slots * pairs * width * block_width * 6,
            bytes_accessed=4 * (slots * block_width * width + 3 * own.size + 2 * tiles_ab * pairs * block_width),
            transcendentals=0,
        ),
    )(offset, local, ab_local, live, before, own, after, blocks, perm)


def exchange_rows(mirrored):
    size = lax.axis_size("row")
    index = lax.axis_index("row")
    width = mirrored.shape[1]
    placed = jnp.zeros((1, size * width, width), mirrored.dtype)
    for shift in range(size):
        block = lax.dynamic_slice_in_dim(mirrored, ((index + shift) % size) * width, width, axis=2)
        if shift:
            block = lax.ppermute(block, "row", [(i, (i + shift) % size) for i in range(size)])
        source = (index - shift + size) % size
        placed = lax.dynamic_update_slice_in_dim(placed, block, source * width, axis=1)
    return placed


def shards(amplitudes, integrals, slot_ab, slot_cd, live_count, pair_list):
    tile_size = lax.axis_size(TILE)
    row_size = lax.axis_size("row")
    tile_index = lax.axis_index(TILE)
    core = lax.axis_index("c")
    cores = lax.axis_size("c")
    shard_tiles = amplitudes.shape[0]
    pair_count = amplitudes.shape[1]
    up = [(i, (i + 1) % tile_size) for i in range(tile_size)]
    down = [(j, i) for i, j in up]
    before = lax.ppermute(amplitudes, TILE, up)
    after = lax.ppermute(amplitudes, TILE, down)
    mirror = find_mirror(pair_list)
    chips_of = jnp.arange(pair_count // cores, dtype=jnp.int32) * cores
    kept = chips_of + core
    sent = chips_of + (cores - 1 - core)
    source = jnp.concatenate([kept, mirror[kept], sent, mirror[sent]])
    perm = (source[:, None] == jnp.arange(pair_count, dtype=jnp.int32)[None, :]).astype(jnp.float32)
    cd_global = slot_cd[0]
    owner_tile = cd_global // shard_tiles
    offset = (owner_tile - tile_index + 1 + tile_size) % tile_size
    a_tiles = SLAB // (row_size * ATS)
    b_tiles = SLAB // TS
    tiles_ab = a_tiles * b_tiles
    mine, other = slot_products(
        offset.astype(jnp.int32),
        (cd_global % shard_tiles).astype(jnp.int32),
        slot_ab[0],
        live_count[0],
        before,
        amplitudes,
        after,
        integrals[0],
        perm,
        tiles_ab,
    )
    summed = mine + lax.ppermute(other, "c", [(0, 1), (1, 0)])
    halves = summed.reshape(tiles_ab, 2, pair_count // cores, summed.shape[2])
    spread = lax.all_to_all(halves, CHIPS, 2, 2, tiled=True)
    reduced = jnp.sum(spread, axis=2)
    own = to_grid(reduced[:, 0][:, None], a_tiles, b_tiles)
    mirrored = to_grid(reduced[:, 1][:, None], a_tiles, b_tiles)
    turned = jnp.transpose(exchange_rows(mirrored), (0, 2, 1))
    return own + turned


def solution(mesh):
    tile_size = mesh.shape["tile"]
    row_size = mesh.shape["row"]
    cores = 2
    split = Mesh(
        mesh.devices.reshape(4, tile_size // (4 * cores), cores, row_size), ("x", "z", "c", "row")
    )
    return jax.shard_map(
        shards,
        mesh=split,
        in_specs=(
            P(TILE, None, None),
            P("row", TILE, None, None),
            P("row", TILE),
            P("row", TILE),
            P("row", TILE),
            P(),
        ),
        out_specs=P(TILE, "row", None),
        check_vma=False,
    )
```

time: 88.6 us -> 77.4 us (0.87)
  blocking collectives: 38.1 us -> 0 us
  waiting for transfers between devices: 12.6 us -> 27.8 us
  starting transfers between devices: 6.22 us -> 18.6 us
  Pallas kernels: 11 us -> 20.8 us
  other arithmetic: 7.31 us -> 1.9 us
  local copies, waits for them, and re-layouts: 11.8 us -> 6.9 us
    all_to_all x1 -> x0, blocking collectives: 38.1 us -> none  [reduce_over_tile(): spread = lax.all_to_all(summed, CHIPS, 2, 2, tiled=True)]
    all_to_all x1, waiting for transfers between devices: 5.12 us -> 19.4 us  [shards(): spread = lax.all_to_all(halves, CHIPS, 2, 2, tiled=True)]
    pallas_call x1, Pallas kernels: 11 us -> 20.8 us  [slot_products(): pl.pallas_call(slot_kernel, grid_spec=grid_spec, out_shape=[jax.ShapeDtyp...]
    all_to_all x1, starting transfers between devices: 4.39 us -> 11.8 us  [shards(): spread = lax.all_to_all(halves, CHIPS, 2, 2, tiled=True)]
    ppermute x3 -> x6, starting transfers between devices: 1.84 us -> 6.72 us  [the longest x3 4.89 us: exchange_rows(): lax.ppermute(block, 'row', [(i, (i + shift) % size) for i in range(size)])]
    select_n x3 -> x2, other arithmetic: 3.27 us -> 0.69 us  [the longest x1 0.69 us: shards(): cd_global % shard_tiles]
    concatenate x2 -> x0, local copies, waits for them, and re-layouts: 2.43 us -> none  [padded(): x = jnp.concatenate([before, x, after], axis=dim)]
    gather x1 -> x2, local copies, waits for them, and re-layouts: 3.56 us -> 1.4 us  [shards(): source = jnp.concatenate([kept, mirror[kept], sent, mirror[sent]])]
  transfers between devices with their start and end apart: 4 -> 7, of which waited for: 3 -> 5; matrix products, arithmetic and copies ran while one was open for 3% -> 6% of each run, Pallas kernels for 0% -> 0%
where the time goes in v3:
time: 77.4 us; the launch traced here: 76.8 us
  waiting for transfers between devices  27.8 us (36%)
  Pallas kernels  20.8 us (27%)
  starting transfers between devices  18.6 us (24%)
  local copies, waits for them, and re-layouts  6.9 us (9%)
  other arithmetic  1.9 us (2%)
  between operations  0.86 us (1%)
    pallas_call x1, Pallas kernels, slot_products(): pl.pallas_call(slot_kernel, grid_spec=grid_spec, out_shape=[jax.ShapeDtyp...  20.8 us
    all_to_all x1, waiting for transfers between devices, shards(): spread = lax.all_to_all(halves, CHIPS, 2, 2, tiled=True)  19.4 us
    all_to_all x1, starting transfers between devices, shards(): spread = lax.all_to_all(halves, CHIPS, 2, 2, tiled=True)  11.8 us
    ppermute x3, starting transfers between devices, exchange_rows(): lax.ppermute(block, 'row', [(i, (i + shift) % size) for i in range(size)])  4.89 us
    ppermute x1, waiting for transfers between devices, shards(): before = lax.ppermute(amplitudes, TILE, up)  3.88 us
    ppermute x3, waiting for transfers between devices, exchange_rows(): lax.ppermute(block, 'row', [(i, (i + shift) % size) for i in range(size)])  2.53 us
    unnamed x8, local copies, waits for them, and re-layouts  2.01 us
    ppermute x1, waiting for transfers between devices, shards(): summed = mine + lax.ppermute(other, 'c', [(0, 1), (1, 0)])  1.99 us
  transfers between devices with their start and end apart: 7, of which 5 were waited for; matrix products, arithmetic and copies ran while one was open for 6% of the time, Pallas kernels for 0%

profile of v3, /device:TPU:32, one launch (start us, length us, event | category | flops | bytes accessed | tf_op | source)
XLA Modules:
  0.0 76.8 jit_solution(17008525013703321010)
XLA Ops:
  0.0 1.7 %collective-permute-start.1 = (f32[9,64,256]{2,1,0:T(8,128)}, f32[9,64,256]{2,1,0:T(8,128)S(1)}, u32[]{:S(2)}, u32[]{:S(2)}) collective-permute-start(f32[9,64,256]{2,1,0:T(8,128)} %own_ref.1), channel_id=1, source_target_pairs={{4,0},{8,4},{12,8},{16,12},{20,16},{24,20},{28,24},{32,28},{36,32}... | collective-permute-start | bytes 1769480 | tf_op jit(solution)/shard_map/ppermute | solution.py:145
  1.7 0.8 slice_bitcast_fusion
  2.5 0.2 select_reduce_fusion
  3.4 0.7 gather_fusion.1
  4.1 0.7 gather_fusion
  4.9 0.7 and_select_fusion
  5.6 3.9 %collective-permute-done.before_ref = f32[9,64,256]{2,1,0:T(8,128)S(1)} collective-permute-done((f32[9,64,256]{2,1,0:T(8,128)}, f32[9,64,256]{2,1,0:T(8,128)S(1)}, u32[]{:S(2)}, u32[]{:S(2)}) %collective-permute-start) | collective-permute-done | bytes 589856 | tf_op jit(solution)/shard_map/ppermute | solution.py:144
  9.5 1.1 %copy-done = f32[9,64,256]{2,1,0:T(8,128)S(1)} copy-done((f32[9,64,256]{2,1,0:T(8,128)S(1)}, f32[9,64,256]{2,1,0:T(8,128)}, u32[]{:S(2)}) %copy-start) | copy-done | bytes 589848
  10.6 0.7 copy-done.1
  11.2 20.8 %shard_map.64 = (f32[18,64,128]{2,1,0:T(8,128)S(1)}, f32[18,64,128]{2,1,0:T(8,128)S(1)}) custom-call(s32[64]{0:T(128)S(1)} %get-tuple-element.18.offset_ref, s32[64]{0:T(128)S(1)} %get-tuple-element.17.local_ref, s32[64]{0:T(128)S(1)} %bitcast.32, s32[1]{0:T(128)} %bitcast.31.live_ref, f32[9,64,256]{2,1,0:T(8,128)S(1)} %collective-permute-done.before_ref, ...), custom_call_target="tpu_custom_call" | custom-call | flops 1610612736 | bytes 11337728 | tf_op jit(solution)/shard_map/pallas_call | solution.py:105
  32.1 2.0 %collective-permute-done.2 = f32[18,64,128]{2,1,0:T(8,128)S(1)} collective-permute-done((f32[18,64,128]{2,1,0:T(8,128)S(1)}, f32[18,64,128]{2,1,0:T(8,128)S(1)}, u32[]{:S(2)}, u32[]{:S(2)}) %collective-permute-start.2) | collective-permute-done | bytes 589856 | tf_op jit(solution)/shard_map/ppermute | solution.py:170
  34.2 1.3 %copy.20 = f32[18,2,32,128]{3,1,0,2:T(2,128)} copy(f32[18,2,32,128]{3,2,1,0:T(8,128)S(1)} %bitcast.34) | data formatting | bytes 1179648 | tf_op jit(solution)/shard_map/reshape | solution.py:171
  35.4 11.8 %all-to-all-start = ((f32[18,2,32,128]{3,1,0,2:T(2,128)}), f32[18,2,32,128]{3,1,0,2:T(2,128)S(1)}, u32[]{:S(2)}, u32[]{:S(2)}) async-start(f32[18,2,32,128]{3,1,0,2:T(2,128)} %copy.20), calls=%async_computation | async-start | bytes 1179648 | tf_op jit(solution)/shard_map/all_to_all | solution.py:172
  47.4 19.4 %all-to-all-done = f32[18,2,32,128]{3,1,0,2:T(2,128)S(1)} async-done(((f32[18,2,32,128]{3,1,0,2:T(2,128)}), f32[18,2,32,128]{3,1,0,2:T(2,128)S(1)}, u32[]{:S(2)}, u32[]{:S(2)}) %all-to-all-start) | async-done | bytes 589856 | tf_op jit(solution)/shard_map/all_to_all | solution.py:172
  66.8 0.2 reduce_sum.19
  67.5 4.8 %collective-permute-start.4 = (f32[1,24,24]{1,2,0:T(8,128)S(1)}, f32[1,24,24]{1,2,0:T(8,128)S(1)}, u32[]{:S(2)}, u32[]{:S(2)}) collective-permute-start(f32[1,24,24]{1,2,0:T(8,128)S(1)} %copy.29), channel_id=1, source_target_pairs={{0,2},{1,3},{2,0},{3,1},{4,6},{5,7},{6,4},{7,5},{8,10},{9,11},{10,... | collective-permute-start | bytes 6920 | tf_op jit(solution)/shard_map/ppermute | solution.py:128
  72.3 0.1 collective-permute-start.5
  72.7 0.2 dynamic_update_slice.12
  72.9 0.3 dynamic_update_slice.13
  73.3 0.7 collective-permute-done.4
  74.0 0.2 dynamic_update_slice.14
  74.2 1.8 %collective-permute-done.5 = f32[1,24,24]{1,2,0:T(8,128)S(1)} collective-permute-done((f32[1,24,24]{1,2,0:T(8,128)S(1)}, f32[1,24,24]{1,2,0:T(8,128)S(1)}, u32[]{:S(2)}, u32[]{:S(2)}) %collective-permute-start.5) | collective-permute-done | bytes 2336 | tf_op jit(solution)/shard_map/ppermute | solution.py:128
  76.0 0.2 dynamic_update_slice.15
  76.2 0.6 bitcast_add_fusion
  (27 shorter events, 1.2 us)
Async XLA Ops:
  0.0 9.5 %collective-permute-start = (f32[9,64,256]{2,1,0:T(8,128)}, f32[9,64,256]{2,1,0:T(8,128)S(1)}, u32[]{:S(2)}, u32[]{:S(2)}) collective-permute-start(f32[9,64,256]{2,1,0:T(8,128)} %own_ref.1), channel_id=1, source_target_pairs={{0,4},{4,8},{8,12},{12,16},{16,20},{20,24},{24,28},{28,32},{32,36}... | collective-permute-start | bytes 1769480 | tf_op jit(solution)/shard_map/ppermute | solution.py:144
  0.0 9.5 %collective-permute-start.1 = (f32[9,64,256]{2,1,0:T(8,128)}, f32[9,64,256]{2,1,0:T(8,128)S(1)}, u32[]{:S(2)}, u32[]{:S(2)}) collective-permute-start(f32[9,64,256]{2,1,0:T(8,128)} %own_ref.1), channel_id=1, source_target_pairs={{4,0},{8,4},{12,8},{16,12},{20,16},{24,20},{28,24},{32,28},{36,32}... | collective-permute-start | bytes 1769480 | tf_op jit(solution)/shard_map/ppermute | solution.py:145
  9.5 1.1 %copy-start = (f32[9,64,256]{2,1,0:T(8,128)S(1)}, f32[9,64,256]{2,1,0:T(8,128)}, u32[]{:S(2)}) copy-start(f32[9,64,256]{2,1,0:T(8,128)} %own_ref.1) | copy-start | bytes 1769476
  10.6 0.7 copy-start.1
  32.0 2.1 %collective-permute-start.2 = (f32[18,64,128]{2,1,0:T(8,128)S(1)}, f32[18,64,128]{2,1,0:T(8,128)S(1)}, u32[]{:S(2)}, u32[]{:S(2)}) collective-permute-start(f32[18,64,128]{2,1,0:T(8,128)S(1)} %get-tuple-element.8), channel_id=1, source_target_pairs={{0,4},{4,0},{1,5},{5,1},{2,6},{6,2},{3,7},{7,3},{8,12},{12,8},{9,1... | collective-permute-start | bytes 1769480 | tf_op jit(solution)/shard_map/ppermute | solution.py:170
  35.4 31.3 %all-to-all-start = ((f32[18,2,32,128]{3,1,0,2:T(2,128)}), f32[18,2,32,128]{3,1,0,2:T(2,128)S(1)}, u32[]{:S(2)}, u32[]{:S(2)}) async-start(f32[18,2,32,128]{3,1,0,2:T(2,128)} %copy.20), calls=%async_computation | async-start | bytes 1179648 | tf_op jit(solution)/shard_map/all_to_all | solution.py:172
  67.4 5.5 %collective-permute-start.3 = (f32[1,24,24]{1,2,0:T(8,128)S(1)}, f32[1,24,24]{1,2,0:T(8,128)S(1)}, u32[]{:S(2)}, u32[]{:S(2)}) collective-permute-start(f32[1,24,24]{1,2,0:T(8,128)S(1)} %copy.28), channel_id=1, source_target_pairs={{0,1},{1,2},{2,3},{3,0},{4,5},{5,6},{6,7},{7,4},{8,9},{9,10},{10,1... | collective-permute-start | bytes 6920 | tf_op jit(solution)/shard_map/ppermute | solution.py:128
  67.5 6.5 %collective-permute-start.4 = (f32[1,24,24]{1,2,0:T(8,128)S(1)}, f32[1,24,24]{1,2,0:T(8,128)S(1)}, u32[]{:S(2)}, u32[]{:S(2)}) collective-permute-start(f32[1,24,24]{1,2,0:T(8,128)S(1)} %copy.29), channel_id=1, source_target_pairs={{0,2},{1,3},{2,0},{3,1},{4,6},{5,7},{6,4},{7,5},{8,10},{9,11},{10,... | collective-permute-start | bytes 6920 | tf_op jit(solution)/shard_map/ppermute | solution.py:128
  72.3 3.7 %collective-permute-start.5 = (f32[1,24,24]{1,2,0:T(8,128)S(1)}, f32[1,24,24]{1,2,0:T(8,128)S(1)}, u32[]{:S(2)}, u32[]{:S(2)}) collective-permute-start(f32[1,24,24]{1,2,0:T(8,128)S(1)} %copy.30), channel_id=1, source_target_pairs={{0,3},{1,0},{2,1},{3,2},{4,7},{5,4},{6,5},{7,6},{8,11},{9,8},{10,9... | collective-permute-start | bytes 6920 | tf_op jit(solution)/shard_map/ppermute | solution.py:128

commit v4 on v3

--- a/solution.py
+++ b/solution.py
@@ -60,7 +60,7 @@
                     amp_ref[local_ref[slot]],
                     block_ref[j],
                     (((1,), (1,)), ((), ())),
-                    precision=lax.Precision.HIGHEST,
+                    precision=lax.Precision.HIGH,
                     preferred_element_type=jnp.float32,
                 )
                 target = ab_ref[slot]

time: 77.4 us -> 73 us (0.943)
  Pallas kernels: 20.8 us -> 9 us
  starting transfers between devices: 18.6 us -> 26.8 us
  waiting for transfers between devices: 27.8 us -> 26.4 us
    pallas_call x1, Pallas kernels: 20.8 us -> 9 us  [slot_products(): pl.pallas_call(slot_kernel, grid_spec=grid_spec, out_shape=[jax.ShapeDtyp...]
    all_to_all x1, starting transfers between devices: 11.8 us -> 17.6 us  [shards(): spread = lax.all_to_all(halves, CHIPS, 2, 2, tiled=True)]
    ppermute x1, starting transfers between devices: 0.09 us -> 1.58 us  [shards(): summed = mine + lax.ppermute(other, 'c', [(0, 1), (1, 0)])]
    ppermute x3, starting transfers between devices: 4.89 us -> 5.92 us  [exchange_rows(): lax.ppermute(block, 'row', [(i, (i + shift) % size) for i in range(size)])]
    ppermute x3, waiting for transfers between devices: 2.53 us -> 1.55 us  [exchange_rows(): lax.ppermute(block, 'row', [(i, (i + shift) % size) for i in range(size)])]
  transfers between devices with their start and end apart: 7 -> 7, of which waited for: 5 -> 4; matrix products, arithmetic and copies ran while one was open for 6% -> 6% of each run, Pallas kernels for 0% -> 0%
where the time goes in v4:
time: 73 us; the launch traced here: 72 us
  starting transfers between devices  26.8 us (37%)
  waiting for transfers between devices  26.4 us (36%)
  Pallas kernels  9 us (12%)
  local copies, waits for them, and re-layouts  7.05 us (10%)
  other arithmetic  1.9 us (3%)
  between operations  0.84 us (1%)
    all_to_all x1, waiting for transfers between devices, shards(): spread = lax.all_to_all(halves, CHIPS, 2, 2, tiled=True)  19.3 us
    all_to_all x1, starting transfers between devices, shards(): spread = lax.all_to_all(halves, CHIPS, 2, 2, tiled=True)  17.6 us
    pallas_call x1, Pallas kernels, slot_products(): pl.pallas_call(slot_kernel, grid_spec=grid_spec, out_shape=[jax.ShapeDtyp...  9 us
    ppermute x3, starting transfers between devices, exchange_rows(): lax.ppermute(block, 'row', [(i, (i + shift) % size) for i in range(size)])  5.92 us
    ppermute x1, waiting for transfers between devices, shards(): before = lax.ppermute(amplitudes, TILE, up)  3.88 us
    unnamed x8, local copies, waits for them, and re-layouts  2 us
    ppermute x1, starting transfers between devices, shards(): after = lax.ppermute(amplitudes, TILE, down)  1.74 us
    ppermute x1, waiting for transfers between devices, shards(): summed = mine + lax.ppermute(other, 'c', [(0, 1), (1, 0)])  1.63 us
  transfers between devices with their start and end apart: 7, of which 4 were waited for; matrix products, arithmetic and copies ran while one was open for 6% of the time, Pallas kernels for 0%

profile of v4, /device:TPU:32, one launch (start us, length us, event | category | flops | bytes accessed | tf_op | source)
XLA Modules:
  0.0 72.0 jit_solution(500627431671642003)
XLA Ops:
  0.0 1.7 %collective-permute-start.1 = (f32[9,64,256]{2,1,0:T(8,128)}, f32[9,64,256]{2,1,0:T(8,128)S(1)}, u32[]{:S(2)}, u32[]{:S(2)}) collective-permute-start(f32[9,64,256]{2,1,0:T(8,128)} %own_ref.1), channel_id=1, source_target_pairs={{4,0},{8,4},{12,8},{16,12},{20,16},{24,20},{28,24},{32,28},{36,32}... | collective-permute-start | bytes 1769480 | tf_op jit(solution)/shard_map/ppermute | solution.py:145
  1.7 0.8 %slice_bitcast_fusion = (s32[64]{0:T(128)S(1)}, s32[64]{0:T(128)S(1)}) fusion(s32[64,2]{0,1:T(2,128)} %param.11), kind=kLoop, calls=%fused_computation.27 | loop fusion | bytes 1024 | tf_op jit(solution)/shard_map/eq | solution.py:34
  3.4 0.7 gather_fusion.1
  4.1 0.7 gather_fusion
  4.9 0.7 and_select_fusion
  5.6 3.9 %collective-permute-done.before_ref = f32[9,64,256]{2,1,0:T(8,128)S(1)} collective-permute-done((f32[9,64,256]{2,1,0:T(8,128)}, f32[9,64,256]{2,1,0:T(8,128)S(1)}, u32[]{:S(2)}, u32[]{:S(2)}) %collective-permute-start) | collective-permute-done | bytes 589856 | tf_op jit(solution)/shard_map/ppermute | solution.py:144
  9.5 1.1 %copy-done = f32[9,64,256]{2,1,0:T(8,128)S(1)} copy-done((f32[9,64,256]{2,1,0:T(8,128)S(1)}, f32[9,64,256]{2,1,0:T(8,128)}, u32[]{:S(2)}) %copy-start) | copy-done | bytes 589848
  10.6 0.7 copy-done.1
  11.2 9.0 %shard_map.64 = (f32[18,64,128]{2,1,0:T(8,128)S(1)}, f32[18,64,128]{2,1,0:T(8,128)S(1)}) custom-call(s32[64]{0:T(128)S(1)} %get-tuple-element.18.offset_ref, s32[64]{0:T(128)S(1)} %get-tuple-element.17.local_ref, s32[64]{0:T(128)S(1)} %bitcast.32, s32[1]{0:T(128)} %bitcast.31.live_ref, f32[9,64,256]{2,1,0:T(8,128)S(1)} %collective-permute-done.before_ref, ...), custom_call_target="tpu_custom_call" | custom-call | flops 1610612736 | bytes 11337728 | tf_op jit(solution)/shard_map/pallas_call | solution.py:105
  20.2 1.6 %collective-permute-start.2 = (f32[18,64,128]{2,1,0:T(8,128)S(1)}, f32[18,64,128]{2,1,0:T(8,128)S(1)}, u32[]{:S(2)}, u32[]{:S(2)}) collective-permute-start(f32[18,64,128]{2,1,0:T(8,128)S(1)} %get-tuple-element.8), channel_id=1, source_target_pairs={{0,4},{4,0},{1,5},{5,1},{2,6},{6,2},{3,7},{7,3},{8,12},{12,8},{9,1... | collective-permute-start | bytes 1769480 | tf_op jit(solution)/shard_map/ppermute | solution.py:170
  21.8 1.6 %collective-permute-done.2 = f32[18,64,128]{2,1,0:T(8,128)S(1)} collective-permute-done((f32[18,64,128]{2,1,0:T(8,128)S(1)}, f32[18,64,128]{2,1,0:T(8,128)S(1)}, u32[]{:S(2)}, u32[]{:S(2)}) %collective-permute-start.2) | collective-permute-done | bytes 589856 | tf_op jit(solution)/shard_map/ppermute | solution.py:170
  23.5 1.3 %copy.20 = f32[18,2,32,128]{3,1,0,2:T(2,128)} copy(f32[18,2,32,128]{3,2,1,0:T(8,128)S(1)} %bitcast.34) | data formatting | bytes 1179648 | tf_op jit(solution)/shard_map/reshape | solution.py:171
  24.8 17.6 %all-to-all-start = ((f32[18,2,32,128]{3,1,0,2:T(2,128)}), f32[18,2,32,128]{3,1,0,2:T(2,128)S(1)}, u32[]{:S(2)}, u32[]{:S(2)}) async-start(f32[18,2,32,128]{3,1,0,2:T(2,128)} %copy.20), calls=%async_computation | async-start | bytes 1179648 | tf_op jit(solution)/shard_map/all_to_all | solution.py:172
  42.5 19.3 %all-to-all-done = f32[18,2,32,128]{3,1,0,2:T(2,128)S(1)} async-done(((f32[18,2,32,128]{3,1,0,2:T(2,128)}), f32[18,2,32,128]{3,1,0,2:T(2,128)S(1)}, u32[]{:S(2)}, u32[]{:S(2)}) %all-to-all-start) | async-done | bytes 589856 | tf_op jit(solution)/shard_map/all_to_all | solution.py:172
  61.8 0.2 reduce_sum.19
  62.4 3.2 %collective-permute-start.3 = (f32[1,24,24]{1,2,0:T(8,128)S(1)}, f32[1,24,24]{1,2,0:T(8,128)S(1)}, u32[]{:S(2)}, u32[]{:S(2)}) collective-permute-start(f32[1,24,24]{1,2,0:T(8,128)S(1)} %copy.28), channel_id=1, source_target_pairs={{0,1},{1,2},{2,3},{3,0},{4,5},{5,6},{6,7},{7,4},{8,9},{9,10},{10,1... | collective-permute-start | bytes 6920 | tf_op jit(solution)/shard_map/ppermute | solution.py:128
  65.7 1.1 %collective-permute-start.4 = (f32[1,24,24]{1,2,0:T(8,128)S(1)}, f32[1,24,24]{1,2,0:T(8,128)S(1)}, u32[]{:S(2)}, u32[]{:S(2)}) collective-permute-start(f32[1,24,24]{1,2,0:T(8,128)S(1)} %copy.29), channel_id=1, source_target_pairs={{0,2},{1,3},{2,0},{3,1},{4,6},{5,7},{6,4},{7,5},{8,10},{9,11},{10,... | collective-permute-start | bytes 6920 | tf_op jit(solution)/shard_map/ppermute | solution.py:128
  66.9 1.6 %collective-permute-start.5 = (f32[1,24,24]{1,2,0:T(8,128)S(1)}, f32[1,24,24]{1,2,0:T(8,128)S(1)}, u32[]{:S(2)}, u32[]{:S(2)}) collective-permute-start(f32[1,24,24]{1,2,0:T(8,128)S(1)} %copy.30), channel_id=1, source_target_pairs={{0,3},{1,0},{2,1},{3,2},{4,7},{5,4},{6,5},{7,6},{8,11},{9,8},{10,9... | collective-permute-start | bytes 6920 | tf_op jit(solution)/shard_map/ppermute | solution.py:128
  68.7 0.2 dynamic_update_slice.12
  69.0 0.3 dynamic_update_slice.13
  69.3 1.5 %collective-permute-done.4 = f32[1,24,24]{1,2,0:T(8,128)S(1)} collective-permute-done((f32[1,24,24]{1,2,0:T(8,128)S(1)}, f32[1,24,24]{1,2,0:T(8,128)S(1)}, u32[]{:S(2)}, u32[]{:S(2)}) %collective-permute-start.4) | collective-permute-done | bytes 2336 | tf_op jit(solution)/shard_map/ppermute | solution.py:128
  70.9 0.2 dynamic_update_slice.14
  71.1 0.3 dynamic_update_slice.15
  71.4 0.6 bitcast_add_fusion
  (27 shorter events, 1.2 us)
Async XLA Ops:
  0.0 9.5 %collective-permute-start = (f32[9,64,256]{2,1,0:T(8,128)}, f32[9,64,256]{2,1,0:T(8,128)S(1)}, u32[]{:S(2)}, u32[]{:S(2)}) collective-permute-start(f32[9,64,256]{2,1,0:T(8,128)} %own_ref.1), channel_id=1, source_target_pairs={{0,4},{4,8},{8,12},{12,16},{16,20},{20,24},{24,28},{28,32},{32,36}... | collective-permute-start | bytes 1769480 | tf_op jit(solution)/shard_map/ppermute | solution.py:144
  0.0 9.5 %collective-permute-start.1 = (f32[9,64,256]{2,1,0:T(8,128)}, f32[9,64,256]{2,1,0:T(8,128)S(1)}, u32[]{:S(2)}, u32[]{:S(2)}) collective-permute-start(f32[9,64,256]{2,1,0:T(8,128)} %own_ref.1), channel_id=1, source_target_pairs={{4,0},{8,4},{12,8},{16,12},{20,16},{24,20},{28,24},{32,28},{36,32}... | collective-permute-start | bytes 1769480 | tf_op jit(solution)/shard_map/ppermute | solution.py:145
  9.5 1.1 %copy-start = (f32[9,64,256]{2,1,0:T(8,128)S(1)}, f32[9,64,256]{2,1,0:T(8,128)}, u32[]{:S(2)}) copy-start(f32[9,64,256]{2,1,0:T(8,128)} %own_ref.1) | copy-start | bytes 1769476
  10.6 0.7 copy-start.1
  20.2 3.2 %collective-permute-start.2 = (f32[18,64,128]{2,1,0:T(8,128)S(1)}, f32[18,64,128]{2,1,0:T(8,128)S(1)}, u32[]{:S(2)}, u32[]{:S(2)}) collective-permute-start(f32[18,64,128]{2,1,0:T(8,128)S(1)} %get-tuple-element.8), channel_id=1, source_target_pairs={{0,4},{4,0},{1,5},{5,1},{2,6},{6,2},{3,7},{7,3},{8,12},{12,8},{9,1... | collective-permute-start | bytes 1769480 | tf_op jit(solution)/shard_map/ppermute | solution.py:170
  24.8 37.0 %all-to-all-start = ((f32[18,2,32,128]{3,1,0,2:T(2,128)}), f32[18,2,32,128]{3,1,0,2:T(2,128)S(1)}, u32[]{:S(2)}, u32[]{:S(2)}) async-start(f32[18,2,32,128]{3,1,0,2:T(2,128)} %copy.20), calls=%async_computation | async-start | bytes 1179648 | tf_op jit(solution)/shard_map/all_to_all | solution.py:172
  62.4 6.6 %collective-permute-start.3 = (f32[1,24,24]{1,2,0:T(8,128)S(1)}, f32[1,24,24]{1,2,0:T(8,128)S(1)}, u32[]{:S(2)}, u32[]{:S(2)}) collective-permute-start(f32[1,24,24]{1,2,0:T(8,128)S(1)} %copy.28), channel_id=1, source_target_pairs={{0,1},{1,2},{2,3},{3,0},{4,5},{5,6},{6,7},{7,4},{8,9},{9,10},{10,1... | collective-permute-start | bytes 6920 | tf_op jit(solution)/shard_map/ppermute | solution.py:128
  65.7 5.2 %collective-permute-start.4 = (f32[1,24,24]{1,2,0:T(8,128)S(1)}, f32[1,24,24]{1,2,0:T(8,128)S(1)}, u32[]{:S(2)}, u32[]{:S(2)}) collective-permute-start(f32[1,24,24]{1,2,0:T(8,128)S(1)} %copy.29), channel_id=1, source_target_pairs={{0,2},{1,3},{2,0},{3,1},{4,6},{5,7},{6,4},{7,5},{8,10},{9,11},{10,... | collective-permute-start | bytes 6920 | tf_op jit(solution)/shard_map/ppermute | solution.py:128
  66.9 4.2 %collective-permute-start.5 = (f32[1,24,24]{1,2,0:T(8,128)S(1)}, f32[1,24,24]{1,2,0:T(8,128)S(1)}, u32[]{:S(2)}, u32[]{:S(2)}) collective-permute-start(f32[1,24,24]{1,2,0:T(8,128)S(1)} %copy.30), channel_id=1, source_target_pairs={{0,3},{1,0},{2,1},{3,2},{4,7},{5,4},{6,5},{7,6},{8,11},{9,8},{10,9... | collective-permute-start | bytes 6920 | tf_op jit(solution)/shard_map/ppermute | solution.py:128

commit v5 on v4

--- a/solution.py
+++ b/solution.py
@@ -42,79 +42,76 @@
     return jnp.transpose(shaped, (2, 0, 3, 1, 4)).reshape(pair_count, a_tiles * ATS, b_tiles * TS)
 
 
-def slot_kernel(offset_ref, local_ref, ab_ref, live_ref, before_ref, own_ref, after_ref,
-                block_ref, perm_ref, mine_ref, other_ref, acc_ref):
+def slot_kernel(picked_ref, ab_ref, live_ref, before_ref, own_ref, after_ref,
+                block_ref, out_ref, amp_ref, acc_ref):
     step = pl.program_id(0)
+    shard_tiles = own_ref.shape[0]
 
     @pl.when(step == 0)
     def _():
         acc_ref[...] = jnp.zeros_like(acc_ref)
+        for side, source in enumerate((before_ref, own_ref, after_ref)):
+            amp_ref[side * shard_tiles:(side + 1) * shard_tiles] = source[...]
 
-    for j in range(GROUP):
-        slot = step * GROUP + j
-        for side, amp_ref in enumerate((before_ref, own_ref, after_ref)):
-
-            @pl.when((slot < live_ref[0]) & (offset_ref[slot] == side))
-            def _():
-                product = lax.dot_general(
-                    amp_ref[local_ref[slot]],
-                    block_ref[j],
-                    (((1,), (1,)), ((), ())),
-                    precision=lax.Precision.HIGH,
-                    preferred_element_type=jnp.float32,
-                )
-                target = ab_ref[slot]
-                acc_ref[target] = acc_ref[target] + product
+    @pl.when(step * GROUP < live_ref[0])
+    def _():
+        for j in range(GROUP):
+            slot = step * GROUP + j
+            product = lax.dot_general(
+                amp_ref[picked_ref[slot]],
+                block_ref[j],
+                (((1,), (1,)), ((), ())),
+                precision=lax.Precision.HIGH,
+                preferred_element_type=jnp.float32,
+            )
+            target = ab_ref[slot]
+            used = slot < live_ref[0]
+            acc_ref[target] = acc_ref[target] + jnp.where(used, product, 0.0)
 
     @pl.when(step == pl.num_programs(0) - 1)
     def _():
-        half = mine_ref.shape[1]
-        for e in range(acc_ref.shape[0]):
-            placed = jnp.dot(
-                perm_ref[...], acc_ref[e], precision=lax.Precision.HIGHEST,
-                preferred_element_type=jnp.float32,
-            )
-            mine_ref[e] = placed[:half]
-            other_ref[e] = placed[half:]
+        out_ref[...] = acc_ref[...]
 
 
-def slot_products(offset, local, ab_local, live, before, own, after, blocks, perm, tiles_ab):
+def slot_products(picked, ab_local, live, before, own, after, blocks, tiles_ab):
     slots, block_width, width = blocks.shape
     pairs = own.shape[1]
     steps = slots // GROUP
 
     def block_map(i, *refs):
-        last = jnp.maximum(refs[3][0] - 1, 0) // GROUP
+        last = jnp.maximum(refs[2][0] - 1, 0) // GROUP
         return (jnp.minimum(i, last), 0, 0)
 
     whole = lambda shape: pl.BlockSpec(shape, lambda i, *_: (0,) * len(shape))
-    out_shape = (tiles_ab, perm.shape[0] // 2, block_width)
+    out_shape = (tiles_ab, pairs, block_width)
     grid_spec = pltpu.PrefetchScalarGridSpec(
-        num_scalar_prefetch=4,
+        num_scalar_prefetch=3,
         grid=(steps,),
         in_specs=[
             whole(before.shape),
             whole(own.shape),
             whole(after.shape),
             pl.BlockSpec((GROUP, block_width, width), block_map),
-            whole(perm.shape),
         ],
-        out_specs=[whole(out_shape), whole(out_shape)],
-        scratch_shapes=[pltpu.VMEM((tiles_ab, pairs, block_width), jnp.float32)],
+        out_specs=whole(out_shape),
+        scratch_shapes=[
+            pltpu.VMEM((3 * own.shape[0],) + own.shape[1:], jnp.float32),
+            pltpu.VMEM((tiles_ab, pairs, block_width), jnp.float32),
+        ],
     )
     return pl.pallas_call(
         slot_kernel,
         grid_spec=grid_spec,
-        out_shape=[jax.ShapeDtypeStruct(out_shape, jnp.float32)] * 2,
+        out_shape=jax.ShapeDtypeStruct(out_shape, jnp.float32),
         compiler_params=pltpu.CompilerParams(
             dimension_semantics=("arbitrary",), vmem_limit_bytes=48 * 1024 * 1024
         ),
         cost_estimate=pl.CostEstimate(
-            flops=2 * slots * pairs * width * block_width * 6,
-            bytes_accessed=4 * (slots * block_width * width + 3 * own.size + 2 * tiles_ab * pairs * block_width),
+            flops=2 * slots * pairs * width * block_width * 3,
+            bytes_accessed=4 * (slots * block_width * width + 3 * own.size + tiles_ab * pairs * block_width),
             transcendentals=0,
         ),
-    )(offset, local, ab_local, live, before, own, after, blocks, perm)
+    )(picked, ab_local, live, before, own, after, blocks)
 
 
 def exchange_rows(mirrored):
@@ -147,26 +144,26 @@
     chips_of = jnp.arange(pair_count // cores, dtype=jnp.int32) * cores
     kept = chips_of + core
     sent = chips_of + (cores - 1 - core)
-    source = jnp.concatenate([kept, mirror[kept], sent, mirror[sent]])
-    perm = (source[:, None] == jnp.arange(pair_count, dtype=jnp.int32)[None, :]).astype(jnp.float32)
+    keep_rows = jnp.concatenate([kept, mirror[kept]])
+    send_rows = jnp.concatenate([sent, mirror[sent]])
     cd_global = slot_cd[0]
     owner_tile = cd_global // shard_tiles
     offset = (owner_tile - tile_index + 1 + tile_size) % tile_size
     a_tiles = SLAB // (row_size * ATS)
     b_tiles = SLAB // TS
     tiles_ab = a_tiles * b_tiles
-    mine, other = slot_products(
-        offset.astype(jnp.int32),
-        (cd_global % shard_tiles).astype(jnp.int32),
+    totals = slot_products(
+        (offset * shard_tiles + cd_global % shard_tiles).astype(jnp.int32),
         slot_ab[0],
         live_count[0],
         before,
         amplitudes,
         after,
         integrals[0],
-        perm,
         tiles_ab,
     )
+    mine = jnp.take(totals, keep_rows, axis=1)
+    other = jnp.take(totals, send_rows, axis=1)
     summed = mine + lax.ppermute(other, "c", [(0, 1), (1, 0)])
     halves = summed.reshape(tiles_ab, 2, pair_count // cores, summed.shape[2])
     spread = lax.all_to_all(halves, CHIPS, 2, 2, tiled=True)

time: 73 us -> 67.2 us (0.921)
  Pallas kernels: 9 us -> 4.75 us
  starting transfers between devices: 26.8 us -> 23.4 us
  local copies, waits for them, and re-layouts: 7.05 us -> 8.6 us
    all_to_all x1, starting transfers between devices: 17.6 us -> 9.64 us  [shards(): spread = lax.all_to_all(halves, CHIPS, 2, 2, tiled=True)]
    ppermute x1, starting transfers between devices: 1.58 us -> 6.67 us  [shards(): summed = mine + lax.ppermute(other, 'c', [(0, 1), (1, 0)])]
    pallas_call x1, Pallas kernels: 9 us -> 4.75 us  [slot_products(): pl.pallas_call(slot_kernel, grid_spec=grid_spec, out_shape=jax.ShapeDtype...]
    ppermute x1, waiting for transfers between devices: 1.63 us -> 0.18 us  [shards(): summed = mine + lax.ppermute(other, 'c', [(0, 1), (1, 0)])]
    gather x2 -> x4, local copies, waits for them, and re-layouts: 1.4 us -> 2.66 us  [the longest x1 0.7 us: shards(): send_rows = jnp.concatenate([sent, mirror[sent]])]
    ppermute x3, waiting for transfers between devices: 1.55 us -> 2.63 us  [exchange_rows(): lax.ppermute(block, 'row', [(i, (i + shift) % size) for i in range(size)])]
    ppermute x1, waiting for transfers between devices: 3.88 us -> 4.68 us  [shards(): before = lax.ppermute(amplitudes, TILE, up)]
    unnamed x8 -> x10, local copies, waits for them, and re-layouts: 2 us -> 2.01 us
  transfers between devices with their start and end apart: 7 -> 7, of which waited for: 4 -> 5; matrix products, arithmetic and copies ran while one was open for 6% -> 8% of each run, Pallas kernels for 0% -> 0%
where the time goes in v5:
time: 67.2 us; the launch traced here: 66.7 us
  waiting for transfers between devices  26.7 us (40%)
  starting transfers between devices  23.4 us (35%)
  local copies, waits for them, and re-layouts  8.6 us (13%)
  Pallas kernels  4.75 us (7%)
  other arithmetic  2.38 us (4%)
  between operations  0.89 us (1%)
    all_to_all x1, waiting for transfers between devices, shards(): spread = lax.all_to_all(halves, CHIPS, 2, 2, tiled=True)  19.2 us
    all_to_all x1, starting transfers between devices, shards(): spread = lax.all_to_all(halves, CHIPS, 2, 2, tiled=True)  9.64 us
    ppermute x1, starting transfers between devices, shards(): summed = mine + lax.ppermute(other, 'c', [(0, 1), (1, 0)])  6.67 us
    ppermute x3, starting transfers between devices, exchange_rows(): lax.ppermute(block, 'row', [(i, (i + shift) % size) for i in range(size)])  5.3 us
    pallas_call x1, Pallas kernels, slot_products(): pl.pallas_call(slot_kernel, grid_spec=grid_spec, out_shape=jax.ShapeDtype...  4.75 us
    ppermute x1, waiting for transfers between devices, shards(): before = lax.ppermute(amplitudes, TILE, up)  4.68 us
    ppermute x3, waiting for transfers between devices, exchange_rows(): lax.ppermute(block, 'row', [(i, (i + shift) % size) for i in range(size)])  2.63 us
    unnamed x10, local copies, waits for them, and re-layouts  2.01 us
  transfers between devices with their start and end apart: 7, of which 5 were waited for; matrix products, arithmetic and copies ran while one was open for 8% of the time, Pallas kernels for 0%

profile of v5, /device:TPU:32, one launch (start us, length us, event | category | flops | bytes accessed | tf_op | source)
XLA Modules:
  0.0 66.7 jit_solution(7910279244467268466)
XLA Ops:
  0.0 1.7 %collective-permute-start.1 = (f32[9,64,256]{2,1,0:T(8,128)}, f32[9,64,256]{2,1,0:T(8,128)S(1)}, u32[]{:S(2)}, u32[]{:S(2)}) collective-permute-start(f32[9,64,256]{2,1,0:T(8,128)} %own_ref.1), channel_id=1, source_target_pairs={{4,0},{8,4},{12,8},{16,12},{20,16},{24,20},{28,24},{32,28},{36,32}... | collective-permute-start | bytes 1769480 | tf_op jit(solution)/shard_map/ppermute | solution.py:142
  1.7 0.8 %slice_bitcast_fusion = (s32[64]{0:T(128)S(1)}, s32[64]{0:T(128)S(1)}) fusion(s32[64,2]{0,1:T(2,128)} %param.13), kind=kLoop, calls=%fused_computation.34 | loop fusion | bytes 1024 | tf_op jit(solution)/shard_map/eq | solution.py:34
  3.4 0.7 %gather_fusion.1 = s32[32]{0:T(128)S(1)} fusion(s32[64]{0:T(128)S(1)} %select_reduce_fusion, s32[1024]{0:T(1024)S(1)} %pad_clamp_fusion.1), kind=kCustom, calls=%fused_computation.3 | custom fusion | bytes 384 | tf_op jit(solution)/shard_map/gather | solution.py:148
  4.2 0.7 %fusion.1.picked_ref = s32[64]{0:T(128)S(1)} fusion(s32[1,64]{1,0:T(1,128)} %param.11, s32[]{:T(128)S(6)} %add.158), kind=kLoop, calls=%fused_computation.28 | loop fusion | flops 1728 | bytes 516 | tf_op jit(solution)/shard_map/add | solution.py:156
  4.8 4.7 %collective-permute-done.before_ref = f32[9,64,256]{2,1,0:T(8,128)S(1)} collective-permute-done((f32[9,64,256]{2,1,0:T(8,128)}, f32[9,64,256]{2,1,0:T(8,128)S(1)}, u32[]{:S(2)}, u32[]{:S(2)}) %collective-permute-start) | collective-permute-done | bytes 589856 | tf_op jit(solution)/shard_map/ppermute | solution.py:141
  9.5 1.1 %copy-done = f32[9,64,256]{2,1,0:T(8,128)S(1)} copy-done((f32[9,64,256]{2,1,0:T(8,128)S(1)}, f32[9,64,256]{2,1,0:T(8,128)}, u32[]{:S(2)}) %copy-start) | copy-done | bytes 589848
  10.6 0.7 copy-done.1
  11.2 4.8 %shard_map.64 = f32[18,64,128]{2,1,0:T(8,128)S(1)} custom-call(s32[64]{0:T(128)S(1)} %fusion.1.picked_ref, s32[64]{0:T(128)S(1)} %bitcast.40, s32[1]{0:T(128)} %bitcast.39.live_ref, f32[9,64,256]{2,1,0:T(8,128)S(1)} %collective-permute-done.before_ref, f32[9,64,256]{2,1,0:T(8,128)S(1)} %copy-done, f32[9,64,256]{2,1,0:T(8,128)S(1)} %collective-permute-done.1.after_ref, ...), custom_call_target="tpu_custom_call" | custom-call | flops 805306368 | bytes 10747904 | tf_op jit(solution)/shard_map/pallas_call | solution.py:102
  16.0 0.4 copy.27
  16.4 0.6 gather_fusion.3
  17.3 6.7 %collective-permute-start.2 = (f32[18,64,128]{2,1,0:T(8,128)S(1)}, f32[18,64,128]{2,1,0:T(8,128)S(1)}, u32[]{:S(2)}, u32[]{:S(2)}) collective-permute-start(f32[18,64,128]{2,1,0:T(8,128)S(1)} %copy.29), channel_id=1, source_target_pairs={{0,4},{4,0},{1,5},{5,1},{2,6},{6,2},{3,7},{7,3},{8,12},{12,8},{9,1... | collective-permute-start | bytes 1769480 | tf_op jit(solution)/shard_map/ppermute | solution.py:167
  24.0 0.7 %gather_fusion = s32[32]{0:T(128)S(1)} fusion(s32[64]{0:T(128)S(1)} %select_reduce_fusion, s32[1024]{0:T(1024)S(1)} %pad_clamp_fusion.3), kind=kCustom, calls=%fused_computation.2 | custom fusion | bytes 384 | tf_op jit(solution)/shard_map/gather | solution.py:147
  24.8 0.6 gather_fusion.2
  25.6 0.4 bitcast_add_fusion
  26.0 1.3 %copy.31 = f32[18,2,32,128]{3,1,0,2:T(2,128)} copy(f32[18,2,32,128]{3,0,2,1:T(8,128)S(1)} %bitcast.42) | data formatting | bytes 1179648 | tf_op jit(solution)/shard_map/reshape | solution.py:168
  27.2 9.6 %all-to-all-start = ((f32[18,2,32,128]{3,1,0,2:T(2,128)}), f32[18,2,32,128]{3,1,0,2:T(2,128)S(1)}, u32[]{:S(2)}, u32[]{:S(2)}) async-start(f32[18,2,32,128]{3,1,0,2:T(2,128)} %copy.31), calls=%async_computation | async-start | bytes 1179648 | tf_op jit(solution)/shard_map/all_to_all | solution.py:169
  37.0 19.2 %all-to-all-done = f32[18,2,32,128]{3,1,0,2:T(2,128)S(1)} async-done(((f32[18,2,32,128]{3,1,0,2:T(2,128)}), f32[18,2,32,128]{3,1,0,2:T(2,128)S(1)}, u32[]{:S(2)}, u32[]{:S(2)}) %all-to-all-start) | async-done | bytes 589856 | tf_op jit(solution)/shard_map/all_to_all | solution.py:169
  56.7 0.7 %collective-permute-start.3 = (f32[1,24,24]{1,2,0:T(8,128)S(1)}, f32[1,24,24]{1,2,0:T(8,128)S(1)}, u32[]{:S(2)}, u32[]{:S(2)}) collective-permute-start(f32[1,24,24]{1,2,0:T(8,128)S(1)} %copy.43), channel_id=1, source_target_pairs={{0,1},{1,2},{2,3},{3,0},{4,5},{5,6},{6,7},{7,4},{8,9},{9,10},{10,1... | collective-permute-start | bytes 6920 | tf_op jit(solution)/shard_map/ppermute | solution.py:125
  57.5 4.5 %collective-permute-start.4 = (f32[1,24,24]{1,2,0:T(8,128)S(1)}, f32[1,24,24]{1,2,0:T(8,128)S(1)}, u32[]{:S(2)}, u32[]{:S(2)}) collective-permute-start(f32[1,24,24]{1,2,0:T(8,128)S(1)} %copy.44), channel_id=1, source_target_pairs={{0,2},{1,3},{2,0},{3,1},{4,6},{5,7},{6,4},{7,5},{8,10},{9,11},{10,... | collective-permute-start | bytes 6920 | tf_op jit(solution)/shard_map/ppermute | solution.py:125
  62.5 0.2 dynamic_update_slice.12
  62.7 0.3 dynamic_update_slice.13
  63.0 0.8 %collective-permute-done.4 = f32[1,24,24]{1,2,0:T(8,128)S(1)} collective-permute-done((f32[1,24,24]{1,2,0:T(8,128)S(1)}, f32[1,24,24]{1,2,0:T(8,128)S(1)}, u32[]{:S(2)}, u32[]{:S(2)}) %collective-permute-start.4) | collective-permute-done | bytes 2336 | tf_op jit(solution)/shard_map/ppermute | solution.py:125
  64.0 1.8 %collective-permute-done.5 = f32[1,24,24]{1,2,0:T(8,128)S(1)} collective-permute-done((f32[1,24,24]{1,2,0:T(8,128)S(1)}, f32[1,24,24]{1,2,0:T(8,128)S(1)}, u32[]{:S(2)}, u32[]{:S(2)}) %collective-permute-start.5) | collective-permute-done | bytes 2336 | tf_op jit(solution)/shard_map/ppermute | solution.py:125
  66.0 0.6 bitcast_add_fusion.1
  (37 shorter events, 2.2 us)
Async XLA Ops:
  0.0 9.5 %collective-permute-start = (f32[9,64,256]{2,1,0:T(8,128)}, f32[9,64,256]{2,1,0:T(8,128)S(1)}, u32[]{:S(2)}, u32[]{:S(2)}) collective-permute-start(f32[9,64,256]{2,1,0:T(8,128)} %own_ref.1), channel_id=1, source_target_pairs={{0,4},{4,8},{8,12},{12,16},{16,20},{20,24},{24,28},{28,32},{32,36}... | collective-permute-start | bytes 1769480 | tf_op jit(solution)/shard_map/ppermute | solution.py:141
  0.0 9.5 %collective-permute-start.1 = (f32[9,64,256]{2,1,0:T(8,128)}, f32[9,64,256]{2,1,0:T(8,128)S(1)}, u32[]{:S(2)}, u32[]{:S(2)}) collective-permute-start(f32[9,64,256]{2,1,0:T(8,128)} %own_ref.1), channel_id=1, source_target_pairs={{4,0},{8,4},{12,8},{16,12},{20,16},{24,20},{28,24},{32,28},{36,32}... | collective-permute-start | bytes 1769480 | tf_op jit(solution)/shard_map/ppermute | solution.py:142
  9.5 1.1 %copy-start = (f32[9,64,256]{2,1,0:T(8,128)S(1)}, f32[9,64,256]{2,1,0:T(8,128)}, u32[]{:S(2)}) copy-start(f32[9,64,256]{2,1,0:T(8,128)} %own_ref.1) | copy-start | bytes 1769476
  10.6 0.7 copy-start.1
  17.3 8.3 %collective-permute-start.2 = (f32[18,64,128]{2,1,0:T(8,128)S(1)}, f32[18,64,128]{2,1,0:T(8,128)S(1)}, u32[]{:S(2)}, u32[]{:S(2)}) collective-permute-start(f32[18,64,128]{2,1,0:T(8,128)S(1)} %copy.29), channel_id=1, source_target_pairs={{0,4},{4,0},{1,5},{5,1},{2,6},{6,2},{3,7},{7,3},{8,12},{12,8},{9,1... | collective-permute-start | bytes 1769480 | tf_op jit(solution)/shard_map/ppermute | solution.py:167
  27.2 28.9 %all-to-all-start = ((f32[18,2,32,128]{3,1,0,2:T(2,128)}), f32[18,2,32,128]{3,1,0,2:T(2,128)S(1)}, u32[]{:S(2)}, u32[]{:S(2)}) async-start(f32[18,2,32,128]{3,1,0,2:T(2,128)} %copy.31), calls=%async_computation | async-start | bytes 1179648 | tf_op jit(solution)/shard_map/all_to_all | solution.py:169
  56.7 6.0 %collective-permute-start.3 = (f32[1,24,24]{1,2,0:T(8,128)S(1)}, f32[1,24,24]{1,2,0:T(8,128)S(1)}, u32[]{:S(2)}, u32[]{:S(2)}) collective-permute-start(f32[1,24,24]{1,2,0:T(8,128)S(1)} %copy.43), channel_id=1, source_target_pairs={{0,1},{1,2},{2,3},{3,0},{4,5},{5,6},{6,7},{7,4},{8,9},{9,10},{10,1... | collective-permute-start | bytes 6920 | tf_op jit(solution)/shard_map/ppermute | solution.py:125
  57.5 6.3 %collective-permute-start.4 = (f32[1,24,24]{1,2,0:T(8,128)S(1)}, f32[1,24,24]{1,2,0:T(8,128)S(1)}, u32[]{:S(2)}, u32[]{:S(2)}) collective-permute-start(f32[1,24,24]{1,2,0:T(8,128)S(1)} %copy.44), channel_id=1, source_target_pairs={{0,2},{1,3},{2,0},{3,1},{4,6},{5,7},{6,4},{7,5},{8,10},{9,11},{10,... | collective-permute-start | bytes 6920 | tf_op jit(solution)/shard_map/ppermute | solution.py:125
  62.2 3.7 %collective-permute-start.5 = (f32[1,24,24]{1,2,0:T(8,128)S(1)}, f32[1,24,24]{1,2,0:T(8,128)S(1)}, u32[]{:S(2)}, u32[]{:S(2)}) collective-permute-start(f32[1,24,24]{1,2,0:T(8,128)S(1)} %copy.45), channel_id=1, source_target_pairs={{0,3},{1,0},{2,1},{3,2},{4,7},{5,4},{6,5},{7,6},{8,11},{9,8},{10,9... | collective-permute-start | bytes 6920 | tf_op jit(solution)/shard_map/ppermute | solution.py:125

commit v6 on v5

--- a/solution.py
+++ b/solution.py
@@ -10,7 +10,7 @@
 TS = 16
 ATS = 8
 SLAB = 96
-GROUP = 8
+GROUP = 16
 CHIPS = ("x", "z")
 TILE = ("x", "z", "c")
 

time: 67.2 us -> 65.5 us (0.975)
  starting transfers between devices: 23.4 us -> 22.3 us
    ppermute x1, starting transfers between devices: 6.67 us -> 2.12 us  [shards(): summed = mine + lax.ppermute(other, 'c', [(0, 1), (1, 0)])]
    all_to_all x1, starting transfers between devices: 9.64 us -> 13.6 us  [shards(): spread = lax.all_to_all(halves, CHIPS, 2, 2, tiled=True)]
where the time goes in v6:
time: 65.5 us; the launch traced here: 65.6 us
  waiting for transfers between devices  26.5 us (40%)
  starting transfers between devices  22.3 us (34%)
  local copies, waits for them, and re-layouts  8.59 us (13%)
  Pallas kernels  4.88 us (7%)
  other arithmetic  2.38 us (4%)
  between operations  0.89 us (1%)
    all_to_all x1, waiting for transfers between devices, shards(): spread = lax.all_to_all(halves, CHIPS, 2, 2, tiled=True)  19.2 us
    all_to_all x1, starting transfers between devices, shards(): spread = lax.all_to_all(halves, CHIPS, 2, 2, tiled=True)  13.6 us
    pallas_call x1, Pallas kernels, slot_products(): pl.pallas_call(slot_kernel, grid_spec=grid_spec, out_shape=jax.ShapeDtype...  4.88 us
    ppermute x3, starting transfers between devices, exchange_rows(): lax.ppermute(block, 'row', [(i, (i + shift) % size) for i in range(size)])  4.84 us
    ppermute x1, waiting for transfers between devices, shards(): before = lax.ppermute(amplitudes, TILE, up)  4.68 us
    ppermute x3, waiting for transfers between devices, exchange_rows(): lax.ppermute(block, 'row', [(i, (i + shift) % size) for i in range(size)])  2.49 us
    ppermute x1, starting transfers between devices, shards(): summed = mine + lax.ppermute(other, 'c', [(0, 1), (1, 0)])  2.12 us
    unnamed x10, local copies, waits for them, and re-layouts  2.01 us
  transfers between devices with their start and end apart: 7, of which 5 were waited for; matrix products, arithmetic and copies ran while one was open for 8% of the time, Pallas kernels for 0%

profile of v6, /device:TPU:32, one launch (start us, length us, event | category | flops | bytes accessed | tf_op | source)
XLA Modules:
  0.0 65.6 jit_solution(11516454428315944754)
XLA Ops:
  0.0 1.7 %collective-permute-start.1 = (f32[9,64,256]{2,1,0:T(8,128)}, f32[9,64,256]{2,1,0:T(8,128)S(1)}, u32[]{:S(2)}, u32[]{:S(2)}) collective-permute-start(f32[9,64,256]{2,1,0:T(8,128)} %own_ref.1), channel_id=1, source_target_pairs={{4,0},{8,4},{12,8},{16,12},{20,16},{24,20},{28,24},{32,28},{36,32}... | collective-permute-start | bytes 1769480 | tf_op jit(solution)/shard_map/ppermute | solution.py:142
  1.7 0.8 %slice_bitcast_fusion = (s32[64]{0:T(128)S(1)}, s32[64]{0:T(128)S(1)}) fusion(s32[64,2]{0,1:T(2,128)} %param.13), kind=kLoop, calls=%fused_computation.34 | loop fusion | bytes 1024 | tf_op jit(solution)/shard_map/eq | solution.py:34
  3.4 0.7 %gather_fusion.1 = s32[32]{0:T(128)S(1)} fusion(s32[64]{0:T(128)S(1)} %select_reduce_fusion, s32[1024]{0:T(1024)S(1)} %pad_clamp_fusion.1), kind=kCustom, calls=%fused_computation.3 | custom fusion | bytes 384 | tf_op jit(solution)/shard_map/gather | solution.py:148
  4.2 0.7 %fusion.1.picked_ref = s32[64]{0:T(128)S(1)} fusion(s32[1,64]{1,0:T(1,128)} %param.11, s32[]{:T(128)S(6)} %add.158), kind=kLoop, calls=%fused_computation.28 | loop fusion | flops 1728 | bytes 516 | tf_op jit(solution)/shard_map/add | solution.py:156
  4.8 4.7 %collective-permute-done.before_ref = f32[9,64,256]{2,1,0:T(8,128)S(1)} collective-permute-done((f32[9,64,256]{2,1,0:T(8,128)}, f32[9,64,256]{2,1,0:T(8,128)S(1)}, u32[]{:S(2)}, u32[]{:S(2)}) %collective-permute-start) | collective-permute-done | bytes 589856 | tf_op jit(solution)/shard_map/ppermute | solution.py:141
  9.5 1.1 %copy-done = f32[9,64,256]{2,1,0:T(8,128)S(1)} copy-done((f32[9,64,256]{2,1,0:T(8,128)S(1)}, f32[9,64,256]{2,1,0:T(8,128)}, u32[]{:S(2)}) %copy-start) | copy-done | bytes 589848
  10.6 0.7 copy-done.1
  11.2 4.9 %shard_map.64 = f32[18,64,128]{2,1,0:T(8,128)S(1)} custom-call(s32[64]{0:T(128)S(1)} %fusion.1.picked_ref, s32[64]{0:T(128)S(1)} %bitcast.40, s32[1]{0:T(128)} %bitcast.39.live_ref, f32[9,64,256]{2,1,0:T(8,128)S(1)} %collective-permute-done.before_ref, f32[9,64,256]{2,1,0:T(8,128)S(1)} %copy-done, f32[9,64,256]{2,1,0:T(8,128)S(1)} %collective-permute-done.1.after_ref, ...), custom_call_target="tpu_custom_call" | custom-call | flops 805306368 | bytes 10747904 | tf_op jit(solution)/shard_map/pallas_call | solution.py:102
  16.1 0.4 copy.27
  16.5 0.6 gather_fusion.3
  17.4 2.1 %collective-permute-start.2 = (f32[18,64,128]{2,1,0:T(8,128)S(1)}, f32[18,64,128]{2,1,0:T(8,128)S(1)}, u32[]{:S(2)}, u32[]{:S(2)}) collective-permute-start(f32[18,64,128]{2,1,0:T(8,128)S(1)} %copy.29), channel_id=1, source_target_pairs={{0,4},{4,0},{1,5},{5,1},{2,6},{6,2},{3,7},{7,3},{8,12},{12,8},{9,1... | collective-permute-start | bytes 1769480 | tf_op jit(solution)/shard_map/ppermute | solution.py:167
  19.5 0.7 %gather_fusion = s32[32]{0:T(128)S(1)} fusion(s32[64]{0:T(128)S(1)} %select_reduce_fusion, s32[1024]{0:T(1024)S(1)} %pad_clamp_fusion.3), kind=kCustom, calls=%fused_computation.2 | custom fusion | bytes 384 | tf_op jit(solution)/shard_map/gather | solution.py:147
  20.3 0.6 gather_fusion.2
  21.1 0.4 bitcast_add_fusion
  21.5 1.3 %copy.31 = f32[18,2,32,128]{3,1,0,2:T(2,128)} copy(f32[18,2,32,128]{3,0,2,1:T(8,128)S(1)} %bitcast.42) | data formatting | bytes 1179648 | tf_op jit(solution)/shard_map/reshape | solution.py:168
  22.8 13.6 %all-to-all-start = ((f32[18,2,32,128]{3,1,0,2:T(2,128)}), f32[18,2,32,128]{3,1,0,2:T(2,128)S(1)}, u32[]{:S(2)}, u32[]{:S(2)}) async-start(f32[18,2,32,128]{3,1,0,2:T(2,128)} %copy.31), calls=%async_computation | async-start | bytes 1179648 | tf_op jit(solution)/shard_map/all_to_all | solution.py:169
  36.4 19.2 %all-to-all-done = f32[18,2,32,128]{3,1,0,2:T(2,128)S(1)} async-done(((f32[18,2,32,128]{3,1,0,2:T(2,128)}), f32[18,2,32,128]{3,1,0,2:T(2,128)S(1)}, u32[]{:S(2)}, u32[]{:S(2)}) %all-to-all-start) | async-done | bytes 589856 | tf_op jit(solution)/shard_map/all_to_all | solution.py:169
  56.2 2.1 %collective-permute-start.3 = (f32[1,24,24]{1,2,0:T(8,128)S(1)}, f32[1,24,24]{1,2,0:T(8,128)S(1)}, u32[]{:S(2)}, u32[]{:S(2)}) collective-permute-start(f32[1,24,24]{1,2,0:T(8,128)S(1)} %copy.43), channel_id=1, source_target_pairs={{0,1},{1,2},{2,3},{3,0},{4,5},{5,6},{6,7},{7,4},{8,9},{9,10},{10,1... | collective-permute-start | bytes 6920 | tf_op jit(solution)/shard_map/ppermute | solution.py:125
  58.4 2.6 %collective-permute-start.4 = (f32[1,24,24]{1,2,0:T(8,128)S(1)}, f32[1,24,24]{1,2,0:T(8,128)S(1)}, u32[]{:S(2)}, u32[]{:S(2)}) collective-permute-start(f32[1,24,24]{1,2,0:T(8,128)S(1)} %copy.44), channel_id=1, source_target_pairs={{0,2},{1,3},{2,0},{3,1},{4,6},{5,7},{6,4},{7,5},{8,10},{9,11},{10,... | collective-permute-start | bytes 6920 | tf_op jit(solution)/shard_map/ppermute | solution.py:125
  61.5 0.2 dynamic_update_slice.12
  61.7 0.3 dynamic_update_slice.13
  62.1 1.5 %collective-permute-done.4 = f32[1,24,24]{1,2,0:T(8,128)S(1)} collective-permute-done((f32[1,24,24]{1,2,0:T(8,128)S(1)}, f32[1,24,24]{1,2,0:T(8,128)S(1)}, u32[]{:S(2)}, u32[]{:S(2)}) %collective-permute-start.4) | collective-permute-done | bytes 2336 | tf_op jit(solution)/shard_map/ppermute | solution.py:125
  63.8 0.9 %collective-permute-done.5 = f32[1,24,24]{1,2,0:T(8,128)S(1)} collective-permute-done((f32[1,24,24]{1,2,0:T(8,128)S(1)}, f32[1,24,24]{1,2,0:T(8,128)S(1)}, u32[]{:S(2)}, u32[]{:S(2)}) %collective-permute-start.5) | collective-permute-done | bytes 2336 | tf_op jit(solution)/shard_map/ppermute | solution.py:125
  64.9 0.6 bitcast_add_fusion.1
  (37 shorter events, 2.3 us)
Async XLA Ops:
  0.0 9.5 %collective-permute-start = (f32[9,64,256]{2,1,0:T(8,128)}, f32[9,64,256]{2,1,0:T(8,128)S(1)}, u32[]{:S(2)}, u32[]{:S(2)}) collective-permute-start(f32[9,64,256]{2,1,0:T(8,128)} %own_ref.1), channel_id=1, source_target_pairs={{0,4},{4,8},{8,12},{12,16},{16,20},{20,24},{24,28},{28,32},{32,36}... | collective-permute-start | bytes 1769480 | tf_op jit(solution)/shard_map/ppermute | solution.py:141
  0.0 9.5 %collective-permute-start.1 = (f32[9,64,256]{2,1,0:T(8,128)}, f32[9,64,256]{2,1,0:T(8,128)S(1)}, u32[]{:S(2)}, u32[]{:S(2)}) collective-permute-start(f32[9,64,256]{2,1,0:T(8,128)} %own_ref.1), channel_id=1, source_target_pairs={{4,0},{8,4},{12,8},{16,12},{20,16},{24,20},{28,24},{32,28},{36,32}... | collective-permute-start | bytes 1769480 | tf_op jit(solution)/shard_map/ppermute | solution.py:142
  9.5 1.1 %copy-start = (f32[9,64,256]{2,1,0:T(8,128)S(1)}, f32[9,64,256]{2,1,0:T(8,128)}, u32[]{:S(2)}) copy-start(f32[9,64,256]{2,1,0:T(8,128)} %own_ref.1) | copy-start | bytes 1769476
  10.6 0.7 copy-start.1
  17.4 3.7 %collective-permute-start.2 = (f32[18,64,128]{2,1,0:T(8,128)S(1)}, f32[18,64,128]{2,1,0:T(8,128)S(1)}, u32[]{:S(2)}, u32[]{:S(2)}) collective-permute-start(f32[18,64,128]{2,1,0:T(8,128)S(1)} %copy.29), channel_id=1, source_target_pairs={{0,4},{4,0},{1,5},{5,1},{2,6},{6,2},{3,7},{7,3},{8,12},{12,8},{9,1... | collective-permute-start | bytes 1769480 | tf_op jit(solution)/shard_map/ppermute | solution.py:167
  22.8 32.8 %all-to-all-start = ((f32[18,2,32,128]{3,1,0,2:T(2,128)}), f32[18,2,32,128]{3,1,0,2:T(2,128)S(1)}, u32[]{:S(2)}, u32[]{:S(2)}) async-start(f32[18,2,32,128]{3,1,0,2:T(2,128)} %copy.31), calls=%async_computation | async-start | bytes 1179648 | tf_op jit(solution)/shard_map/all_to_all | solution.py:169
  56.2 5.5 %collective-permute-start.3 = (f32[1,24,24]{1,2,0:T(8,128)S(1)}, f32[1,24,24]{1,2,0:T(8,128)S(1)}, u32[]{:S(2)}, u32[]{:S(2)}) collective-permute-start(f32[1,24,24]{1,2,0:T(8,128)S(1)} %copy.43), channel_id=1, source_target_pairs={{0,1},{1,2},{2,3},{3,0},{4,5},{5,6},{6,7},{7,4},{8,9},{9,10},{10,1... | collective-permute-start | bytes 6920 | tf_op jit(solution)/shard_map/ppermute | solution.py:125
  58.4 5.2 %collective-permute-start.4 = (f32[1,24,24]{1,2,0:T(8,128)S(1)}, f32[1,24,24]{1,2,0:T(8,128)S(1)}, u32[]{:S(2)}, u32[]{:S(2)}) collective-permute-start(f32[1,24,24]{1,2,0:T(8,128)S(1)} %copy.44), channel_id=1, source_target_pairs={{0,2},{1,3},{2,0},{3,1},{4,6},{5,7},{6,4},{7,5},{8,10},{9,11},{10,... | collective-permute-start | bytes 6920 | tf_op jit(solution)/shard_map/ppermute | solution.py:125
  61.1 3.7 %collective-permute-start.5 = (f32[1,24,24]{1,2,0:T(8,128)S(1)}, f32[1,24,24]{1,2,0:T(8,128)S(1)}, u32[]{:S(2)}, u32[]{:S(2)}) collective-permute-start(f32[1,24,24]{1,2,0:T(8,128)S(1)} %copy.45), channel_id=1, source_target_pairs={{0,3},{1,0},{2,1},{3,2},{4,7},{5,4},{6,5},{7,6},{8,11},{9,8},{10,9... | collective-permute-start | bytes 6920 | tf_op jit(solution)/shard_map/ppermute | solution.py:125

commit v7 on v6

--- a/solution.py
+++ b/solution.py
@@ -42,29 +42,35 @@
     return jnp.transpose(shaped, (2, 0, 3, 1, 4)).reshape(pair_count, a_tiles * ATS, b_tiles * TS)
 
 
-def slot_kernel(picked_ref, ab_ref, live_ref, before_ref, own_ref, after_ref,
-                block_ref, out_ref, amp_ref, acc_ref):
+def slot_kernel(index_ref, live_ref, before_ref, own_ref, after_ref,
+                block_ref, out_ref, amp_ref, acc_ref, sem_ref):
     step = pl.program_id(0)
     shard_tiles = own_ref.shape[0]
+    slots = index_ref.shape[0] // 2
 
     @pl.when(step == 0)
     def _():
+        fetch = pltpu.make_async_copy(
+            own_ref, amp_ref.at[shard_tiles:2 * shard_tiles], sem_ref.at[0]
+        )
+        fetch.start()
         acc_ref[...] = jnp.zeros_like(acc_ref)
-        for side, source in enumerate((before_ref, own_ref, after_ref)):
-            amp_ref[side * shard_tiles:(side + 1) * shard_tiles] = source[...]
+        amp_ref[:shard_tiles] = before_ref[...]
+        amp_ref[2 * shard_tiles:] = after_ref[...]
+        fetch.wait()
 
     @pl.when(step * GROUP < live_ref[0])
     def _():
         for j in range(GROUP):
             slot = step * GROUP + j
             product = lax.dot_general(
-                amp_ref[picked_ref[slot]],
+                amp_ref[index_ref[slot]],
                 block_ref[j],
                 (((1,), (1,)), ((), ())),
                 precision=lax.Precision.HIGH,
                 preferred_element_type=jnp.float32,
             )
-            target = ab_ref[slot]
+            target = index_ref[slots + slot]
             used = slot < live_ref[0]
             acc_ref[target] = acc_ref[target] + jnp.where(used, product, 0.0)
 
@@ -73,23 +79,23 @@
         out_ref[...] = acc_ref[...]
 
 
-def slot_products(picked, ab_local, live, before, own, after, blocks, tiles_ab):
+def slot_products(index, live, before, own, after, blocks, tiles_ab):
     slots, block_width, width = blocks.shape
     pairs = own.shape[1]
     steps = slots // GROUP
 
     def block_map(i, *refs):
-        last = jnp.maximum(refs[2][0] - 1, 0) // GROUP
+        last = jnp.maximum(refs[1][0] - 1, 0) // GROUP
         return (jnp.minimum(i, last), 0, 0)
 
     whole = lambda shape: pl.BlockSpec(shape, lambda i, *_: (0,) * len(shape))
     out_shape = (tiles_ab, pairs, block_width)
     grid_spec = pltpu.PrefetchScalarGridSpec(
-        num_scalar_prefetch=3,
+        num_scalar_prefetch=2,
         grid=(steps,),
         in_specs=[
             whole(before.shape),
-            whole(own.shape),
+            pl.BlockSpec(memory_space=pltpu.HBM),
             whole(after.shape),
             pl.BlockSpec((GROUP, block_width, width), block_map),
         ],
@@ -97,6 +103,7 @@
         scratch_shapes=[
             pltpu.VMEM((3 * own.shape[0],) + own.shape[1:], jnp.float32),
             pltpu.VMEM((tiles_ab, pairs, block_width), jnp.float32),
+            pltpu.SemaphoreType.DMA((1,)),
         ],
     )
     return pl.pallas_call(
@@ -111,7 +118,7 @@
             bytes_accessed=4 * (slots * block_width * width + 3 * own.size + tiles_ab * pairs * block_width),
             transcendentals=0,
         ),
-    )(picked, ab_local, live, before, own, after, blocks)
+    )(index, live, before, own, after, blocks)
 
 
 def exchange_rows(mirrored):
@@ -153,8 +160,7 @@
     b_tiles = SLAB // TS
     tiles_ab = a_tiles * b_tiles
     totals = slot_products(
-        (offset * shard_tiles + cd_global % shard_tiles).astype(jnp.int32),
-        slot_ab[0],
+        jnp.concatenate([offset * shard_tiles + cd_global % shard_tiles, slot_ab[0]]).astype(jnp.int32),
         live_count[0],
         before,
         amplitudes,

time: 65.5 us -> 65.1 us (level)
  Pallas kernels: 4.88 us -> 7.79 us
  starting transfers between devices: 22.3 us -> 19.6 us
  waiting for transfers between devices: 26.5 us -> 25.3 us
  other arithmetic: 2.38 us -> 3.12 us
    pallas_call x1, Pallas kernels: 4.88 us -> 7.79 us  [slot_products(): pl.pallas_call(slot_kernel, grid_spec=grid_spec, out_shape=jax.ShapeDtype...]
    all_to_all x1, starting transfers between devices: 13.6 us -> 11.2 us  [shards(): spread = lax.all_to_all(halves, CHIPS, 2, 2, tiled=True)]
    ppermute x1, starting transfers between devices: 2.12 us -> 0.09 us  [shards(): summed = mine + lax.ppermute(other, 'c', [(0, 1), (1, 0)])]
    ppermute x3, starting transfers between devices: 4.84 us -> 6.48 us  [exchange_rows(): lax.ppermute(block, 'row', [(i, (i + shift) % size) for i in range(size)])]
    ppermute x3, waiting for transfers between devices: 2.49 us -> 1.43 us  [exchange_rows(): lax.ppermute(block, 'row', [(i, (i + shift) % size) for i in range(size)])]
    ppermute x1, waiting for transfers between devices: 4.68 us -> 3.95 us  [shards(): before = lax.ppermute(amplitudes, TILE, up)]
    concatenate x0 -> x1, other arithmetic: none -> 0.73 us  [shards(): jnp.concatenate([offset * shard_tiles + cd_global % shard_tiles, slot_ab[...]
    unnamed x10 -> x8, local copies, waits for them, and re-layouts: 2.01 us -> 1.36 us
  transfers between devices with their start and end apart: 7 -> 7, of which waited for: 5 -> 4; matrix products, arithmetic and copies ran while one was open for 8% -> 9% of each run, Pallas kernels for 0% -> 0%
where the time goes in v7:
time: 65.1 us; the launch traced here: 64.8 us
  waiting for transfers between devices  25.3 us (39%)
  starting transfers between devices  19.6 us (30%)
  local copies, waits for them, and re-layouts  8.1 us (12%)
  Pallas kernels  7.79 us (12%)
  other arithmetic  3.12 us (5%)
  between operations  0.9 us (1%)
    all_to_all x1, waiting for transfers between devices, shards(): spread = lax.all_to_all(halves, CHIPS, 2, 2, tiled=True)  19.4 us
    all_to_all x1, starting transfers between devices, shards(): spread = lax.all_to_all(halves, CHIPS, 2, 2, tiled=True)  11.2 us
    pallas_call x1, Pallas kernels, slot_products(): pl.pallas_call(slot_kernel, grid_spec=grid_spec, out_shape=jax.ShapeDtype...  7.79 us
    ppermute x3, starting transfers between devices, exchange_rows(): lax.ppermute(block, 'row', [(i, (i + shift) % size) for i in range(size)])  6.48 us
    ppermute x1, waiting for transfers between devices, shards(): before = lax.ppermute(amplitudes, TILE, up)  3.95 us
    ppermute x1, starting transfers between devices, shards(): after = lax.ppermute(amplitudes, TILE, down)  1.74 us
    ppermute x3, waiting for transfers between devices, exchange_rows(): lax.ppermute(block, 'row', [(i, (i + shift) % size) for i in range(size)])  1.43 us
    unnamed x8, local copies, waits for them, and re-layouts  1.36 us
  transfers between devices with their start and end apart: 7, of which 4 were waited for; matrix products, arithmetic and copies ran while one was open for 9% of the time, Pallas kernels for 0%

profile of v7, /device:TPU:32, one launch (start us, length us, event | category | flops | bytes accessed | tf_op | source)
XLA Modules:
  0.0 64.8 jit_solution(13755351918965684578)
XLA Ops:
  0.0 1.7 %collective-permute-start.1 = (f32[9,64,256]{2,1,0:T(8,128)}, f32[9,64,256]{2,1,0:T(8,128)S(1)}, u32[]{:S(2)}, u32[]{:S(2)}) collective-permute-start(f32[9,64,256]{2,1,0:T(8,128)} %own_ref.1), channel_id=1, source_target_pairs={{4,0},{8,4},{12,8},{16,12},{20,16},{24,20},{28,24},{32,28},{36,32}... | collective-permute-start | bytes 1769480 | tf_op jit(solution)/shard_map/ppermute | solution.py:149
  1.7 0.8 %slice_bitcast_fusion = (s32[64]{0:T(128)S(1)}, s32[64]{0:T(128)S(1)}) fusion(s32[64,2]{0,1:T(2,128)} %param.13), kind=kLoop, calls=%fused_computation.35 | loop fusion | bytes 1024 | tf_op jit(solution)/shard_map/eq | solution.py:34
  3.4 0.7 %gather_fusion.1 = s32[32]{0:T(128)S(1)} fusion(s32[64]{0:T(128)S(1)} %select_reduce_fusion, s32[1024]{0:T(1024)S(1)} %pad_clamp_fusion.1), kind=kCustom, calls=%fused_computation.3 | custom fusion | bytes 384 | tf_op jit(solution)/shard_map/gather | solution.py:155
  4.1 0.7 %fusion.1 = s32[64]{0:T(128)S(1)} fusion(s32[1,64]{1,0:T(1,128)} %param.11, s32[]{:T(128)S(6)} %add.158), kind=kLoop, calls=%fused_computation.28 | loop fusion | flops 1728 | bytes 516 | tf_op jit(solution)/shard_map/add | solution.py:163
  4.8 0.7 %pad_add_fusion.index_ref = s32[128]{0:T(128)S(1)} fusion(s32[64]{0:T(128)} %bitcast.44, s32[64]{0:T(128)S(1)} %fusion.1), kind=kLoop, calls=%fused_computation.33 | loop fusion | flops 128 | bytes 1024 | tf_op jit(solution)/shard_map/concatenate | solution.py:163
  5.6 3.9 %collective-permute-done.before_ref = f32[9,64,256]{2,1,0:T(8,128)S(1)} collective-permute-done((f32[9,64,256]{2,1,0:T(8,128)}, f32[9,64,256]{2,1,0:T(8,128)S(1)}, u32[]{:S(2)}, u32[]{:S(2)}) %collective-permute-start) | collective-permute-done | bytes 589856 | tf_op jit(solution)/shard_map/ppermute | solution.py:148
  9.5 1.1 %copy-done = f32[9,64,256]{2,1,0:T(8,128)S(1)} copy-done((f32[9,64,256]{2,1,0:T(8,128)S(1)}, f32[9,64,256]{2,1,0:T(8,128)}, u32[]{:S(2)}) %copy-start) | copy-done | bytes 589848
  10.6 7.8 %shard_map.64 = f32[18,64,128]{2,1,0:T(8,128)S(1)} custom-call(s32[128]{0:T(128)S(1)} %pad_add_fusion.index_ref, s32[1]{0:T(128)} %bitcast.39.live_ref, f32[9,64,256]{2,1,0:T(8,128)S(1)} %collective-permute-done.before_ref, f32[9,64,256]{2,1,0:T(8,128)S(1)} %copy-done, f32[9,64,256]{2,1,0:T(8,128)S(1)} %collective-permute-done.1.after_ref, ...), custom_call_target="tpu_custom_call" | custom-call | flops 805306368 | bytes 10747904 | tf_op jit(solution)/shard_map/pallas_call | solution.py:109
  18.4 0.4 copy.27
  18.7 0.6 gather_fusion.3
  19.8 0.7 %gather_fusion = s32[32]{0:T(128)S(1)} fusion(s32[64]{0:T(128)S(1)} %select_reduce_fusion, s32[1024]{0:T(1024)S(1)} %pad_clamp_fusion.3), kind=kCustom, calls=%fused_computation.2 | custom fusion | bytes 384 | tf_op jit(solution)/shard_map/gather | solution.py:154
  20.6 0.6 gather_fusion.2
  21.2 0.5 collective-permute-done.2
  21.7 0.4 bitcast_add_fusion
  22.1 1.3 %copy.31 = f32[18,2,32,128]{3,1,0,2:T(2,128)} copy(f32[18,2,32,128]{3,0,2,1:T(8,128)S(1)} %bitcast.41) | data formatting | bytes 1179648 | tf_op jit(solution)/shard_map/reshape | solution.py:174
  23.4 11.2 %all-to-all-start = ((f32[18,2,32,128]{3,1,0,2:T(2,128)}), f32[18,2,32,128]{3,1,0,2:T(2,128)S(1)}, u32[]{:S(2)}, u32[]{:S(2)}) async-start(f32[18,2,32,128]{3,1,0,2:T(2,128)} %copy.31), calls=%async_computation | async-start | bytes 1179648 | tf_op jit(solution)/shard_map/all_to_all | solution.py:175
  34.7 19.4 %all-to-all-done = f32[18,2,32,128]{3,1,0,2:T(2,128)S(1)} async-done(((f32[18,2,32,128]{3,1,0,2:T(2,128)}), f32[18,2,32,128]{3,1,0,2:T(2,128)S(1)}, u32[]{:S(2)}, u32[]{:S(2)}) %all-to-all-start) | async-done | bytes 589856 | tf_op jit(solution)/shard_map/all_to_all | solution.py:175
  54.7 1.9 %collective-permute-start.3 = (f32[1,24,24]{1,2,0:T(8,128)S(1)}, f32[1,24,24]{1,2,0:T(8,128)S(1)}, u32[]{:S(2)}, u32[]{:S(2)}) collective-permute-start(f32[1,24,24]{1,2,0:T(8,128)S(1)} %copy.43), channel_id=1, source_target_pairs={{0,1},{1,2},{2,3},{3,0},{4,5},{5,6},{6,7},{7,4},{8,9},{9,10},{10,1... | collective-permute-start | bytes 6920 | tf_op jit(solution)/shard_map/ppermute | solution.py:132
  56.7 3.6 %collective-permute-start.4 = (f32[1,24,24]{1,2,0:T(8,128)S(1)}, f32[1,24,24]{1,2,0:T(8,128)S(1)}, u32[]{:S(2)}, u32[]{:S(2)}) collective-permute-start(f32[1,24,24]{1,2,0:T(8,128)S(1)} %copy.44), channel_id=1, source_target_pairs={{0,2},{1,3},{2,0},{3,1},{4,6},{5,7},{6,4},{7,5},{8,10},{9,11},{10,... | collective-permute-start | bytes 6920 | tf_op jit(solution)/shard_map/ppermute | solution.py:132
  60.3 1.1 %collective-permute-start.5 = (f32[1,24,24]{1,2,0:T(8,128)S(1)}, f32[1,24,24]{1,2,0:T(8,128)S(1)}, u32[]{:S(2)}, u32[]{:S(2)}) collective-permute-start(f32[1,24,24]{1,2,0:T(8,128)S(1)} %copy.45), channel_id=1, source_target_pairs={{0,3},{1,0},{2,1},{3,2},{4,7},{5,4},{6,5},{7,6},{8,11},{9,8},{10,9... | collective-permute-start | bytes 6920 | tf_op jit(solution)/shard_map/ppermute | solution.py:132
  61.9 0.3 dynamic_update_slice.13
  62.2 0.3 dynamic_update_slice.14
  62.6 1.4 %collective-permute-done.5 = f32[1,24,24]{1,2,0:T(8,128)S(1)} collective-permute-done((f32[1,24,24]{1,2,0:T(8,128)S(1)}, f32[1,24,24]{1,2,0:T(8,128)S(1)}, u32[]{:S(2)}, u32[]{:S(2)}) %collective-permute-start.5) | collective-permute-done | bytes 2336 | tf_op jit(solution)/shard_map/ppermute | solution.py:132
  64.2 0.6 bitcast_add_fusion.1
  (36 shorter events, 2.1 us)
Async XLA Ops:
  0.0 9.5 %collective-permute-start = (f32[9,64,256]{2,1,0:T(8,128)}, f32[9,64,256]{2,1,0:T(8,128)S(1)}, u32[]{:S(2)}, u32[]{:S(2)}) collective-permute-start(f32[9,64,256]{2,1,0:T(8,128)} %own_ref.1), channel_id=1, source_target_pairs={{0,4},{4,8},{8,12},{12,16},{16,20},{20,24},{24,28},{28,32},{32,36}... | collective-permute-start | bytes 1769480 | tf_op jit(solution)/shard_map/ppermute | solution.py:148
  0.0 9.5 %collective-permute-start.1 = (f32[9,64,256]{2,1,0:T(8,128)}, f32[9,64,256]{2,1,0:T(8,128)S(1)}, u32[]{:S(2)}, u32[]{:S(2)}) collective-permute-start(f32[9,64,256]{2,1,0:T(8,128)} %own_ref.1), channel_id=1, source_target_pairs={{4,0},{8,4},{12,8},{16,12},{20,16},{24,20},{28,24},{32,28},{36,32}... | collective-permute-start | bytes 1769480 | tf_op jit(solution)/shard_map/ppermute | solution.py:149
  9.5 1.1 %copy-start = (f32[9,64,256]{2,1,0:T(8,128)S(1)}, f32[9,64,256]{2,1,0:T(8,128)}, u32[]{:S(2)}) copy-start(f32[9,64,256]{2,1,0:T(8,128)} %own_ref.1) | copy-start | bytes 1769476
  19.7 2.1 %collective-permute-start.2 = (f32[18,64,128]{2,1,0:T(8,128)S(1)}, f32[18,64,128]{2,1,0:T(8,128)S(1)}, u32[]{:S(2)}, u32[]{:S(2)}) collective-permute-start(f32[18,64,128]{2,1,0:T(8,128)S(1)} %copy.29), channel_id=1, source_target_pairs={{0,4},{4,0},{1,5},{5,1},{2,6},{6,2},{3,7},{7,3},{8,12},{12,8},{9,1... | collective-permute-start | bytes 1769480 | tf_op jit(solution)/shard_map/ppermute | solution.py:173
  23.4 30.7 %all-to-all-start = ((f32[18,2,32,128]{3,1,0,2:T(2,128)}), f32[18,2,32,128]{3,1,0,2:T(2,128)S(1)}, u32[]{:S(2)}, u32[]{:S(2)}) async-start(f32[18,2,32,128]{3,1,0,2:T(2,128)} %copy.31), calls=%async_computation | async-start | bytes 1179648 | tf_op jit(solution)/shard_map/all_to_all | solution.py:175
  54.7 7.1 %collective-permute-start.3 = (f32[1,24,24]{1,2,0:T(8,128)S(1)}, f32[1,24,24]{1,2,0:T(8,128)S(1)}, u32[]{:S(2)}, u32[]{:S(2)}) collective-permute-start(f32[1,24,24]{1,2,0:T(8,128)S(1)} %copy.43), channel_id=1, source_target_pairs={{0,1},{1,2},{2,3},{3,0},{4,5},{5,6},{6,7},{7,4},{8,9},{9,10},{10,1... | collective-permute-start | bytes 6920 | tf_op jit(solution)/shard_map/ppermute | solution.py:132
  56.7 5.6 %collective-permute-start.4 = (f32[1,24,24]{1,2,0:T(8,128)S(1)}, f32[1,24,24]{1,2,0:T(8,128)S(1)}, u32[]{:S(2)}, u32[]{:S(2)}) collective-permute-start(f32[1,24,24]{1,2,0:T(8,128)S(1)} %copy.44), channel_id=1, source_target_pairs={{0,2},{1,3},{2,0},{3,1},{4,6},{5,7},{6,4},{7,5},{8,10},{9,11},{10,... | collective-permute-start | bytes 6920 | tf_op jit(solution)/shard_map/ppermute | solution.py:132
  60.3 3.7 %collective-permute-start.5 = (f32[1,24,24]{1,2,0:T(8,128)S(1)}, f32[1,24,24]{1,2,0:T(8,128)S(1)}, u32[]{:S(2)}, u32[]{:S(2)}) collective-permute-start(f32[1,24,24]{1,2,0:T(8,128)S(1)} %copy.45), channel_id=1, source_target_pairs={{0,3},{1,0},{2,1},{3,2},{4,7},{5,4},{6,5},{7,6},{8,11},{9,8},{10,9... | collective-permute-start | bytes 6920 | tf_op jit(solution)/shard_map/ppermute | solution.py:132

commit v8 on v7

--- a/solution.py
+++ b/solution.py
@@ -67,7 +67,7 @@
                 amp_ref[index_ref[slot]],
                 block_ref[j],
                 (((1,), (1,)), ((), ())),
-                precision=lax.Precision.HIGH,
+                precision=lax.Precision.HIGHEST,
                 preferred_element_type=jnp.float32,
             )
             target = index_ref[slots + slot]
@@ -114,7 +114,7 @@
             dimension_semantics=("arbitrary",), vmem_limit_bytes=48 * 1024 * 1024
         ),
         cost_estimate=pl.CostEstimate(
-            flops=2 * slots * pairs * width * block_width * 3,
+            flops=2 * slots * pairs * width * block_width * 6,
             bytes_accessed=4 * (slots * block_width * width + 3 * own.size + tiles_ab * pairs * block_width),
             transcendentals=0,
         ),

time: 65.1 us -> 68.9 us (1.058)
  starting transfers between devices: 19.6 us -> 26.7 us
  Pallas kernels: 7.79 us -> 4.83 us
    ppermute x1, starting transfers between devices: 0.09 us -> 4.39 us  [shards(): summed = mine + lax.ppermute(other, 'c', [(0, 1), (1, 0)])]
    all_to_all x1, starting transfers between devices: 11.2 us -> 14.8 us  [shards(): spread = lax.all_to_all(halves, CHIPS, 2, 2, tiled=True)]
    pallas_call x1, Pallas kernels: 7.79 us -> 4.83 us  [slot_products(): pl.pallas_call(slot_kernel, grid_spec=grid_spec, out_shape=jax.ShapeDtype...]
  transfers between devices with their start and end apart: 7 -> 7, of which waited for: 4 -> 5; matrix products, arithmetic and copies ran while one was open for 9% -> 8% of each run, Pallas kernels for 0% -> 0%
where the time goes in v8:
time: 68.9 us; the launch traced here: 68.4 us
  starting transfers between devices  26.7 us (39%)
  waiting for transfers between devices  24.9 us (36%)
  local copies, waits for them, and re-layouts  7.94 us (12%)
  Pallas kernels  4.83 us (7%)
  other arithmetic  3.11 us (5%)
  between operations  0.88 us (1%)
    all_to_all x1, waiting for transfers between devices, shards(): spread = lax.all_to_all(halves, CHIPS, 2, 2, tiled=True)  19.4 us
    all_to_all x1, starting transfers between devices, shards(): spread = lax.all_to_all(halves, CHIPS, 2, 2, tiled=True)  14.8 us
    ppermute x3, starting transfers between devices, exchange_rows(): lax.ppermute(block, 'row', [(i, (i + shift) % size) for i in range(size)])  5.85 us
    pallas_call x1, Pallas kernels, slot_products(): pl.pallas_call(slot_kernel, grid_spec=grid_spec, out_shape=jax.ShapeDtype...  4.83 us
    ppermute x1, starting transfers between devices, shards(): summed = mine + lax.ppermute(other, 'c', [(0, 1), (1, 0)])  4.39 us
    ppermute x1, waiting for transfers between devices, shards(): before = lax.ppermute(amplitudes, TILE, up)  3.95 us
    ppermute x1, starting transfers between devices, shards(): after = lax.ppermute(amplitudes, TILE, down)  1.74 us
  transfers between devices with their start and end apart: 7, of which 5 were waited for; matrix products, arithmetic and copies ran while one was open for 8% of the time, Pallas kernels for 0%

profile of v8, /device:TPU:32, one launch (start us, length us, event | category | flops | bytes accessed | tf_op | source)
XLA Modules:
  0.0 68.4 jit_solution(7586076508122468570)
XLA Ops:
  0.0 1.7 %collective-permute-start.1 = (f32[9,64,256]{2,1,0:T(8,128)}, f32[9,64,256]{2,1,0:T(8,128)S(1)}, u32[]{:S(2)}, u32[]{:S(2)}) collective-permute-start(f32[9,64,256]{2,1,0:T(8,128)} %own_ref.1), channel_id=1, source_target_pairs={{4,0},{8,4},{12,8},{16,12},{20,16},{24,20},{28,24},{32,28},{36,32}... | collective-permute-start | bytes 1769480 | tf_op jit(solution)/shard_map/ppermute | solution.py:149
  1.7 0.8 %slice_bitcast_fusion = (s32[64]{0:T(128)S(1)}, s32[64]{0:T(128)S(1)}) fusion(s32[64,2]{0,1:T(2,128)} %param.13), kind=kLoop, calls=%fused_computation.35 | loop fusion | bytes 1024 | tf_op jit(solution)/shard_map/eq | solution.py:34
  3.4 0.7 %gather_fusion.1 = s32[32]{0:T(128)S(1)} fusion(s32[64]{0:T(128)S(1)} %select_reduce_fusion, s32[1024]{0:T(1024)S(1)} %pad_clamp_fusion.1), kind=kCustom, calls=%fused_computation.3 | custom fusion | bytes 384 | tf_op jit(solution)/shard_map/gather | solution.py:155
  4.1 0.7 %fusion.1 = s32[64]{0:T(128)S(1)} fusion(s32[1,64]{1,0:T(1,128)} %param.11, s32[]{:T(128)S(6)} %add.158), kind=kLoop, calls=%fused_computation.28 | loop fusion | flops 1728 | bytes 516 | tf_op jit(solution)/shard_map/add | solution.py:163
  4.8 0.7 %pad_add_fusion.index_ref = s32[128]{0:T(128)S(1)} fusion(s32[64]{0:T(128)} %bitcast.44, s32[64]{0:T(128)S(1)} %fusion.1), kind=kLoop, calls=%fused_computation.33 | loop fusion | flops 128 | bytes 1024 | tf_op jit(solution)/shard_map/concatenate | solution.py:163
  5.6 3.9 %collective-permute-done.before_ref = f32[9,64,256]{2,1,0:T(8,128)S(1)} collective-permute-done((f32[9,64,256]{2,1,0:T(8,128)}, f32[9,64,256]{2,1,0:T(8,128)S(1)}, u32[]{:S(2)}, u32[]{:S(2)}) %collective-permute-start) | collective-permute-done | bytes 589856 | tf_op jit(solution)/shard_map/ppermute | solution.py:148
  9.5 1.1 %copy-done = f32[9,64,256]{2,1,0:T(8,128)S(1)} copy-done((f32[9,64,256]{2,1,0:T(8,128)S(1)}, f32[9,64,256]{2,1,0:T(8,128)}, u32[]{:S(2)}) %copy-start) | copy-done | bytes 589848
  10.6 4.8 %shard_map.64 = f32[18,64,128]{2,1,0:T(8,128)S(1)} custom-call(s32[128]{0:T(128)S(1)} %pad_add_fusion.index_ref, s32[1]{0:T(128)} %bitcast.39.live_ref, f32[9,64,256]{2,1,0:T(8,128)S(1)} %collective-permute-done.before_ref, f32[9,64,256]{2,1,0:T(8,128)S(1)} %copy-done, f32[9,64,256]{2,1,0:T(8,128)S(1)} %collective-permute-done.1.after_ref, ...), custom_call_target="tpu_custom_call" | custom-call | flops 1610612736 | bytes 10747904 | tf_op jit(solution)/shard_map/pallas_call | solution.py:109
  15.4 0.4 copy.27
  15.8 0.6 gather_fusion.3
  16.7 4.4 %collective-permute-start.2 = (f32[18,64,128]{2,1,0:T(8,128)S(1)}, f32[18,64,128]{2,1,0:T(8,128)S(1)}, u32[]{:S(2)}, u32[]{:S(2)}) collective-permute-start(f32[18,64,128]{2,1,0:T(8,128)S(1)} %copy.29), channel_id=1, source_target_pairs={{0,4},{4,0},{1,5},{5,1},{2,6},{6,2},{3,7},{7,3},{8,12},{12,8},{9,1... | collective-permute-start | bytes 1769480 | tf_op jit(solution)/shard_map/ppermute | solution.py:173
  21.1 0.7 %gather_fusion = s32[32]{0:T(128)S(1)} fusion(s32[64]{0:T(128)S(1)} %select_reduce_fusion, s32[1024]{0:T(1024)S(1)} %pad_clamp_fusion.3), kind=kCustom, calls=%fused_computation.2 | custom fusion | bytes 384 | tf_op jit(solution)/shard_map/gather | solution.py:154
  21.9 0.6 gather_fusion.2
  22.7 0.4 bitcast_add_fusion
  23.1 1.3 %copy.31 = f32[18,2,32,128]{3,1,0,2:T(2,128)} copy(f32[18,2,32,128]{3,0,2,1:T(8,128)S(1)} %bitcast.41) | data formatting | bytes 1179648 | tf_op jit(solution)/shard_map/reshape | solution.py:174
  24.4 14.8 %all-to-all-start = ((f32[18,2,32,128]{3,1,0,2:T(2,128)}), f32[18,2,32,128]{3,1,0,2:T(2,128)S(1)}, u32[]{:S(2)}, u32[]{:S(2)}) async-start(f32[18,2,32,128]{3,1,0,2:T(2,128)} %copy.31), calls=%async_computation | async-start | bytes 1179648 | tf_op jit(solution)/shard_map/all_to_all | solution.py:175
  39.2 19.4 %all-to-all-done = f32[18,2,32,128]{3,1,0,2:T(2,128)S(1)} async-done(((f32[18,2,32,128]{3,1,0,2:T(2,128)}), f32[18,2,32,128]{3,1,0,2:T(2,128)S(1)}, u32[]{:S(2)}, u32[]{:S(2)}) %all-to-all-start) | async-done | bytes 589856 | tf_op jit(solution)/shard_map/all_to_all | solution.py:175
  59.2 2.4 %collective-permute-start.3 = (f32[1,24,24]{1,2,0:T(8,128)S(1)}, f32[1,24,24]{1,2,0:T(8,128)S(1)}, u32[]{:S(2)}, u32[]{:S(2)}) collective-permute-start(f32[1,24,24]{1,2,0:T(8,128)S(1)} %copy.43), channel_id=1, source_target_pairs={{0,1},{1,2},{2,3},{3,0},{4,5},{5,6},{6,7},{7,4},{8,9},{9,10},{10,1... | collective-permute-start | bytes 6920 | tf_op jit(solution)/shard_map/ppermute | solution.py:132
  61.7 2.1 %collective-permute-start.4 = (f32[1,24,24]{1,2,0:T(8,128)S(1)}, f32[1,24,24]{1,2,0:T(8,128)S(1)}, u32[]{:S(2)}, u32[]{:S(2)}) collective-permute-start(f32[1,24,24]{1,2,0:T(8,128)S(1)} %copy.44), channel_id=1, source_target_pairs={{0,2},{1,3},{2,0},{3,1},{4,6},{5,7},{6,4},{7,5},{8,10},{9,11},{10,... | collective-permute-start | bytes 6920 | tf_op jit(solution)/shard_map/ppermute | solution.py:132
  63.9 1.3 %collective-permute-start.5 = (f32[1,24,24]{1,2,0:T(8,128)S(1)}, f32[1,24,24]{1,2,0:T(8,128)S(1)}, u32[]{:S(2)}, u32[]{:S(2)}) collective-permute-start(f32[1,24,24]{1,2,0:T(8,128)S(1)} %copy.45), channel_id=1, source_target_pairs={{0,3},{1,0},{2,1},{3,2},{4,7},{5,4},{6,5},{7,6},{8,11},{9,8},{10,9... | collective-permute-start | bytes 6920 | tf_op jit(solution)/shard_map/ppermute | solution.py:132
  65.7 0.3 dynamic_update_slice.13
  66.1 0.8 %collective-permute-done.4 = f32[1,24,24]{1,2,0:T(8,128)S(1)} collective-permute-done((f32[1,24,24]{1,2,0:T(8,128)S(1)}, f32[1,24,24]{1,2,0:T(8,128)S(1)}, u32[]{:S(2)}, u32[]{:S(2)}) %collective-permute-start.4) | collective-permute-done | bytes 2336 | tf_op jit(solution)/shard_map/ppermute | solution.py:132
  67.1 0.5 collective-permute-done.5
  67.8 0.6 bitcast_add_fusion.1
  (36 shorter events, 2.4 us)
Async XLA Ops:
  0.0 9.5 %collective-permute-start = (f32[9,64,256]{2,1,0:T(8,128)}, f32[9,64,256]{2,1,0:T(8,128)S(1)}, u32[]{:S(2)}, u32[]{:S(2)}) collective-permute-start(f32[9,64,256]{2,1,0:T(8,128)} %own_ref.1), channel_id=1, source_target_pairs={{0,4},{4,8},{8,12},{12,16},{16,20},{20,24},{24,28},{28,32},{32,36}... | collective-permute-start | bytes 1769480 | tf_op jit(solution)/shard_map/ppermute | solution.py:148
  0.0 9.5 %collective-permute-start.1 = (f32[9,64,256]{2,1,0:T(8,128)}, f32[9,64,256]{2,1,0:T(8,128)S(1)}, u32[]{:S(2)}, u32[]{:S(2)}) collective-permute-start(f32[9,64,256]{2,1,0:T(8,128)} %own_ref.1), channel_id=1, source_target_pairs={{4,0},{8,4},{12,8},{16,12},{20,16},{24,20},{28,24},{32,28},{36,32}... | collective-permute-start | bytes 1769480 | tf_op jit(solution)/shard_map/ppermute | solution.py:149
  9.5 1.1 %copy-start = (f32[9,64,256]{2,1,0:T(8,128)S(1)}, f32[9,64,256]{2,1,0:T(8,128)}, u32[]{:S(2)}) copy-start(f32[9,64,256]{2,1,0:T(8,128)} %own_ref.1) | copy-start | bytes 1769476
  16.7 6.0 %collective-permute-start.2 = (f32[18,64,128]{2,1,0:T(8,128)S(1)}, f32[18,64,128]{2,1,0:T(8,128)S(1)}, u32[]{:S(2)}, u32[]{:S(2)}) collective-permute-start(f32[18,64,128]{2,1,0:T(8,128)S(1)} %copy.29), channel_id=1, source_target_pairs={{0,4},{4,0},{1,5},{5,1},{2,6},{6,2},{3,7},{7,3},{8,12},{12,8},{9,1... | collective-permute-start | bytes 1769480 | tf_op jit(solution)/shard_map/ppermute | solution.py:173
  24.4 34.2 %all-to-all-start = ((f32[18,2,32,128]{3,1,0,2:T(2,128)}), f32[18,2,32,128]{3,1,0,2:T(2,128)S(1)}, u32[]{:S(2)}, u32[]{:S(2)}) async-start(f32[18,2,32,128]{3,1,0,2:T(2,128)} %copy.31), calls=%async_computation | async-start | bytes 1179648 | tf_op jit(solution)/shard_map/all_to_all | solution.py:175
  59.2 6.5 %collective-permute-start.3 = (f32[1,24,24]{1,2,0:T(8,128)S(1)}, f32[1,24,24]{1,2,0:T(8,128)S(1)}, u32[]{:S(2)}, u32[]{:S(2)}) collective-permute-start(f32[1,24,24]{1,2,0:T(8,128)S(1)} %copy.43), channel_id=1, source_target_pairs={{0,1},{1,2},{2,3},{3,0},{4,5},{5,6},{6,7},{7,4},{8,9},{9,10},{10,1... | collective-permute-start | bytes 6920 | tf_op jit(solution)/shard_map/ppermute | solution.py:132
  61.7 5.2 %collective-permute-start.4 = (f32[1,24,24]{1,2,0:T(8,128)S(1)}, f32[1,24,24]{1,2,0:T(8,128)S(1)}, u32[]{:S(2)}, u32[]{:S(2)}) collective-permute-start(f32[1,24,24]{1,2,0:T(8,128)S(1)} %copy.44), channel_id=1, source_target_pairs={{0,2},{1,3},{2,0},{3,1},{4,6},{5,7},{6,4},{7,5},{8,10},{9,11},{10,... | collective-permute-start | bytes 6920 | tf_op jit(solution)/shard_map/ppermute | solution.py:132
  63.9 3.7 %collective-permute-start.5 = (f32[1,24,24]{1,2,0:T(8,128)S(1)}, f32[1,24,24]{1,2,0:T(8,128)S(1)}, u32[]{:S(2)}, u32[]{:S(2)}) collective-permute-start(f32[1,24,24]{1,2,0:T(8,128)S(1)} %copy.45), channel_id=1, source_target_pairs={{0,3},{1,0},{2,1},{3,2},{4,7},{5,4},{6,5},{7,6},{8,11},{9,8},{10,9... | collective-permute-start | bytes 6920 | tf_op jit(solution)/shard_map/ppermute | solution.py:132

commit v9 on v8

--- a/solution.py
+++ b/solution.py
@@ -168,8 +168,16 @@
         integrals[0],
         tiles_ab,
     )
-    mine = jnp.take(totals, keep_rows, axis=1)
-    other = jnp.take(totals, send_rows, axis=1)
+    pairs_axis = jnp.arange(pair_count, dtype=jnp.int32)[None, :]
+    pick = lambda rows: jnp.einsum(
+        "qp,epb->eqb",
+        (rows[:, None] == pairs_axis).astype(jnp.float32),
+        totals,
+        precision=lax.Precision.HIGHEST,
+        preferred_element_type=jnp.float32,
+    )
+    mine = pick(keep_rows)
+    other = pick(send_rows)
     summed = mine + lax.ppermute(other, "c", [(0, 1), (1, 0)])
     halves = summed.reshape(tiles_ab, 2, pair_count // cores, summed.shape[2])
     spread = lax.all_to_all(halves, CHIPS, 2, 2, tiled=True)

time: 68.9 us -> 68 us (0.987)
  starting transfers between devices: 26.7 us -> 19.8 us
  Pallas kernels: 4.83 us -> 11.7 us
  local copies, waits for them, and re-layouts: 7.94 us -> 6.38 us
  matrix products: 0 us -> 0.88 us
    pallas_call x1, Pallas kernels: 4.83 us -> 11.7 us  [slot_products(): pl.pallas_call(slot_kernel, grid_spec=grid_spec, out_shape=jax.ShapeDtype...]
    ppermute x1, starting transfers between devices: 4.39 us -> 0.09 us  [shards(): summed = mine + lax.ppermute(other, 'c', [(0, 1), (1, 0)])]
    all_to_all x1, starting transfers between devices: 14.8 us -> 12.4 us  [shards(): spread = lax.all_to_all(halves, CHIPS, 2, 2, tiled=True)]
    gather x2 -> x0, local copies, waits for them, and re-layouts: 1.27 us -> none  [the longest x1 0.64 us: shards(): mine = jnp.take(totals, keep_rows, axis=1)]
    ppermute x3, waiting for transfers between devices: 1.32 us -> 0.2 us  [exchange_rows(): lax.ppermute(block, 'row', [(i, (i + shift) % size) for i in range(size)])]
    ppermute x1, waiting for transfers between devices: 0.18 us -> 1.18 us  [shards(): summed = mine + lax.ppermute(other, 'c', [(0, 1), (1, 0)])]
    dot_general x0 -> x2, matrix products: none -> 0.88 us  [shards(): jnp.einsum('qp,epb->eqb', (rows[:, None] == pairs_axis).astype(jnp.float3...]
  transfers between devices with their start and end apart: 7 -> 7, of which waited for: 5 -> 4; matrix products, arithmetic and copies ran while one was open for 8% -> 8% of each run, Pallas kernels for 0% -> 0%
where the time goes in v9:
time: 68 us; the launch traced here: 67 us
  waiting for transfers between devices  24.8 us (36%)
  starting transfers between devices  19.8 us (29%)
  Pallas kernels  11.7 us (17%)
  local copies, waits for them, and re-layouts  6.38 us (9%)
  other arithmetic  2.54 us (4%)
  matrix products  0.88 us (1%)
  between operations  0.86 us (1%)
    all_to_all x1, waiting for transfers between devices, shards(): spread = lax.all_to_all(halves, CHIPS, 2, 2, tiled=True)  19.4 us
    all_to_all x1, starting transfers between devices, shards(): spread = lax.all_to_all(halves, CHIPS, 2, 2, tiled=True)  12.4 us
    pallas_call x1, Pallas kernels, slot_products(): pl.pallas_call(slot_kernel, grid_spec=grid_spec, out_shape=jax.ShapeDtype...  11.7 us
    ppermute x3, starting transfers between devices, exchange_rows(): lax.ppermute(block, 'row', [(i, (i + shift) % size) for i in range(size)])  5.57 us
    ppermute x1, waiting for transfers between devices, shards(): before = lax.ppermute(amplitudes, TILE, up)  3.99 us
    ppermute x1, starting transfers between devices, shards(): after = lax.ppermute(amplitudes, TILE, down)  1.74 us
  transfers between devices with their start and end apart: 7, of which 4 were waited for; matrix products, arithmetic and copies ran while one was open for 8% of the time, Pallas kernels for 0%

profile of v9, /device:TPU:32, one launch (start us, length us, event | category | flops | bytes accessed | tf_op | source)
XLA Modules:
  0.0 67.0 jit_solution(15805909797016544690)
XLA Ops:
  0.0 1.7 %collective-permute-start.1 = (f32[9,64,256]{2,1,0:T(8,128)}, f32[9,64,256]{2,1,0:T(8,128)S(1)}, u32[]{:S(2)}, u32[]{:S(2)}) collective-permute-start(f32[9,64,256]{2,1,0:T(8,128)} %own_ref.1), channel_id=1, source_target_pairs={{4,0},{8,4},{12,8},{16,12},{20,16},{24,20},{28,24},{32,28},{36,32}... | collective-permute-start | bytes 1769480 | tf_op jit(solution)/shard_map/ppermute | solution.py:149
  1.7 0.8 %slice_bitcast_fusion = (s32[64]{0:T(128)S(1)}, s32[64]{0:T(128)S(1)}) fusion(s32[64,2]{0,1:T(2,128)} %param.11), kind=kLoop, calls=%fused_computation.38 | loop fusion | bytes 1024 | tf_op jit(solution)/shard_map/eq | solution.py:34
  3.4 0.7 %gather_fusion.1 = s32[32]{0:T(128)S(1)} fusion(s32[64]{0:T(128)S(1)} %select_reduce_fusion, s32[1024]{0:T(1024)S(1)} %pad_clamp_fusion), kind=kCustom, calls=%fused_computation.1 | custom fusion | bytes 384 | tf_op jit(solution)/shard_map/gather | solution.py:155
  4.1 0.7 %fusion.8 = (s32[64]{0:T(128)S(1)}, s32[64]{0:T(128)S(1)}) fusion(s32[1,64]{1,0:T(1,128)} %param.9, s32[]{:T(128)S(6)} %add.152, s32[32]{0:T(128)S(1)} %gather_fusion.1, s32[32]{0:T(128)S(1)} %fusion.13), kind=kLoop, calls=%fused_computation.29 | loop fusion | flops 1792 | bytes 1028 | tf_op jit(solution)/shard_map/add | solution.py:163
  4.8 0.7 %pad_add_fusion.index_ref = s32[128]{0:T(128)S(1)} fusion(s32[64]{0:T(128)} %bitcast.50, s32[64]{0:T(128)S(1)} %get-tuple-element.13), kind=kLoop, calls=%fused_computation.34 | loop fusion | flops 128 | bytes 1024 | tf_op jit(solution)/shard_map/concatenate | solution.py:163
  5.5 4.0 %collective-permute-done.before_ref = f32[9,64,256]{2,1,0:T(8,128)S(1)} collective-permute-done((f32[9,64,256]{2,1,0:T(8,128)}, f32[9,64,256]{2,1,0:T(8,128)S(1)}, u32[]{:S(2)}, u32[]{:S(2)}) %collective-permute-start) | collective-permute-done | bytes 589856 | tf_op jit(solution)/shard_map/ppermute | solution.py:148
  9.5 1.1 %copy-done = f32[9,64,256]{2,1,0:T(8,128)S(1)} copy-done((f32[9,64,256]{2,1,0:T(8,128)S(1)}, f32[9,64,256]{2,1,0:T(8,128)}, u32[]{:S(2)}) %copy-start) | copy-done | bytes 589848
  10.6 11.7 %shard_map.64 = f32[18,64,128]{2,1,0:T(8,128)S(1)} custom-call(s32[128]{0:T(128)S(1)} %pad_add_fusion.index_ref, s32[1]{0:T(128)} %bitcast.45.live_ref, f32[9,64,256]{2,1,0:T(8,128)S(1)} %collective-permute-done.before_ref, f32[9,64,256]{2,1,0:T(8,128)S(1)} %copy-done, f32[9,64,256]{2,1,0:T(8,128)S(1)} %collective-permute-done.1.after_ref, ...), custom_call_target="tpu_custom_call" | custom-call | flops 1610612736 | bytes 10747904 | tf_op jit(solution)/shard_map/pallas_call | solution.py:109
  22.2 0.4 convolution_bitcast_fusion
  22.8 0.7 %gather_fusion = s32[32]{0:T(128)S(1)} fusion(s32[64]{0:T(128)S(1)} %select_reduce_fusion, s32[1024]{0:T(1024)S(1)} %pad_clamp_fusion.1), kind=kCustom, calls=%fused_computation | custom fusion | bytes 384 | tf_op jit(solution)/shard_map/gather | solution.py:154
  23.6 1.2 %collective-permute-done.2 = f32[18,64,128]{2,1,0:T(8,128)S(1)} collective-permute-done((f32[18,64,128]{2,1,0:T(8,128)S(1)}, f32[18,64,128]{2,1,0:T(8,128)S(1)}, u32[]{:S(2)}, u32[]{:S(2)}) %collective-permute-start.2) | collective-permute-done | bytes 589856 | tf_op jit(solution)/shard_map/ppermute | solution.py:181
  24.8 0.4 fusion
  25.2 1.3 %copy.20 = f32[18,2,32,128]{3,1,0,2:T(2,128)} copy(f32[18,2,32,128]{3,2,1,0:T(8,128)S(1)} %bitcast.47) | data formatting | bytes 1179648 | tf_op jit(solution)/shard_map/reshape | solution.py:182
  26.5 12.4 %all-to-all-start = ((f32[18,2,32,128]{3,1,0,2:T(2,128)}), f32[18,2,32,128]{3,1,0,2:T(2,128)S(1)}, u32[]{:S(2)}, u32[]{:S(2)}) async-start(f32[18,2,32,128]{3,1,0,2:T(2,128)} %copy.20), calls=%async_computation | async-start | bytes 1179648 | tf_op jit(solution)/shard_map/all_to_all | solution.py:183
  39.0 19.4 %all-to-all-done = f32[18,2,32,128]{3,1,0,2:T(2,128)S(1)} async-done(((f32[18,2,32,128]{3,1,0,2:T(2,128)}), f32[18,2,32,128]{3,1,0,2:T(2,128)S(1)}, u32[]{:S(2)}, u32[]{:S(2)}) %all-to-all-start) | async-done | bytes 589856 | tf_op jit(solution)/shard_map/all_to_all | solution.py:183
  59.0 0.7 collective-permute-start.3
  59.8 2.3 %collective-permute-start.4 = (f32[1,24,24]{1,2,0:T(8,128)S(1)}, f32[1,24,24]{1,2,0:T(8,128)S(1)}, u32[]{:S(2)}, u32[]{:S(2)}) collective-permute-start(f32[1,24,24]{1,2,0:T(8,128)S(1)} %copy.29), channel_id=1, source_target_pairs={{0,2},{1,3},{2,0},{3,1},{4,6},{5,7},{6,4},{7,5},{8,10},{9,11},{10,... | collective-permute-start | bytes 6920 | tf_op jit(solution)/shard_map/ppermute | solution.py:132
  62.2 2.6 %collective-permute-start.5 = (f32[1,24,24]{1,2,0:T(8,128)S(1)}, f32[1,24,24]{1,2,0:T(8,128)S(1)}, u32[]{:S(2)}, u32[]{:S(2)}) collective-permute-start(f32[1,24,24]{1,2,0:T(8,128)S(1)} %copy.30), channel_id=1, source_target_pairs={{0,3},{1,0},{2,1},{3,2},{4,7},{5,4},{6,5},{7,6},{8,11},{9,8},{10,9... | collective-permute-start | bytes 6920 | tf_op jit(solution)/shard_map/ppermute | solution.py:132
  65.0 0.2 dynamic_update_slice.12
  65.3 0.3 dynamic_update_slice.13
  65.6 0.3 dynamic_update_slice.14
  66.0 0.2 collective-permute-done.5
  66.2 0.2 dynamic_update_slice.15
  66.3 0.6 bitcast_add_fusion
  (28 shorter events, 1.4 us)
Async XLA Ops:
  0.0 9.5 %collective-permute-start = (f32[9,64,256]{2,1,0:T(8,128)}, f32[9,64,256]{2,1,0:T(8,128)S(1)}, u32[]{:S(2)}, u32[]{:S(2)}) collective-permute-start(f32[9,64,256]{2,1,0:T(8,128)} %own_ref.1), channel_id=1, source_target_pairs={{0,4},{4,8},{8,12},{12,16},{16,20},{20,24},{24,28},{28,32},{32,36}... | collective-permute-start | bytes 1769480 | tf_op jit(solution)/shard_map/ppermute | solution.py:148
  0.0 9.5 %collective-permute-start.1 = (f32[9,64,256]{2,1,0:T(8,128)}, f32[9,64,256]{2,1,0:T(8,128)S(1)}, u32[]{:S(2)}, u32[]{:S(2)}) collective-permute-start(f32[9,64,256]{2,1,0:T(8,128)} %own_ref.1), channel_id=1, source_target_pairs={{4,0},{8,4},{12,8},{16,12},{20,16},{24,20},{28,24},{32,28},{36,32}... | collective-permute-start | bytes 1769480 | tf_op jit(solution)/shard_map/ppermute | solution.py:149
  9.5 1.1 %copy-start = (f32[9,64,256]{2,1,0:T(8,128)S(1)}, f32[9,64,256]{2,1,0:T(8,128)}, u32[]{:S(2)}) copy-start(f32[9,64,256]{2,1,0:T(8,128)} %own_ref.1) | copy-start | bytes 1769476
  22.7 2.1 %collective-permute-start.2 = (f32[18,64,128]{2,1,0:T(8,128)S(1)}, f32[18,64,128]{2,1,0:T(8,128)S(1)}, u32[]{:S(2)}, u32[]{:S(2)}) collective-permute-start(f32[18,64,128]{2,1,0:T(8,128)S(1)} %convolution_bitcast_fusion), channel_id=1, source_target_pairs={{0,4},{4,0},{1,5},{5,1},{2,6},{6,2},{3,7},{7,3},{8,12},{12,8},{9,1... | collective-permute-start | bytes 1769480 | tf_op jit(solution)/shard_map/ppermute | solution.py:181
  26.5 31.9 %all-to-all-start = ((f32[18,2,32,128]{3,1,0,2:T(2,128)}), f32[18,2,32,128]{3,1,0,2:T(2,128)S(1)}, u32[]{:S(2)}, u32[]{:S(2)}) async-start(f32[18,2,32,128]{3,1,0,2:T(2,128)} %copy.20), calls=%async_computation | async-start | bytes 1179648 | tf_op jit(solution)/shard_map/all_to_all | solution.py:183
  59.0 6.2 %collective-permute-start.3 = (f32[1,24,24]{1,2,0:T(8,128)S(1)}, f32[1,24,24]{1,2,0:T(8,128)S(1)}, u32[]{:S(2)}, u32[]{:S(2)}) collective-permute-start(f32[1,24,24]{1,2,0:T(8,128)S(1)} %copy.28), channel_id=1, source_target_pairs={{0,1},{1,2},{2,3},{3,0},{4,5},{5,6},{6,7},{7,4},{8,9},{9,10},{10,1... | collective-permute-start | bytes 6920 | tf_op jit(solution)/shard_map/ppermute | solution.py:132
  59.8 5.9 %collective-permute-start.4 = (f32[1,24,24]{1,2,0:T(8,128)S(1)}, f32[1,24,24]{1,2,0:T(8,128)S(1)}, u32[]{:S(2)}, u32[]{:S(2)}) collective-permute-start(f32[1,24,24]{1,2,0:T(8,128)S(1)} %copy.29), channel_id=1, source_target_pairs={{0,2},{1,3},{2,0},{3,1},{4,6},{5,7},{6,4},{7,5},{8,10},{9,11},{10,... | collective-permute-start | bytes 6920 | tf_op jit(solution)/shard_map/ppermute | solution.py:132
  62.2 4.0 %collective-permute-start.5 = (f32[1,24,24]{1,2,0:T(8,128)S(1)}, f32[1,24,24]{1,2,0:T(8,128)S(1)}, u32[]{:S(2)}, u32[]{:S(2)}) collective-permute-start(f32[1,24,24]{1,2,0:T(8,128)S(1)} %copy.30), channel_id=1, source_target_pairs={{0,3},{1,0},{2,1},{3,2},{4,7},{5,4},{6,5},{7,6},{8,11},{9,8},{10,9... | collective-permute-start | bytes 6920 | tf_op jit(solution)/shard_map/ppermute | solution.py:132

commit v10 on v9

--- a/solution.py
+++ b/solution.py
@@ -169,9 +169,10 @@
         tiles_ab,
     )
     pairs_axis = jnp.arange(pair_count, dtype=jnp.int32)[None, :]
+    chips = pair_count // cores
     pick = lambda rows: jnp.einsum(
-        "qp,epb->eqb",
-        (rows[:, None] == pairs_axis).astype(jnp.float32),
+        "qp,epb->qeb",
+        (rows.reshape(2, chips).T.reshape(-1)[:, None] == pairs_axis).astype(jnp.float32),
         totals,
         precision=lax.Precision.HIGHEST,
         preferred_element_type=jnp.float32,
@@ -179,11 +180,11 @@
     mine = pick(keep_rows)
     other = pick(send_rows)
     summed = mine + lax.ppermute(other, "c", [(0, 1), (1, 0)])
-    halves = summed.reshape(tiles_ab, 2, pair_count // cores, summed.shape[2])
-    spread = lax.all_to_all(halves, CHIPS, 2, 2, tiled=True)
-    reduced = jnp.sum(spread, axis=2)
-    own = to_grid(reduced[:, 0][:, None], a_tiles, b_tiles)
-    mirrored = to_grid(reduced[:, 1][:, None], a_tiles, b_tiles)
+    halves = summed.reshape(chips, 2 * summed.shape[1], summed.shape[2])
+    spread = lax.all_to_all(halves, CHIPS, 0, 0, tiled=True)
+    reduced = jnp.sum(spread, axis=0).reshape(2, tiles_ab, summed.shape[2])
+    own = to_grid(reduced[0][:, None], a_tiles, b_tiles)
+    mirrored = to_grid(reduced[1][:, None], a_tiles, b_tiles)
     turned = jnp.transpose(exchange_rows(mirrored), (0, 2, 1))
     return own + turned
 

time: 68 us -> 69.2 us (1.018)
  starting transfers between devices: 19.8 us -> 27.3 us
  Pallas kernels: 11.7 us -> 4.83 us
  waiting for transfers between devices: 24.8 us -> 25.8 us
    pallas_call x1, Pallas kernels: 11.7 us -> 4.83 us  [slot_products(): pl.pallas_call(slot_kernel, grid_spec=grid_spec, out_shape=jax.ShapeDtype...]
    ppermute x1, starting transfers between devices: 0.09 us -> 4.39 us  [shards(): summed = mine + lax.ppermute(other, 'c', [(0, 1), (1, 0)])]
    all_to_all x1, starting transfers between devices: 12.4 us -> 15.3 us  [shards(): spread = lax.all_to_all(halves, CHIPS, 0, 0, tiled=True)]
    all_to_all x1, waiting for transfers between devices: 19.4 us -> 20.5 us  [shards(): spread = lax.all_to_all(halves, CHIPS, 0, 0, tiled=True)]
    ppermute x3, waiting for transfers between devices: 0.2 us -> 1.01 us  [exchange_rows(): lax.ppermute(block, 'row', [(i, (i + shift) % size) for i in range(size)])]
  transfers between devices with their start and end apart: 7 -> 7, of which waited for: 4 -> 5; matrix products, arithmetic and copies ran while one was open for 8% -> 8% of each run, Pallas kernels for 0% -> 0%
where the time goes in v10:
time: 69.2 us; the launch traced here: 68.8 us
  starting transfers between devices  27.3 us (39%)
  waiting for transfers between devices  25.8 us (37%)
  local copies, waits for them, and re-layouts  6.73 us (10%)
  Pallas kernels  4.83 us (7%)
  other arithmetic  2.43 us (4%)
  matrix products  0.9 us (1%)
  between operations  0.87 us (1%)
    all_to_all x1, waiting for transfers between devices, shards(): spread = lax.all_to_all(halves, CHIPS, 0, 0, tiled=True)  20.5 us
    all_to_all x1, starting transfers between devices, shards(): spread = lax.all_to_all(halves, CHIPS, 0, 0, tiled=True)  15.3 us
    ppermute x3, starting transfers between devices, exchange_rows(): lax.ppermute(block, 'row', [(i, (i + shift) % size) for i in range(size)])  5.85 us
    pallas_call x1, Pallas kernels, slot_products(): pl.pallas_call(slot_kernel, grid_spec=grid_spec, out_shape=jax.ShapeDtype...  4.83 us
    ppermute x1, starting transfers between devices, shards(): summed = mine + lax.ppermute(other, 'c', [(0, 1), (1, 0)])  4.39 us
    ppermute x1, waiting for transfers between devices, shards(): before = lax.ppermute(amplitudes, TILE, up)  3.67 us
    ppermute x1, starting transfers between devices, shards(): after = lax.ppermute(amplitudes, TILE, down)  1.74 us
  transfers between devices with their start and end apart: 7, of which 5 were waited for; matrix products, arithmetic and copies ran while one was open for 8% of the time, Pallas kernels for 0%

profile of v10, /device:TPU:32, one launch (start us, length us, event | category | flops | bytes accessed | tf_op | source)
XLA Modules:
  0.0 68.8 jit_solution(2083002299118114569)
XLA Ops:
  0.0 1.7 %collective-permute-start.1 = (f32[9,64,256]{2,1,0:T(8,128)}, f32[9,64,256]{2,1,0:T(8,128)S(1)}, u32[]{:S(2)}, u32[]{:S(2)}) collective-permute-start(f32[9,64,256]{2,1,0:T(8,128)} %own_ref.1), channel_id=1, source_target_pairs={{4,0},{8,4},{12,8},{16,12},{20,16},{24,20},{28,24},{32,28},{36,32}... | collective-permute-start | bytes 1769480 | tf_op jit(solution)/shard_map/ppermute | solution.py:149
  1.7 0.8 %slice_bitcast_fusion = (s32[64]{0:T(128)S(1)}, s32[64]{0:T(128)S(1)}) fusion(s32[64,2]{0,1:T(2,128)} %param.11), kind=kLoop, calls=%fused_computation.35 | loop fusion | bytes 1024 | tf_op jit(solution)/shard_map/eq | solution.py:34
  3.4 0.7 %gather_fusion.1 = s32[32]{0:T(128)S(1)} fusion(s32[64]{0:T(128)S(1)} %select_reduce_fusion, s32[1024]{0:T(1024)S(1)} %pad_clamp_fusion), kind=kCustom, calls=%fused_computation.1 | custom fusion | bytes 384 | tf_op jit(solution)/shard_map/gather | solution.py:155
  4.4 0.7 fusion.8
  5.1 0.7 %pad_add_fusion.1.index_ref = s32[128]{0:T(128)S(1)} fusion(s32[64]{0:T(128)} %bitcast.46, s32[64]{0:T(128)S(1)} %fusion.8), kind=kLoop, calls=%fused_computation.32 | loop fusion | flops 128 | bytes 1024 | tf_op jit(solution)/shard_map/concatenate | solution.py:163
  5.8 3.7 %collective-permute-done.before_ref = f32[9,64,256]{2,1,0:T(8,128)S(1)} collective-permute-done((f32[9,64,256]{2,1,0:T(8,128)}, f32[9,64,256]{2,1,0:T(8,128)S(1)}, u32[]{:S(2)}, u32[]{:S(2)}) %collective-permute-start) | collective-permute-done | bytes 589856 | tf_op jit(solution)/shard_map/ppermute | solution.py:148
  9.5 1.1 %copy-done = f32[9,64,256]{2,1,0:T(8,128)S(1)} copy-done((f32[9,64,256]{2,1,0:T(8,128)S(1)}, f32[9,64,256]{2,1,0:T(8,128)}, u32[]{:S(2)}) %copy-start) | copy-done | bytes 589848
  10.6 4.8 %shard_map.64 = f32[18,64,128]{2,1,0:T(8,128)S(1)} custom-call(s32[128]{0:T(128)S(1)} %pad_add_fusion.1.index_ref, s32[1]{0:T(128)} %bitcast.40.live_ref, f32[9,64,256]{2,1,0:T(8,128)S(1)} %collective-permute-done.before_ref, f32[9,64,256]{2,1,0:T(8,128)S(1)} %copy-done, f32[9,64,256]{2,1,0:T(8,128)S(1)} %collective-permute-done.1.after_ref, ...), custom_call_target="tpu_custom_call" | custom-call | flops 1610612736 | bytes 10747904 | tf_op jit(solution)/shard_map/pallas_call | solution.py:109
  15.4 0.4 fusion.3
  15.9 4.4 %collective-permute-start.2 = (f32[64,18,128]{2,0,1:T(8,128)S(1)}, f32[64,18,128]{2,0,1:T(8,128)S(1)}, u32[]{:S(2)}, u32[]{:S(2)}) collective-permute-start(f32[64,18,128]{2,0,1:T(8,128)S(1)} %fusion.3), channel_id=1, source_target_pairs={{0,4},{4,0},{1,5},{5,1},{2,6},{6,2},{3,7},{7,3},{8,12},{12,8},{9,1... | collective-permute-start | bytes 1769480 | tf_op jit(solution)/shard_map/ppermute | solution.py:182
  20.3 0.7 %gather_fusion = s32[32]{0:T(128)S(1)} fusion(s32[64]{0:T(128)S(1)} %select_reduce_fusion, s32[1024]{0:T(1024)S(1)} %pad_clamp_fusion.1), kind=kCustom, calls=%fused_computation | custom fusion | bytes 384 | tf_op jit(solution)/shard_map/gather | solution.py:154
  21.3 0.6 collective-permute-done.2
  21.9 0.5 convolution_add_fusion
  22.4 0.4 copy.20
  22.7 0.9 %reshape.65 = f32[32,36,128]{2,1,0:T(8,128)} reshape(f32[64,18,128]{2,1,0:T(8,128)S(1)} %copy.20) | data formatting | bytes 1179648 | tf_op jit(solution)/shard_map/reshape | solution.py:183
  23.6 15.3 %all-to-all-start = ((f32[32,36,128]{2,1,0:T(8,128)}), f32[32,36,128]{2,1,0:T(8,128)S(1)}, u32[]{:S(2)}, u32[]{:S(2)}) async-start(f32[32,36,128]{2,1,0:T(8,128)} %reshape.65), calls=%async_computation | async-start | bytes 1310720 | tf_op jit(solution)/shard_map/all_to_all | solution.py:184
  39.0 20.5 %all-to-all-done = f32[32,36,128]{2,1,0:T(8,128)S(1)} async-done(((f32[32,36,128]{2,1,0:T(8,128)}), f32[32,36,128]{2,1,0:T(8,128)S(1)}, u32[]{:S(2)}, u32[]{:S(2)}) %all-to-all-start) | async-done | bytes 589856 | tf_op jit(solution)/shard_map/all_to_all | solution.py:184
  60.0 2.1 %collective-permute-start.3 = (f32[1,24,24]{1,2,0:T(8,128)S(1)}, f32[1,24,24]{1,2,0:T(8,128)S(1)}, u32[]{:S(2)}, u32[]{:S(2)}) collective-permute-start(f32[1,24,24]{1,2,0:T(8,128)S(1)} %copy.28), channel_id=1, source_target_pairs={{0,1},{1,2},{2,3},{3,0},{4,5},{5,6},{6,7},{7,4},{8,9},{9,10},{10,1... | collective-permute-start | bytes 6920 | tf_op jit(solution)/shard_map/ppermute | solution.py:132
  62.2 2.1 %collective-permute-start.4 = (f32[1,24,24]{1,2,0:T(8,128)S(1)}, f32[1,24,24]{1,2,0:T(8,128)S(1)}, u32[]{:S(2)}, u32[]{:S(2)}) collective-permute-start(f32[1,24,24]{1,2,0:T(8,128)S(1)} %copy.29), channel_id=1, source_target_pairs={{0,2},{1,3},{2,0},{3,1},{4,6},{5,7},{6,4},{7,5},{8,10},{9,11},{10,... | collective-permute-start | bytes 6920 | tf_op jit(solution)/shard_map/ppermute | solution.py:132
  64.3 1.6 %collective-permute-start.5 = (f32[1,24,24]{1,2,0:T(8,128)S(1)}, f32[1,24,24]{1,2,0:T(8,128)S(1)}, u32[]{:S(2)}, u32[]{:S(2)}) collective-permute-start(f32[1,24,24]{1,2,0:T(8,128)S(1)} %copy.30), channel_id=1, source_target_pairs={{0,3},{1,0},{2,1},{3,2},{4,7},{5,4},{6,5},{7,6},{8,11},{9,8},{10,9... | collective-permute-start | bytes 6920 | tf_op jit(solution)/shard_map/ppermute | solution.py:132
  66.5 0.3 dynamic_update_slice.13
  66.8 0.6 collective-permute-done.4
  67.6 0.4 collective-permute-done.5
  68.2 0.6 bitcast_add_fusion
  (35 shorter events, 2.3 us)
Async XLA Ops:
  0.0 9.5 %collective-permute-start = (f32[9,64,256]{2,1,0:T(8,128)}, f32[9,64,256]{2,1,0:T(8,128)S(1)}, u32[]{:S(2)}, u32[]{:S(2)}) collective-permute-start(f32[9,64,256]{2,1,0:T(8,128)} %own_ref.1), channel_id=1, source_target_pairs={{0,4},{4,8},{8,12},{12,16},{16,20},{20,24},{24,28},{28,32},{32,36}... | collective-permute-start | bytes 1769480 | tf_op jit(solution)/shard_map/ppermute | solution.py:148
  0.0 9.5 %collective-permute-start.1 = (f32[9,64,256]{2,1,0:T(8,128)}, f32[9,64,256]{2,1,0:T(8,128)S(1)}, u32[]{:S(2)}, u32[]{:S(2)}) collective-permute-start(f32[9,64,256]{2,1,0:T(8,128)} %own_ref.1), channel_id=1, source_target_pairs={{4,0},{8,4},{12,8},{16,12},{20,16},{24,20},{28,24},{32,28},{36,32}... | collective-permute-start | bytes 1769480 | tf_op jit(solution)/shard_map/ppermute | solution.py:149
  9.5 1.1 %copy-start = (f32[9,64,256]{2,1,0:T(8,128)S(1)}, f32[9,64,256]{2,1,0:T(8,128)}, u32[]{:S(2)}) copy-start(f32[9,64,256]{2,1,0:T(8,128)} %own_ref.1) | copy-start | bytes 1769476
  15.9 6.0 %collective-permute-start.2 = (f32[64,18,128]{2,0,1:T(8,128)S(1)}, f32[64,18,128]{2,0,1:T(8,128)S(1)}, u32[]{:S(2)}, u32[]{:S(2)}) collective-permute-start(f32[64,18,128]{2,0,1:T(8,128)S(1)} %fusion.3), channel_id=1, source_target_pairs={{0,4},{4,0},{1,5},{5,1},{2,6},{6,2},{3,7},{7,3},{8,12},{12,8},{9,1... | collective-permute-start | bytes 1769480 | tf_op jit(solution)/shard_map/ppermute | solution.py:182
  23.6 35.9 %all-to-all-start = ((f32[32,36,128]{2,1,0:T(8,128)}), f32[32,36,128]{2,1,0:T(8,128)S(1)}, u32[]{:S(2)}, u32[]{:S(2)}) async-start(f32[32,36,128]{2,1,0:T(8,128)} %reshape.65), calls=%async_computation | async-start | bytes 1310720 | tf_op jit(solution)/shard_map/all_to_all | solution.py:184
  60.0 6.5 %collective-permute-start.3 = (f32[1,24,24]{1,2,0:T(8,128)S(1)}, f32[1,24,24]{1,2,0:T(8,128)S(1)}, u32[]{:S(2)}, u32[]{:S(2)}) collective-permute-start(f32[1,24,24]{1,2,0:T(8,128)S(1)} %copy.28), channel_id=1, source_target_pairs={{0,1},{1,2},{2,3},{3,0},{4,5},{5,6},{6,7},{7,4},{8,9},{9,10},{10,1... | collective-permute-start | bytes 6920 | tf_op jit(solution)/shard_map/ppermute | solution.py:132
  62.2 5.2 %collective-permute-start.4 = (f32[1,24,24]{1,2,0:T(8,128)S(1)}, f32[1,24,24]{1,2,0:T(8,128)S(1)}, u32[]{:S(2)}, u32[]{:S(2)}) collective-permute-start(f32[1,24,24]{1,2,0:T(8,128)S(1)} %copy.29), channel_id=1, source_target_pairs={{0,2},{1,3},{2,0},{3,1},{4,6},{5,7},{6,4},{7,5},{8,10},{9,11},{10,... | collective-permute-start | bytes 6920 | tf_op jit(solution)/shard_map/ppermute | solution.py:132
  64.3 3.7 %collective-permute-start.5 = (f32[1,24,24]{1,2,0:T(8,128)S(1)}, f32[1,24,24]{1,2,0:T(8,128)S(1)}, u32[]{:S(2)}, u32[]{:S(2)}) collective-permute-start(f32[1,24,24]{1,2,0:T(8,128)S(1)} %copy.30), channel_id=1, source_target_pairs={{0,3},{1,0},{2,1},{3,2},{4,7},{5,4},{6,5},{7,6},{8,11},{9,8},{10,9... | collective-permute-start | bytes 6920 | tf_op jit(solution)/shard_map/ppermute | solution.py:132

commit v11 on v9

--- a/solution.py
+++ b/solution.py
@@ -125,14 +125,15 @@
     size = lax.axis_size("row")
     index = lax.axis_index("row")
     width = mirrored.shape[1]
-    placed = jnp.zeros((1, size * width, width), mirrored.dtype)
-    for shift in range(size):
-        block = lax.dynamic_slice_in_dim(mirrored, ((index + shift) % size) * width, width, axis=2)
-        if shift:
-            block = lax.ppermute(block, "row", [(i, (i + shift) % size) for i in range(size)])
-        source = (index - shift + size) % size
-        placed = lax.dynamic_update_slice_in_dim(placed, block, source * width, axis=1)
-    return placed
+    received = [mirrored] + [
+        lax.ppermute(mirrored, "row", [(i, (i + shift) % size) for i in range(size)])
+        for shift in range(1, size)
+    ]
+    by_source = jnp.stack(received[::-1] + received[::-1], axis=0)
+    start = (size - 1 - index) % size
+    ordered = lax.dynamic_slice_in_dim(by_source, start, size, axis=0)
+    columns = lax.dynamic_slice_in_dim(ordered, index * width, width, axis=3)
+    return columns.reshape(1, size * width, width)
 
 
 def shards(amplitudes, integrals, slot_ab, slot_cd, live_count, pair_list):

time: 68 us -> 66.7 us (0.981); the launches traced: 67 us -> 66.7 us
  blocking collectives: 0 us -> 35.7 us
  waiting for transfers between devices: 24.8 us -> 8.74 us
  starting transfers between devices: 19.8 us -> 6.53 us
  Pallas kernels: 11.7 us -> 7.1 us
  local copies, waits for them, and re-layouts: 6.38 us -> 4.35 us
    all_to_all x0 -> x1, blocking collectives: none -> 35.7 us  [shards(): spread = lax.all_to_all(halves, CHIPS, 2, 2, tiled=True)]
    all_to_all x1 -> x0, waiting for transfers between devices: 19.4 us -> none  [shards(): spread = lax.all_to_all(halves, CHIPS, 2, 2, tiled=True)]
    all_to_all x1 -> x0, starting transfers between devices: 12.4 us -> none  [shards(): spread = lax.all_to_all(halves, CHIPS, 2, 2, tiled=True)]
    pallas_call x1, Pallas kernels: 11.7 us -> 7.1 us  [slot_products(): pl.pallas_call(slot_kernel, grid_spec=grid_spec, out_shape=jax.ShapeDtype...]
    ppermute x3, waiting for transfers between devices: 0.2 us -> 3.58 us  [exchange_rows(): lax.ppermute(mirrored, 'row', [(i, (i + shift) % size) for i in range(siz...]
    dynamic_update_slice x4 -> x0, local copies, waits for them, and re-layouts: 1.09 us -> none  [exchange_rows(): lax.dynamic_update_slice_in_dim(placed, block, source * width, axis=1)]
    ppermute x3, starting transfers between devices: 5.57 us -> 4.69 us  [exchange_rows(): lax.ppermute(mirrored, 'row', [(i, (i + shift) % size) for i in range(siz...]
    reshape x1, local copies, waits for them, and re-layouts: 1.27 us -> 0.46 us  [shards(): halves = summed.reshape(tiles_ab, 2, pair_count // cores, summed.shape[2])]
  transfers between devices with their start and end apart: 7 -> 6, of which waited for: 4 -> 3; matrix products, arithmetic and copies ran while one was open for 8% -> 6% of each run, Pallas kernels for 0% -> 0%
where the time goes in v11:
time: 66.7 us
  blocking collectives  35.7 us (54%)
  waiting for transfers between devices  8.74 us (13%)
  Pallas kernels  7.1 us (11%)
  starting transfers between devices  6.53 us (10%)
  local copies, waits for them, and re-layouts  4.35 us (7%)
  other arithmetic  2.58 us (4%)
  matrix products  0.88 us (1%)
  between operations  0.84 us (1%)
    all_to_all x1, blocking collectives, shards(): spread = lax.all_to_all(halves, CHIPS, 2, 2, tiled=True)  35.7 us
    pallas_call x1, Pallas kernels, slot_products(): pl.pallas_call(slot_kernel, grid_spec=grid_spec, out_shape=jax.ShapeDtype...  7.1 us
    ppermute x3, starting transfers between devices, exchange_rows(): lax.ppermute(mirrored, 'row', [(i, (i + shift) % size) for i in range(siz...  4.69 us
    ppermute x1, waiting for transfers between devices, shards(): before = lax.ppermute(amplitudes, TILE, up)  3.95 us
    ppermute x3, waiting for transfers between devices, exchange_rows(): lax.ppermute(mirrored, 'row', [(i, (i + shift) % size) for i in range(siz...  3.58 us
    ppermute x1, starting transfers between devices, shards(): after = lax.ppermute(amplitudes, TILE, down)  1.74 us
  transfers between devices with their start and end apart: 6, of which 3 were waited for; matrix products, arithmetic and copies ran while one was open for 6% of the time, Pallas kernels for 0%

profile of v11, /device:TPU:32, one launch (start us, length us, event | category | flops | bytes accessed | tf_op | source)
XLA Modules:
  0.0 66.7 jit_solution(8124689591647691176)
XLA Ops:
  0.0 1.7 %collective-permute-start.1 = (f32[9,64,256]{2,1,0:T(8,128)}, f32[9,64,256]{2,1,0:T(8,128)S(1)}, u32[]{:S(2)}, u32[]{:S(2)}) collective-permute-start(f32[9,64,256]{2,1,0:T(8,128)} %own_ref.1), channel_id=1, source_target_pairs={{4,0},{8,4},{12,8},{16,12},{20,16},{24,20},{28,24},{32,28},{36,32}... | collective-permute-start | bytes 1769480 | tf_op jit(solution)/shard_map/ppermute | solution.py:150
  1.8 0.8 %slice_bitcast_fusion = (s32[64]{0:T(128)S(1)}, s32[64]{0:T(128)S(1)}) fusion(s32[64,2]{0,1:T(2,128)} %param.11), kind=kLoop, calls=%fused_computation.42 | loop fusion | bytes 1024 | tf_op jit(solution)/shard_map/eq | solution.py:34
  2.5 0.2 select_reduce_fusion
  3.4 0.7 %gather_fusion.1 = s32[32]{0:T(128)S(1)} fusion(s32[64]{0:T(128)S(1)} %select_reduce_fusion, s32[1024]{0:T(1024)S(1)} %get-tuple-element.9), kind=kCustom, calls=%fused_computation.1 | custom fusion | bytes 384 | tf_op jit(solution)/shard_map/gather | solution.py:156
  4.1 0.7 %fusion.8 = s32[64]{0:T(128)S(1)} fusion(s32[1,64]{1,0:T(1,128)} %param.9, s32[]{:T(128)S(6)} %add.105), kind=kLoop, calls=%fused_computation.33 | loop fusion | flops 1728 | bytes 516 | tf_op jit(solution)/shard_map/add | solution.py:164
  4.8 0.7 %pad_add_fusion.index_ref = s32[128]{0:T(128)S(1)} fusion(s32[64]{0:T(128)} %bitcast.61, s32[64]{0:T(128)S(1)} %fusion.8), kind=kLoop, calls=%fused_computation.38 | loop fusion | flops 128 | bytes 1024 | tf_op jit(solution)/shard_map/concatenate | solution.py:164
  5.6 4.0 %collective-permute-done.before_ref = f32[9,64,256]{2,1,0:T(8,128)S(1)} collective-permute-done((f32[9,64,256]{2,1,0:T(8,128)}, f32[9,64,256]{2,1,0:T(8,128)S(1)}, u32[]{:S(2)}, u32[]{:S(2)}) %collective-permute-start) | collective-permute-done | bytes 589856 | tf_op jit(solution)/shard_map/ppermute | solution.py:149
  9.5 1.1 %copy-done = f32[9,64,256]{2,1,0:T(8,128)S(1)} copy-done((f32[9,64,256]{2,1,0:T(8,128)S(1)}, f32[9,64,256]{2,1,0:T(8,128)}, u32[]{:S(2)}) %copy-start) | copy-done | bytes 589848
  10.6 7.1 %shard_map.64 = f32[18,64,128]{2,1,0:T(8,128)S(1)} custom-call(s32[128]{0:T(128)S(1)} %pad_add_fusion.index_ref, s32[1]{0:T(128)} %bitcast.55.live_ref, f32[9,64,256]{2,1,0:T(8,128)S(1)} %collective-permute-done.before_ref, f32[9,64,256]{2,1,0:T(8,128)S(1)} %copy-done, f32[9,64,256]{2,1,0:T(8,128)S(1)} %collective-permute-done.1.after_ref, ...), custom_call_target="tpu_custom_call" | custom-call | flops 1610612736 | bytes 10747904 | tf_op jit(solution)/shard_map/pallas_call | solution.py:109
  17.7 0.4 convolution_bitcast_fusion
  18.1 0.1 collective-permute-start.2
  18.2 0.7 %gather_fusion = s32[32]{0:T(128)S(1)} fusion(s32[64]{0:T(128)S(1)} %select_reduce_fusion, s32[1024]{0:T(1024)S(1)} %get-tuple-element.10), kind=kCustom, calls=%fused_computation | custom fusion | bytes 384 | tf_op jit(solution)/shard_map/gather | solution.py:155
  19.0 1.2 %collective-permute-done.2 = f32[18,64,128]{2,1,0:T(8,128)S(1)} collective-permute-done((f32[18,64,128]{2,1,0:T(8,128)S(1)}, f32[18,64,128]{2,1,0:T(8,128)S(1)}, u32[]{:S(2)}, u32[]{:S(2)}) %collective-permute-start.2) | collective-permute-done | bytes 589856 | tf_op jit(solution)/shard_map/ppermute | solution.py:182
  20.2 0.4 fusion
  20.7 0.5 copy.20
  21.2 35.7 %all_to_all.5 = f32[18,2,32,128]{3,1,0,2:T(2,128)S(1)} all-to-all(f32[18,2,32,128]{3,1,0,2:T(2,128)S(1)} %copy.20), channel_id=1, replica_groups=mesh['x'=4,'z'=8,'c'=2,'row'=4] {'x','z'}, dimensions={2} | all-to-all | bytes 1179648 | tf_op jit(solution)/shard_map/all_to_all | solution.py:184
  56.8 0.2 reduce_sum.19
  57.1 0.1 reshape_broadcast_in_dim_squeeze.7
  57.2 0.1 reshape.57
  57.3 3.1 %collective-permute-start.3 = (f32[1,24,96]{2,1,0:T(8,128)S(1)}, f32[1,24,96]{2,1,0:T(8,128)S(1)}, u32[]{:S(2)}, u32[]{:S(2)}) collective-permute-start(f32[1,24,96]{2,1,0:T(8,128)S(1)} %reshape.57), channel_id=1, source_target_pairs={{0,3},{1,0},{2,1},{3,2},{4,7},{5,4},{6,5},{7,6},{8,11},{9,8},{10,9... | collective-permute-start | bytes 27656 | tf_op jit(solution)/shard_map/ppermute | solution.py:129
  60.5 0.1 collective-permute-start.5
  60.6 1.5 %collective-permute-start.4 = (f32[1,24,96]{2,1,0:T(8,128)S(1)}, f32[1,24,96]{2,1,0:T(8,128)S(1)}, u32[]{:S(2)}, u32[]{:S(2)}) collective-permute-start(f32[1,24,96]{2,1,0:T(8,128)S(1)} %reshape.57), channel_id=1, source_target_pairs={{0,2},{1,3},{2,0},{3,1},{4,6},{5,7},{6,4},{7,5},{8,10},{9,11},{10,... | collective-permute-start | bytes 27656 | tf_op jit(solution)/shard_map/ppermute | solution.py:129
  62.3 3.6 %collective-permute-done.4 = f32[1,24,96]{2,1,0:T(8,128)S(1)} collective-permute-done((f32[1,24,96]{2,1,0:T(8,128)S(1)}, f32[1,24,96]{2,1,0:T(8,128)S(1)}, u32[]{:S(2)}, u32[]{:S(2)}) %collective-permute-start.4) | collective-permute-done | bytes 9248 | tf_op jit(solution)/shard_map/ppermute | solution.py:129
  66.1 0.6 bitcast_add_fusion
  (28 shorter events, 0.7 us)
Async XLA Ops:
  0.0 9.5 %collective-permute-start = (f32[9,64,256]{2,1,0:T(8,128)}, f32[9,64,256]{2,1,0:T(8,128)S(1)}, u32[]{:S(2)}, u32[]{:S(2)}) collective-permute-start(f32[9,64,256]{2,1,0:T(8,128)} %own_ref.1), channel_id=1, source_target_pairs={{0,4},{4,8},{8,12},{12,16},{16,20},{20,24},{24,28},{28,32},{32,36}... | collective-permute-start | bytes 1769480 | tf_op jit(solution)/shard_map/ppermute | solution.py:149
  0.0 9.5 %collective-permute-start.1 = (f32[9,64,256]{2,1,0:T(8,128)}, f32[9,64,256]{2,1,0:T(8,128)S(1)}, u32[]{:S(2)}, u32[]{:S(2)}) collective-permute-start(f32[9,64,256]{2,1,0:T(8,128)} %own_ref.1), channel_id=1, source_target_pairs={{4,0},{8,4},{12,8},{16,12},{20,16},{24,20},{28,24},{32,28},{36,32}... | collective-permute-start | bytes 1769480 | tf_op jit(solution)/shard_map/ppermute | solution.py:150
  9.5 1.1 %copy-start = (f32[9,64,256]{2,1,0:T(8,128)S(1)}, f32[9,64,256]{2,1,0:T(8,128)}, u32[]{:S(2)}) copy-start(f32[9,64,256]{2,1,0:T(8,128)} %own_ref.1) | copy-start | bytes 1769476
  18.1 2.1 %collective-permute-start.2 = (f32[18,64,128]{2,1,0:T(8,128)S(1)}, f32[18,64,128]{2,1,0:T(8,128)S(1)}, u32[]{:S(2)}, u32[]{:S(2)}) collective-permute-start(f32[18,64,128]{2,1,0:T(8,128)S(1)} %convolution_bitcast_fusion), channel_id=1, source_target_pairs={{0,4},{4,0},{1,5},{5,1},{2,6},{6,2},{3,7},{7,3},{8,12},{12,8},{9,1... | collective-permute-start | bytes 1769480 | tf_op jit(solution)/shard_map/ppermute | solution.py:182
  57.3 5.0 %collective-permute-start.3 = (f32[1,24,96]{2,1,0:T(8,128)S(1)}, f32[1,24,96]{2,1,0:T(8,128)S(1)}, u32[]{:S(2)}, u32[]{:S(2)}) collective-permute-start(f32[1,24,96]{2,1,0:T(8,128)S(1)} %reshape.57), channel_id=1, source_target_pairs={{0,3},{1,0},{2,1},{3,2},{4,7},{5,4},{6,5},{7,6},{8,11},{9,8},{10,9... | collective-permute-start | bytes 27656 | tf_op jit(solution)/shard_map/ppermute | solution.py:129
  60.5 5.4 %collective-permute-start.5 = (f32[1,24,96]{2,1,0:T(8,128)S(1)}, f32[1,24,96]{2,1,0:T(8,128)S(1)}, u32[]{:S(2)}, u32[]{:S(2)}) collective-permute-start(f32[1,24,96]{2,1,0:T(8,128)S(1)} %reshape.57), channel_id=1, source_target_pairs={{0,1},{1,2},{2,3},{3,0},{4,5},{5,6},{6,7},{7,4},{8,9},{9,10},{10,1... | collective-permute-start | bytes 27656 | tf_op jit(solution)/shard_map/ppermute | solution.py:129
  60.6 5.3 %collective-permute-start.4 = (f32[1,24,96]{2,1,0:T(8,128)S(1)}, f32[1,24,96]{2,1,0:T(8,128)S(1)}, u32[]{:S(2)}, u32[]{:S(2)}) collective-permute-start(f32[1,24,96]{2,1,0:T(8,128)S(1)} %reshape.57), channel_id=1, source_target_pairs={{0,2},{1,3},{2,0},{3,1},{4,6},{5,7},{6,4},{7,5},{8,10},{9,11},{10,... | collective-permute-start | bytes 27656 | tf_op jit(solution)/shard_map/ppermute | solution.py:129

commit v12 on v11

--- a/solution.py
+++ b/solution.py
@@ -151,9 +151,7 @@
     mirror = find_mirror(pair_list)
     chips_of = jnp.arange(pair_count // cores, dtype=jnp.int32) * cores
     kept = chips_of + core
-    sent = chips_of + (cores - 1 - core)
     keep_rows = jnp.concatenate([kept, mirror[kept]])
-    send_rows = jnp.concatenate([sent, mirror[sent]])
     cd_global = slot_cd[0]
     owner_tile = cd_global // shard_tiles
     offset = (owner_tile - tile_index + 1 + tile_size) % tile_size
@@ -170,16 +168,15 @@
         tiles_ab,
     )
     pairs_axis = jnp.arange(pair_count, dtype=jnp.int32)[None, :]
-    pick = lambda rows: jnp.einsum(
+    pick = lambda rows, source: jnp.einsum(
         "qp,epb->eqb",
         (rows[:, None] == pairs_axis).astype(jnp.float32),
-        totals,
+        source,
         precision=lax.Precision.HIGHEST,
         preferred_element_type=jnp.float32,
     )
-    mine = pick(keep_rows)
-    other = pick(send_rows)
-    summed = mine + lax.ppermute(other, "c", [(0, 1), (1, 0)])
+    both_cores = totals + lax.ppermute(totals, "c", [(0, 1), (1, 0)])
+    summed = pick(keep_rows, both_cores)
     halves = summed.reshape(tiles_ab, 2, pair_count // cores, summed.shape[2])
     spread = lax.all_to_all(halves, CHIPS, 2, 2, tiled=True)
     reduced = jnp.sum(spread, axis=2)

time: 66.7 us -> 66.9 us (level)
  starting transfers between devices: 6.53 us -> 8.56 us
  local copies, waits for them, and re-layouts: 4.35 us -> 2.91 us
  blocking collectives: 35.7 us -> 34.6 us
  waiting for transfers between devices: 8.74 us -> 9.62 us
    ppermute x1, starting transfers between devices: 0.09 us -> 2.12 us  [shards(): both_cores = totals + lax.ppermute(totals, 'c', [(0, 1), (1, 0)])]
    ppermute x1, waiting for transfers between devices: 3.95 us -> 5.69 us  [shards(): before = lax.ppermute(amplitudes, TILE, up)]
    all_to_all x1, blocking collectives: 35.7 us -> 34.6 us  [shards(): spread = lax.all_to_all(halves, CHIPS, 2, 2, tiled=True)]
    eq x1, local copies, waits for them, and re-layouts: 0.76 us -> 0.01 us  [find_mirror(): first_orb[:, None] == second[None, :]]
    gather x1 -> x0, local copies, waits for them, and re-layouts: 0.7 us -> none  [shards(): send_rows = jnp.concatenate([sent, mirror[sent]])]
  transfers between devices with their start and end apart: 6 -> 6, of which waited for: 3 -> 4; matrix products, arithmetic and copies ran while one was open for 6% -> 4% of each run, Pallas kernels for 0% -> 0%
where the time goes in v12:
time: 66.9 us; the launch traced here: 66.5 us
  blocking collectives  34.6 us (52%)
  waiting for transfers between devices  9.62 us (14%)
  starting transfers between devices  8.56 us (13%)
  Pallas kernels  7.1 us (11%)
  local copies, waits for them, and re-layouts  2.91 us (4%)
  other arithmetic  2.49 us (4%)
  between operations  0.8 us (1%)
    all_to_all x1, blocking collectives, shards(): spread = lax.all_to_all(halves, CHIPS, 2, 2, tiled=True)  34.6 us
    pallas_call x1, Pallas kernels, slot_products(): pl.pallas_call(slot_kernel, grid_spec=grid_spec, out_shape=jax.ShapeDtype...  7.1 us
    ppermute x1, waiting for transfers between devices, shards(): before = lax.ppermute(amplitudes, TILE, up)  5.69 us
    ppermute x3, starting transfers between devices, exchange_rows(): lax.ppermute(mirrored, 'row', [(i, (i + shift) % size) for i in range(siz...  4.7 us
    ppermute x3, waiting for transfers between devices, exchange_rows(): lax.ppermute(mirrored, 'row', [(i, (i + shift) % size) for i in range(siz...  3.29 us
    ppermute x1, starting transfers between devices, shards(): both_cores = totals + lax.ppermute(totals, 'c', [(0, 1), (1, 0)])  2.12 us
    ppermute x1, starting transfers between devices, shards(): after = lax.ppermute(amplitudes, TILE, down)  1.74 us
  transfers between devices with their start and end apart: 6, of which 4 were waited for; matrix products, arithmetic and copies ran while one was open for 4% of the time, Pallas kernels for 0%

profile of v12, /device:TPU:32, one launch (start us, length us, event | category | flops | bytes accessed | tf_op | source)
XLA Modules:
  0.0 66.5 jit_solution(4142576826635597195)
XLA Ops:
  0.0 1.7 %collective-permute-start.1 = (f32[9,64,256]{2,1,0:T(8,128)}, f32[9,64,256]{2,1,0:T(8,128)S(1)}, u32[]{:S(2)}, u32[]{:S(2)}) collective-permute-start(f32[9,64,256]{2,1,0:T(8,128)} %own_ref.1), channel_id=1, source_target_pairs={{4,0},{8,4},{12,8},{16,12},{20,16},{24,20},{28,24},{32,28},{36,32}... | collective-permute-start | bytes 1769480 | tf_op jit(solution)/shard_map/ppermute | solution.py:150
  2.4 0.7 %fusion.6 = s32[64]{0:T(128)S(1)} fusion(s32[1,64]{1,0:T(1,128)} %param.9, s32[]{:T(128)S(6)} %add.81), kind=kLoop, calls=%fused_computation.26 | loop fusion | flops 1728 | bytes 516 | tf_op jit(solution)/shard_map/add | solution.py:162
  3.1 0.7 %pad_add_fusion.index_ref = s32[128]{0:T(128)S(1)} fusion(s32[64]{0:T(128)} %bitcast.50, s32[64]{0:T(128)S(1)} %fusion.6), kind=kLoop, calls=%fused_computation.30 | loop fusion | flops 128 | bytes 1024 | tf_op jit(solution)/shard_map/concatenate | solution.py:162
  3.8 5.7 %collective-permute-done.before_ref = f32[9,64,256]{2,1,0:T(8,128)S(1)} collective-permute-done((f32[9,64,256]{2,1,0:T(8,128)}, f32[9,64,256]{2,1,0:T(8,128)S(1)}, u32[]{:S(2)}, u32[]{:S(2)}) %collective-permute-start) | collective-permute-done | bytes 589856 | tf_op jit(solution)/shard_map/ppermute | solution.py:149
  9.5 1.1 %copy-done = f32[9,64,256]{2,1,0:T(8,128)S(1)} copy-done((f32[9,64,256]{2,1,0:T(8,128)S(1)}, f32[9,64,256]{2,1,0:T(8,128)}, u32[]{:S(2)}) %copy-start) | copy-done | bytes 589848
  10.6 7.1 %shard_map.64 = f32[18,64,128]{2,1,0:T(8,128)S(1)} custom-call(s32[128]{0:T(128)S(1)} %pad_add_fusion.index_ref, s32[1]{0:T(128)} %bitcast.44.live_ref, f32[9,64,256]{2,1,0:T(8,128)S(1)} %collective-permute-done.before_ref, f32[9,64,256]{2,1,0:T(8,128)S(1)} %copy-done, f32[9,64,256]{2,1,0:T(8,128)S(1)} %collective-permute-done.1.after_ref, ...), custom_call_target="tpu_custom_call" | custom-call | flops 1610612736 | bytes 10747904 | tf_op jit(solution)/shard_map/pallas_call | solution.py:109
  17.7 2.1 %collective-permute-start.2 = (f32[18,64,128]{2,1,0:T(8,128)S(1)}, f32[18,64,128]{2,1,0:T(8,128)S(1)}, u32[]{:S(2)}, u32[]{:S(2)}) collective-permute-start(f32[18,64,128]{2,1,0:T(8,128)S(1)} %shard_map.64), channel_id=1, source_target_pairs={{0,4},{4,0},{1,5},{5,1},{2,6},{6,2},{3,7},{7,3},{8,12},{12,8},{9,1... | collective-permute-start | bytes 1769480 | tf_op jit(solution)/shard_map/ppermute | solution.py:178
  19.8 0.2 select_reduce_fusion
  20.0 0.7 %gather_fusion = s32[32]{0:T(128)S(1)} fusion(s32[64]{0:T(128)S(1)} %select_reduce_fusion, s32[1024]{0:T(1024)S(1)} %pad_clamp_fusion), kind=kCustom, calls=%fused_computation | custom fusion | bytes 384 | tf_op jit(solution)/shard_map/gather | solution.py:154
  20.8 0.6 collective-permute-done.2
  21.4 0.4 fusion
  21.9 0.5 copy.20
  22.4 34.6 %all_to_all.5 = f32[18,2,32,128]{3,1,0,2:T(2,128)S(1)} all-to-all(f32[18,2,32,128]{3,1,0,2:T(2,128)S(1)} %copy.20), channel_id=1, replica_groups=mesh['x'=4,'z'=8,'c'=2,'row'=4] {'x','z'}, dimensions={2} | all-to-all | bytes 1179648 | tf_op jit(solution)/shard_map/all_to_all | solution.py:181
  57.0 0.2 reduce_sum.19
  57.2 0.1 reshape_broadcast_in_dim_squeeze.7
  57.3 0.1 reshape.43
  57.4 2.6 %collective-permute-start.3 = (f32[1,24,96]{2,1,0:T(8,128)S(1)}, f32[1,24,96]{2,1,0:T(8,128)S(1)}, u32[]{:S(2)}, u32[]{:S(2)}) collective-permute-start(f32[1,24,96]{2,1,0:T(8,128)S(1)} %reshape.43), channel_id=1, source_target_pairs={{0,3},{1,0},{2,1},{3,2},{4,7},{5,4},{6,5},{7,6},{8,11},{9,8},{10,9... | collective-permute-start | bytes 27656 | tf_op jit(solution)/shard_map/ppermute | solution.py:129
  60.0 0.8 %collective-permute-start.4 = (f32[1,24,96]{2,1,0:T(8,128)S(1)}, f32[1,24,96]{2,1,0:T(8,128)S(1)}, u32[]{:S(2)}, u32[]{:S(2)}) collective-permute-start(f32[1,24,96]{2,1,0:T(8,128)S(1)} %reshape.43), channel_id=1, source_target_pairs={{0,2},{1,3},{2,0},{3,1},{4,6},{5,7},{6,4},{7,5},{8,10},{9,11},{10,... | collective-permute-start | bytes 27656 | tf_op jit(solution)/shard_map/ppermute | solution.py:129
  60.8 1.3 %collective-permute-start.5 = (f32[1,24,96]{2,1,0:T(8,128)S(1)}, f32[1,24,96]{2,1,0:T(8,128)S(1)}, u32[]{:S(2)}, u32[]{:S(2)}) collective-permute-start(f32[1,24,96]{2,1,0:T(8,128)S(1)} %reshape.43), channel_id=1, source_target_pairs={{0,1},{1,2},{2,3},{3,0},{4,5},{5,6},{6,7},{7,4},{8,9},{9,10},{10,1... | collective-permute-start | bytes 27656 | tf_op jit(solution)/shard_map/ppermute | solution.py:129
  62.2 0.1 reshape_broadcast_in_dim_squeeze.6
  62.3 0.1 reshape.42
  62.4 2.7 %collective-permute-done.4 = f32[1,24,96]{2,1,0:T(8,128)S(1)} collective-permute-done((f32[1,24,96]{2,1,0:T(8,128)S(1)}, f32[1,24,96]{2,1,0:T(8,128)S(1)}, u32[]{:S(2)}, u32[]{:S(2)}) %collective-permute-start.4) | collective-permute-done | bytes 9248 | tf_op jit(solution)/shard_map/ppermute | solution.py:129
  65.2 0.5 collective-permute-done.5
  65.9 0.6 bitcast_add_fusion
  (25 shorter events, 0.5 us)
Async XLA Ops:
  0.0 19.8 %copy-start.1 = (s32[64,2]{0,1:T(2,128)S(1)}, s32[64,2]{0,1:T(2,128)}, u32[]{:S(2)}) copy-start(s32[64,2]{0,1:T(2,128)} %param.11) | copy-start | bytes 1540
  0.0 9.5 %collective-permute-start = (f32[9,64,256]{2,1,0:T(8,128)}, f32[9,64,256]{2,1,0:T(8,128)S(1)}, u32[]{:S(2)}, u32[]{:S(2)}) collective-permute-start(f32[9,64,256]{2,1,0:T(8,128)} %own_ref.1), channel_id=1, source_target_pairs={{0,4},{4,8},{8,12},{12,16},{16,20},{20,24},{24,28},{28,32},{32,36}... | collective-permute-start | bytes 1769480 | tf_op jit(solution)/shard_map/ppermute | solution.py:149
  0.0 9.5 %collective-permute-start.1 = (f32[9,64,256]{2,1,0:T(8,128)}, f32[9,64,256]{2,1,0:T(8,128)S(1)}, u32[]{:S(2)}, u32[]{:S(2)}) collective-permute-start(f32[9,64,256]{2,1,0:T(8,128)} %own_ref.1), channel_id=1, source_target_pairs={{4,0},{8,4},{12,8},{16,12},{20,16},{24,20},{28,24},{32,28},{36,32}... | collective-permute-start | bytes 1769480 | tf_op jit(solution)/shard_map/ppermute | solution.py:150
  9.5 1.1 %copy-start = (f32[9,64,256]{2,1,0:T(8,128)S(1)}, f32[9,64,256]{2,1,0:T(8,128)}, u32[]{:S(2)}) copy-start(f32[9,64,256]{2,1,0:T(8,128)} %own_ref.1) | copy-start | bytes 1769476
  17.7 3.7 %collective-permute-start.2 = (f32[18,64,128]{2,1,0:T(8,128)S(1)}, f32[18,64,128]{2,1,0:T(8,128)S(1)}, u32[]{:S(2)}, u32[]{:S(2)}) collective-permute-start(f32[18,64,128]{2,1,0:T(8,128)S(1)} %shard_map.64), channel_id=1, source_target_pairs={{0,4},{4,0},{1,5},{5,1},{2,6},{6,2},{3,7},{7,3},{8,12},{12,8},{9,1... | collective-permute-start | bytes 1769480 | tf_op jit(solution)/shard_map/ppermute | solution.py:178
  57.4 5.0 %collective-permute-start.3 = (f32[1,24,96]{2,1,0:T(8,128)S(1)}, f32[1,24,96]{2,1,0:T(8,128)S(1)}, u32[]{:S(2)}, u32[]{:S(2)}) collective-permute-start(f32[1,24,96]{2,1,0:T(8,128)S(1)} %reshape.43), channel_id=1, source_target_pairs={{0,3},{1,0},{2,1},{3,2},{4,7},{5,4},{6,5},{7,6},{8,11},{9,8},{10,9... | collective-permute-start | bytes 27656 | tf_op jit(solution)/shard_map/ppermute | solution.py:129
  60.0 5.2 %collective-permute-start.4 = (f32[1,24,96]{2,1,0:T(8,128)S(1)}, f32[1,24,96]{2,1,0:T(8,128)S(1)}, u32[]{:S(2)}, u32[]{:S(2)}) collective-permute-start(f32[1,24,96]{2,1,0:T(8,128)S(1)} %reshape.43), channel_id=1, source_target_pairs={{0,2},{1,3},{2,0},{3,1},{4,6},{5,7},{6,4},{7,5},{8,10},{9,11},{10,... | collective-permute-start | bytes 27656 | tf_op jit(solution)/shard_map/ppermute | solution.py:129
  60.8 4.9 %collective-permute-start.5 = (f32[1,24,96]{2,1,0:T(8,128)S(1)}, f32[1,24,96]{2,1,0:T(8,128)S(1)}, u32[]{:S(2)}, u32[]{:S(2)}) collective-permute-start(f32[1,24,96]{2,1,0:T(8,128)S(1)} %reshape.43), channel_id=1, source_target_pairs={{0,1},{1,2},{2,3},{3,0},{4,5},{5,6},{6,7},{7,4},{8,9},{9,10},{10,1... | collective-permute-start | bytes 27656 | tf_op jit(solution)/shard_map/ppermute | solution.py:129

commit v13 on v12

--- a/solution.py
+++ b/solution.py
@@ -10,7 +10,7 @@
 TS = 16
 ATS = 8
 SLAB = 96
-GROUP = 16
+GROUP = 32
 CHIPS = ("x", "z")
 TILE = ("x", "z", "c")
 

time: 66.9 us -> 66.6 us (level)
  blocking collectives: 34.6 us -> 28.7 us
  starting transfers between devices: 8.56 us -> 12.4 us
  waiting for transfers between devices: 9.62 us -> 10.6 us
    all_to_all x1, blocking collectives: 34.6 us -> 28.7 us  [shards(): spread = lax.all_to_all(halves, CHIPS, 2, 2, tiled=True)]
    ppermute x1, starting transfers between devices: 2.12 us -> 6.57 us  [shards(): both_cores = totals + lax.ppermute(totals, 'c', [(0, 1), (1, 0)])]
    ppermute x3, waiting for transfers between devices: 3.29 us -> 4.26 us  [exchange_rows(): lax.ppermute(mirrored, 'row', [(i, (i + shift) % size) for i in range(siz...]
  transfers between devices with their start and end apart: 6 -> 6, of which waited for: 4 -> 5; matrix products, arithmetic and copies ran while one was open for 4% -> 4% of each run, Pallas kernels for 0% -> 0%
where the time goes in v13:
time: 66.6 us; the launch traced here: 65.8 us
  blocking collectives  28.7 us (43%)
  starting transfers between devices  12.4 us (19%)
  waiting for transfers between devices  10.6 us (16%)
  Pallas kernels  7.53 us (11%)
  local copies, waits for them, and re-layouts  2.91 us (4%)
  other arithmetic  2.49 us (4%)
  between operations  0.79 us (1%)
    all_to_all x1, blocking collectives, shards(): spread = lax.all_to_all(halves, CHIPS, 2, 2, tiled=True)  28.7 us
    pallas_call x1, Pallas kernels, slot_products(): pl.pallas_call(slot_kernel, grid_spec=grid_spec, out_shape=jax.ShapeDtype...  7.53 us
    ppermute x1, starting transfers between devices, shards(): both_cores = totals + lax.ppermute(totals, 'c', [(0, 1), (1, 0)])  6.57 us
    ppermute x1, waiting for transfers between devices, shards(): before = lax.ppermute(amplitudes, TILE, up)  5.69 us
    ppermute x3, waiting for transfers between devices, exchange_rows(): lax.ppermute(mirrored, 'row', [(i, (i + shift) % size) for i in range(siz...  4.26 us
    ppermute x3, starting transfers between devices, exchange_rows(): lax.ppermute(mirrored, 'row', [(i, (i + shift) % size) for i in range(siz...  4.07 us
    ppermute x1, starting transfers between devices, shards(): after = lax.ppermute(amplitudes, TILE, down)  1.74 us
  transfers between devices with their start and end apart: 6, of which 5 were waited for; matrix products, arithmetic and copies ran while one was open for 4% of the time, Pallas kernels for 0%

profile of v13, /device:TPU:32, one launch (start us, length us, event | category | flops | bytes accessed | tf_op | source)
XLA Modules:
  0.0 65.8 jit_solution(6073119289842158636)
XLA Ops:
  0.0 1.7 %collective-permute-start.1 = (f32[9,64,256]{2,1,0:T(8,128)}, f32[9,64,256]{2,1,0:T(8,128)S(1)}, u32[]{:S(2)}, u32[]{:S(2)}) collective-permute-start(f32[9,64,256]{2,1,0:T(8,128)} %own_ref.1), channel_id=1, source_target_pairs={{4,0},{8,4},{12,8},{16,12},{20,16},{24,20},{28,24},{32,28},{36,32}... | collective-permute-start | bytes 1769480 | tf_op jit(solution)/shard_map/ppermute | solution.py:150
  2.4 0.7 %fusion.6 = s32[64]{0:T(128)S(1)} fusion(s32[1,64]{1,0:T(1,128)} %param.9, s32[]{:T(128)S(6)} %add.81), kind=kLoop, calls=%fused_computation.26 | loop fusion | flops 1728 | bytes 516 | tf_op jit(solution)/shard_map/add | solution.py:162
  3.1 0.7 %pad_add_fusion.index_ref = s32[128]{0:T(128)S(1)} fusion(s32[64]{0:T(128)} %bitcast.50, s32[64]{0:T(128)S(1)} %fusion.6), kind=kLoop, calls=%fused_computation.30 | loop fusion | flops 128 | bytes 1024 | tf_op jit(solution)/shard_map/concatenate | solution.py:162
  3.8 5.7 %collective-permute-done.before_ref = f32[9,64,256]{2,1,0:T(8,128)S(1)} collective-permute-done((f32[9,64,256]{2,1,0:T(8,128)}, f32[9,64,256]{2,1,0:T(8,128)S(1)}, u32[]{:S(2)}, u32[]{:S(2)}) %collective-permute-start) | collective-permute-done | bytes 589856 | tf_op jit(solution)/shard_map/ppermute | solution.py:149
  9.5 1.1 %copy-done = f32[9,64,256]{2,1,0:T(8,128)S(1)} copy-done((f32[9,64,256]{2,1,0:T(8,128)S(1)}, f32[9,64,256]{2,1,0:T(8,128)}, u32[]{:S(2)}) %copy-start) | copy-done | bytes 589848
  10.6 7.5 %shard_map.64 = f32[18,64,128]{2,1,0:T(8,128)S(1)} custom-call(s32[128]{0:T(128)S(1)} %pad_add_fusion.index_ref, s32[1]{0:T(128)} %bitcast.44.live_ref, f32[9,64,256]{2,1,0:T(8,128)S(1)} %collective-permute-done.before_ref, f32[9,64,256]{2,1,0:T(8,128)S(1)} %copy-done, f32[9,64,256]{2,1,0:T(8,128)S(1)} %collective-permute-done.1.after_ref, ...), custom_call_target="tpu_custom_call" | custom-call | flops 1610612736 | bytes 10747904 | tf_op jit(solution)/shard_map/pallas_call | solution.py:109
  18.1 6.6 %collective-permute-start.2 = (f32[18,64,128]{2,1,0:T(8,128)S(1)}, f32[18,64,128]{2,1,0:T(8,128)S(1)}, u32[]{:S(2)}, u32[]{:S(2)}) collective-permute-start(f32[18,64,128]{2,1,0:T(8,128)S(1)} %shard_map.64), channel_id=1, source_target_pairs={{0,4},{4,0},{1,5},{5,1},{2,6},{6,2},{3,7},{7,3},{8,12},{12,8},{9,1... | collective-permute-start | bytes 1769480 | tf_op jit(solution)/shard_map/ppermute | solution.py:178
  24.7 0.2 select_reduce_fusion
  24.9 0.7 %gather_fusion = s32[32]{0:T(128)S(1)} fusion(s32[64]{0:T(128)S(1)} %select_reduce_fusion, s32[1024]{0:T(1024)S(1)} %pad_clamp_fusion), kind=kCustom, calls=%fused_computation | custom fusion | bytes 384 | tf_op jit(solution)/shard_map/gather | solution.py:154
  25.7 0.6 collective-permute-done.2
  26.3 0.4 fusion
  26.8 0.5 copy.20
  27.2 28.7 %all_to_all.5 = f32[18,2,32,128]{3,1,0,2:T(2,128)S(1)} all-to-all(f32[18,2,32,128]{3,1,0,2:T(2,128)S(1)} %copy.20), channel_id=1, replica_groups=mesh['x'=4,'z'=8,'c'=2,'row'=4] {'x','z'}, dimensions={2} | all-to-all | bytes 1179648 | tf_op jit(solution)/shard_map/all_to_all | solution.py:181
  55.9 0.2 reduce_sum.19
  56.2 0.1 reshape_broadcast_in_dim_squeeze.7
  56.3 0.1 reshape.43
  56.4 3.1 %collective-permute-start.3 = (f32[1,24,96]{2,1,0:T(8,128)S(1)}, f32[1,24,96]{2,1,0:T(8,128)S(1)}, u32[]{:S(2)}, u32[]{:S(2)}) collective-permute-start(f32[1,24,96]{2,1,0:T(8,128)S(1)} %reshape.43), channel_id=1, source_target_pairs={{0,3},{1,0},{2,1},{3,2},{4,7},{5,4},{6,5},{7,6},{8,11},{9,8},{10,9... | collective-permute-start | bytes 27656 | tf_op jit(solution)/shard_map/ppermute | solution.py:129
  59.5 0.6 collective-permute-start.4
  60.1 0.3 collective-permute-start.5
  60.5 0.1 reshape_broadcast_in_dim_squeeze.6
  60.7 0.1 collective-permute-done.3
  60.9 3.8 %collective-permute-done.4 = f32[1,24,96]{2,1,0:T(8,128)S(1)} collective-permute-done((f32[1,24,96]{2,1,0:T(8,128)S(1)}, f32[1,24,96]{2,1,0:T(8,128)S(1)}, u32[]{:S(2)}, u32[]{:S(2)}) %collective-permute-start.4) | collective-permute-done | bytes 9248 | tf_op jit(solution)/shard_map/ppermute | solution.py:129
  64.7 0.3 collective-permute-done.5
  65.2 0.6 bitcast_add_fusion
  (25 shorter events, 0.5 us)
Async XLA Ops:
  0.0 24.7 %copy-start.1 = (s32[64,2]{0,1:T(2,128)S(1)}, s32[64,2]{0,1:T(2,128)}, u32[]{:S(2)}) copy-start(s32[64,2]{0,1:T(2,128)} %param.11) | copy-start | bytes 1540
  0.0 9.5 %collective-permute-start = (f32[9,64,256]{2,1,0:T(8,128)}, f32[9,64,256]{2,1,0:T(8,128)S(1)}, u32[]{:S(2)}, u32[]{:S(2)}) collective-permute-start(f32[9,64,256]{2,1,0:T(8,128)} %own_ref.1), channel_id=1, source_target_pairs={{0,4},{4,8},{8,12},{12,16},{16,20},{20,24},{24,28},{28,32},{32,36}... | collective-permute-start | bytes 1769480 | tf_op jit(solution)/shard_map/ppermute | solution.py:149
  0.0 9.5 %collective-permute-start.1 = (f32[9,64,256]{2,1,0:T(8,128)}, f32[9,64,256]{2,1,0:T(8,128)S(1)}, u32[]{:S(2)}, u32[]{:S(2)}) collective-permute-start(f32[9,64,256]{2,1,0:T(8,128)} %own_ref.1), channel_id=1, source_target_pairs={{4,0},{8,4},{12,8},{16,12},{20,16},{24,20},{28,24},{32,28},{36,32}... | collective-permute-start | bytes 1769480 | tf_op jit(solution)/shard_map/ppermute | solution.py:150
  9.5 1.1 %copy-start = (f32[9,64,256]{2,1,0:T(8,128)S(1)}, f32[9,64,256]{2,1,0:T(8,128)}, u32[]{:S(2)}) copy-start(f32[9,64,256]{2,1,0:T(8,128)} %own_ref.1) | copy-start | bytes 1769476
  18.1 8.2 %collective-permute-start.2 = (f32[18,64,128]{2,1,0:T(8,128)S(1)}, f32[18,64,128]{2,1,0:T(8,128)S(1)}, u32[]{:S(2)}, u32[]{:S(2)}) collective-permute-start(f32[18,64,128]{2,1,0:T(8,128)S(1)} %shard_map.64), channel_id=1, source_target_pairs={{0,4},{4,0},{1,5},{5,1},{2,6},{6,2},{3,7},{7,3},{8,12},{12,8},{9,1... | collective-permute-start | bytes 1769480 | tf_op jit(solution)/shard_map/ppermute | solution.py:178
  56.4 4.5 %collective-permute-start.3 = (f32[1,24,96]{2,1,0:T(8,128)S(1)}, f32[1,24,96]{2,1,0:T(8,128)S(1)}, u32[]{:S(2)}, u32[]{:S(2)}) collective-permute-start(f32[1,24,96]{2,1,0:T(8,128)S(1)} %reshape.43), channel_id=1, source_target_pairs={{0,3},{1,0},{2,1},{3,2},{4,7},{5,4},{6,5},{7,6},{8,11},{9,8},{10,9... | collective-permute-start | bytes 27656 | tf_op jit(solution)/shard_map/ppermute | solution.py:129
  59.5 5.2 %collective-permute-start.4 = (f32[1,24,96]{2,1,0:T(8,128)S(1)}, f32[1,24,96]{2,1,0:T(8,128)S(1)}, u32[]{:S(2)}, u32[]{:S(2)}) collective-permute-start(f32[1,24,96]{2,1,0:T(8,128)S(1)} %reshape.43), channel_id=1, source_target_pairs={{0,2},{1,3},{2,0},{3,1},{4,6},{5,7},{6,4},{7,5},{8,10},{9,11},{10,... | collective-permute-start | bytes 27656 | tf_op jit(solution)/shard_map/ppermute | solution.py:129
  60.1 4.9 %collective-permute-start.5 = (f32[1,24,96]{2,1,0:T(8,128)S(1)}, f32[1,24,96]{2,1,0:T(8,128)S(1)}, u32[]{:S(2)}, u32[]{:S(2)}) collective-permute-start(f32[1,24,96]{2,1,0:T(8,128)S(1)} %reshape.43), channel_id=1, source_target_pairs={{0,1},{1,2},{2,3},{3,0},{4,5},{5,6},{6,7},{7,4},{8,9},{9,10},{10,1... | collective-permute-start | bytes 27656 | tf_op jit(solution)/shard_map/ppermute | solution.py:129

commit v14 on v12

--- a/solution.py
+++ b/solution.py
@@ -64,8 +64,8 @@
         for j in range(GROUP):
             slot = step * GROUP + j
             product = lax.dot_general(
+                block_ref[j],
                 amp_ref[index_ref[slot]],
-                block_ref[j],
                 (((1,), (1,)), ((), ())),
                 precision=lax.Precision.HIGHEST,
                 preferred_element_type=jnp.float32,
@@ -89,7 +89,7 @@
         return (jnp.minimum(i, last), 0, 0)
 
     whole = lambda shape: pl.BlockSpec(shape, lambda i, *_: (0,) * len(shape))
-    out_shape = (tiles_ab, pairs, block_width)
+    out_shape = (tiles_ab, block_width, pairs)
     grid_spec = pltpu.PrefetchScalarGridSpec(
         num_scalar_prefetch=2,
         grid=(steps,),
@@ -102,7 +102,7 @@
         out_specs=whole(out_shape),
         scratch_shapes=[
             pltpu.VMEM((3 * own.shape[0],) + own.shape[1:], jnp.float32),
-            pltpu.VMEM((tiles_ab, pairs, block_width), jnp.float32),
+            pltpu.VMEM((tiles_ab, block_width, pairs), jnp.float32),
             pltpu.SemaphoreType.DMA((1,)),
         ],
     )
@@ -169,7 +169,7 @@
     )
     pairs_axis = jnp.arange(pair_count, dtype=jnp.int32)[None, :]
     pick = lambda rows, source: jnp.einsum(
-        "qp,epb->eqb",
+        "qp,ebp->eqb",
         (rows[:, None] == pairs_axis).astype(jnp.float32),
         source,
         precision=lax.Precision.HIGHEST,

time: 66.9 us -> 66.2 us (0.990)
  Pallas kernels: 7.1 us -> 4.45 us
  blocking collectives: 34.6 us -> 35.5 us
  local copies, waits for them, and re-layouts: 2.91 us -> 3.63 us
    pallas_call x1, Pallas kernels: 7.1 us -> 4.45 us  [slot_products(): pl.pallas_call(slot_kernel, grid_spec=grid_spec, out_shape=jax.ShapeDtype...]
    all_to_all x1, blocking collectives: 34.6 us -> 35.5 us  [shards(): spread = lax.all_to_all(halves, CHIPS, 2, 2, tiled=True)]
where the time goes in v14:
time: 66.2 us; the launch traced here: 65.9 us
  blocking collectives  35.5 us (54%)
  waiting for transfers between devices  10.2 us (15%)
  starting transfers between devices  7.99 us (12%)
  Pallas kernels  4.45 us (7%)
  local copies, waits for them, and re-layouts  3.63 us (5%)
  other arithmetic  2.49 us (4%)
  matrix products  0.88 us (1%)
  between operations  0.83 us (1%)
    all_to_all x1, blocking collectives, shards(): spread = lax.all_to_all(halves, CHIPS, 2, 2, tiled=True)  35.5 us
    ppermute x1, waiting for transfers between devices, shards(): before = lax.ppermute(amplitudes, TILE, up)  5.69 us
    pallas_call x1, Pallas kernels, slot_products(): pl.pallas_call(slot_kernel, grid_spec=grid_spec, out_shape=jax.ShapeDtype...  4.45 us
    ppermute x3, starting transfers between devices, exchange_rows(): lax.ppermute(mirrored, 'row', [(i, (i + shift) % size) for i in range(siz...  4.13 us
    ppermute x3, waiting for transfers between devices, exchange_rows(): lax.ppermute(mirrored, 'row', [(i, (i + shift) % size) for i in range(siz...  3.85 us
    ppermute x1, starting transfers between devices, shards(): both_cores = totals + lax.ppermute(totals, 'c', [(0, 1), (1, 0)])  2.11 us
    ppermute x1, starting transfers between devices, shards(): after = lax.ppermute(amplitudes, TILE, down)  1.74 us
  transfers between devices with their start and end apart: 6, of which 4 were waited for; matrix products, arithmetic and copies ran while one was open for 4% of the time, Pallas kernels for 0%

profile of v14, /device:TPU:32, one launch (start us, length us, event | category | flops | bytes accessed | tf_op | source)
XLA Modules:
  0.0 65.9 jit_solution(2604594502494057298)
XLA Ops:
  0.0 1.7 %collective-permute-start.1 = (f32[9,64,256]{2,1,0:T(8,128)}, f32[9,64,256]{2,1,0:T(8,128)S(1)}, u32[]{:S(2)}, u32[]{:S(2)}) collective-permute-start(f32[9,64,256]{2,1,0:T(8,128)} %own_ref.1), channel_id=1, source_target_pairs={{4,0},{8,4},{12,8},{16,12},{20,16},{24,20},{28,24},{32,28},{36,32}... | collective-permute-start | bytes 1769480 | tf_op jit(solution)/shard_map/ppermute | solution.py:150
  2.4 0.7 %fusion.6 = s32[64]{0:T(128)S(1)} fusion(s32[1,64]{1,0:T(1,128)} %param.9, s32[]{:T(128)S(6)} %add.81), kind=kLoop, calls=%fused_computation.26 | loop fusion | flops 1728 | bytes 516 | tf_op jit(solution)/shard_map/add | solution.py:162
  3.1 0.7 %pad_add_fusion.index_ref = s32[128]{0:T(128)S(1)} fusion(s32[64]{0:T(128)} %bitcast.50, s32[64]{0:T(128)S(1)} %fusion.6), kind=kLoop, calls=%fused_computation.30 | loop fusion | flops 128 | bytes 1024 | tf_op jit(solution)/shard_map/concatenate | solution.py:162
  3.8 5.7 %collective-permute-done.before_ref = f32[9,64,256]{2,1,0:T(8,128)S(1)} collective-permute-done((f32[9,64,256]{2,1,0:T(8,128)}, f32[9,64,256]{2,1,0:T(8,128)S(1)}, u32[]{:S(2)}, u32[]{:S(2)}) %collective-permute-start) | collective-permute-done | bytes 589856 | tf_op jit(solution)/shard_map/ppermute | solution.py:149
  9.5 1.1 %copy-done = f32[9,64,256]{2,1,0:T(8,128)S(1)} copy-done((f32[9,64,256]{2,1,0:T(8,128)S(1)}, f32[9,64,256]{2,1,0:T(8,128)}, u32[]{:S(2)}) %copy-start) | copy-done | bytes 589848
  10.6 4.5 %shard_map.64 = f32[18,128,64]{2,1,0:T(8,128)S(1)} custom-call(s32[128]{0:T(128)S(1)} %pad_add_fusion.index_ref, s32[1]{0:T(128)} %bitcast.44.live_ref, f32[9,64,256]{2,1,0:T(8,128)S(1)} %collective-permute-done.before_ref, f32[9,64,256]{2,1,0:T(8,128)S(1)} %copy-done, f32[9,64,256]{2,1,0:T(8,128)S(1)} %collective-permute-done.1.after_ref, ...), custom_call_target="tpu_custom_call" | custom-call | flops 1610612736 | bytes 10747904 | tf_op jit(solution)/shard_map/pallas_call | solution.py:109
  15.1 0.3 copy.33
  15.4 2.1 %collective-permute-start.2 = (f32[18,128,64]{1,2,0:T(8,128)S(1)}, f32[18,128,64]{1,2,0:T(8,128)S(1)}, u32[]{:S(2)}, u32[]{:S(2)}) collective-permute-start(f32[18,128,64]{1,2,0:T(8,128)S(1)} %copy.33), channel_id=1, source_target_pairs={{0,4},{4,0},{1,5},{5,1},{2,6},{6,2},{3,7},{7,3},{8,12},{12,8},{9,1... | collective-permute-start | bytes 1769480 | tf_op jit(solution)/shard_map/ppermute | solution.py:178
  17.6 0.2 select_reduce_fusion
  17.7 0.7 %gather_fusion = s32[32]{0:T(128)S(1)} fusion(s32[64]{0:T(128)S(1)} %select_reduce_fusion, s32[1024]{0:T(1024)S(1)} %pad_clamp_fusion), kind=kCustom, calls=%fused_computation | custom fusion | bytes 384 | tf_op jit(solution)/shard_map/gather | solution.py:154
  18.5 0.6 collective-permute-done.2
  19.2 0.4 copy.34
  19.5 0.9 %fusion = f32[18,128,64]{1,2,0:T(8,128)S(1)} fusion(f32[18,128,64]{2,1,0:T(8,128)S(1)} %shard_map.64, f32[18,128,64]{2,1,0:T(8,128)S(1)} %copy.34, s32[64]{0:T(128)S(1)} %pad_add_fusion.1), kind=kOutput, calls=%fused_computation.1 | convolution fusion | flops 113397760 | bytes 1769728 | tf_op jit(solution)/shard_map/qp,ebp->eqb/dot_general | solution.py:171
  20.4 0.5 copy.36
  20.9 35.5 %all_to_all.5 = f32[18,2,32,128]{3,1,0,2:T(2,128)S(1)} all-to-all(f32[18,2,32,128]{3,1,0,2:T(2,128)S(1)} %copy.36), channel_id=1, replica_groups=mesh['x'=4,'z'=8,'c'=2,'row'=4] {'x','z'}, dimensions={2} | all-to-all | bytes 1179648 | tf_op jit(solution)/shard_map/all_to_all | solution.py:181
  56.4 0.2 reduce_sum.19
  56.6 0.1 reshape_broadcast_in_dim_squeeze.7
  56.7 0.1 reshape.43
  56.8 3.1 %collective-permute-start.3 = (f32[1,24,96]{2,1,0:T(8,128)S(1)}, f32[1,24,96]{2,1,0:T(8,128)S(1)}, u32[]{:S(2)}, u32[]{:S(2)}) collective-permute-start(f32[1,24,96]{2,1,0:T(8,128)S(1)} %reshape.43), channel_id=1, source_target_pairs={{0,3},{1,0},{2,1},{3,2},{4,7},{5,4},{6,5},{7,6},{8,11},{9,8},{10,9... | collective-permute-start | bytes 27656 | tf_op jit(solution)/shard_map/ppermute | solution.py:129
  59.9 1.0 %collective-permute-start.5 = (f32[1,24,96]{2,1,0:T(8,128)S(1)}, f32[1,24,96]{2,1,0:T(8,128)S(1)}, u32[]{:S(2)}, u32[]{:S(2)}) collective-permute-start(f32[1,24,96]{2,1,0:T(8,128)S(1)} %reshape.43), channel_id=1, source_target_pairs={{0,1},{1,2},{2,3},{3,0},{4,5},{5,6},{6,7},{7,4},{8,9},{9,10},{10,1... | collective-permute-start | bytes 27656 | tf_op jit(solution)/shard_map/ppermute | solution.py:129
  61.0 0.1 reshape_broadcast_in_dim_squeeze.6
  61.2 0.1 reshape.42
  61.3 3.8 %collective-permute-done.4 = f32[1,24,96]{2,1,0:T(8,128)S(1)} collective-permute-done((f32[1,24,96]{2,1,0:T(8,128)S(1)}, f32[1,24,96]{2,1,0:T(8,128)S(1)}, u32[]{:S(2)}, u32[]{:S(2)}) %collective-permute-start.4) | collective-permute-done | bytes 9248 | tf_op jit(solution)/shard_map/ppermute | solution.py:129
  65.3 0.6 bitcast_add_fusion
  (27 shorter events, 0.5 us)
Async XLA Ops:
  0.0 9.5 %collective-permute-start = (f32[9,64,256]{2,1,0:T(8,128)}, f32[9,64,256]{2,1,0:T(8,128)S(1)}, u32[]{:S(2)}, u32[]{:S(2)}) collective-permute-start(f32[9,64,256]{2,1,0:T(8,128)} %own_ref.1), channel_id=1, source_target_pairs={{0,4},{4,8},{8,12},{12,16},{16,20},{20,24},{24,28},{28,32},{32,36}... | collective-permute-start | bytes 1769480 | tf_op jit(solution)/shard_map/ppermute | solution.py:149
  0.0 9.5 %collective-permute-start.1 = (f32[9,64,256]{2,1,0:T(8,128)}, f32[9,64,256]{2,1,0:T(8,128)S(1)}, u32[]{:S(2)}, u32[]{:S(2)}) collective-permute-start(f32[9,64,256]{2,1,0:T(8,128)} %own_ref.1), channel_id=1, source_target_pairs={{4,0},{8,4},{12,8},{16,12},{20,16},{24,20},{28,24},{32,28},{36,32}... | collective-permute-start | bytes 1769480 | tf_op jit(solution)/shard_map/ppermute | solution.py:150
  9.5 1.1 %copy-start = (f32[9,64,256]{2,1,0:T(8,128)S(1)}, f32[9,64,256]{2,1,0:T(8,128)}, u32[]{:S(2)}) copy-start(f32[9,64,256]{2,1,0:T(8,128)} %own_ref.1) | copy-start | bytes 1769476
  15.0 2.5 %copy-start.1 = (s32[64,2]{0,1:T(2,128)S(1)}, s32[64,2]{0,1:T(2,128)}, u32[]{:S(2)}) copy-start(s32[64,2]{0,1:T(2,128)} %param.11) | copy-start | bytes 1540
  15.4 3.7 %collective-permute-start.2 = (f32[18,128,64]{1,2,0:T(8,128)S(1)}, f32[18,128,64]{1,2,0:T(8,128)S(1)}, u32[]{:S(2)}, u32[]{:S(2)}) collective-permute-start(f32[18,128,64]{1,2,0:T(8,128)S(1)} %copy.33), channel_id=1, source_target_pairs={{0,4},{4,0},{1,5},{5,1},{2,6},{6,2},{3,7},{7,3},{8,12},{12,8},{9,1... | collective-permute-start | bytes 1769480 | tf_op jit(solution)/shard_map/ppermute | solution.py:178
  56.8 4.5 %collective-permute-start.3 = (f32[1,24,96]{2,1,0:T(8,128)S(1)}, f32[1,24,96]{2,1,0:T(8,128)S(1)}, u32[]{:S(2)}, u32[]{:S(2)}) collective-permute-start(f32[1,24,96]{2,1,0:T(8,128)S(1)} %reshape.43), channel_id=1, source_target_pairs={{0,3},{1,0},{2,1},{3,2},{4,7},{5,4},{6,5},{7,6},{8,11},{9,8},{10,9... | collective-permute-start | bytes 27656 | tf_op jit(solution)/shard_map/ppermute | solution.py:129
  59.9 5.2 %collective-permute-start.4 = (f32[1,24,96]{2,1,0:T(8,128)S(1)}, f32[1,24,96]{2,1,0:T(8,128)S(1)}, u32[]{:S(2)}, u32[]{:S(2)}) collective-permute-start(f32[1,24,96]{2,1,0:T(8,128)S(1)} %reshape.43), channel_id=1, source_target_pairs={{0,2},{1,3},{2,0},{3,1},{4,6},{5,7},{6,4},{7,5},{8,10},{9,11},{10,... | collective-permute-start | bytes 27656 | tf_op jit(solution)/shard_map/ppermute | solution.py:129
  59.9 5.2 %collective-permute-start.5 = (f32[1,24,96]{2,1,0:T(8,128)S(1)}, f32[1,24,96]{2,1,0:T(8,128)S(1)}, u32[]{:S(2)}, u32[]{:S(2)}) collective-permute-start(f32[1,24,96]{2,1,0:T(8,128)S(1)} %reshape.43), channel_id=1, source_target_pairs={{0,1},{1,2},{2,3},{3,0},{4,5},{5,6},{6,7},{7,4},{8,9},{9,10},{10,1... | collective-permute-start | bytes 27656 | tf_op jit(solution)/shard_map/ppermute | solution.py:129

commit v15 on v14

--- a/solution.py
+++ b/solution.py
@@ -10,7 +10,7 @@
 TS = 16
 ATS = 8
 SLAB = 96
-GROUP = 16
+GROUP = 32
 CHIPS = ("x", "z")
 TILE = ("x", "z", "c")
 

time: 66.2 us -> 66.7 us (level)
  blocking collectives: 35.5 us -> 32.3 us
  Pallas kernels: 4.45 us -> 6.62 us
  waiting for transfers between devices: 10.2 us -> 10.9 us
    all_to_all x1, blocking collectives: 35.5 us -> 32.3 us  [shards(): spread = lax.all_to_all(halves, CHIPS, 2, 2, tiled=True)]
    pallas_call x1, Pallas kernels: 4.45 us -> 6.62 us  [slot_products(): pl.pallas_call(slot_kernel, grid_spec=grid_spec, out_shape=jax.ShapeDtype...]
    ppermute x3, waiting for transfers between devices: 3.85 us -> 4.58 us  [exchange_rows(): lax.ppermute(mirrored, 'row', [(i, (i + shift) % size) for i in range(siz...]
where the time goes in v15:
time: 66.7 us; the launch traced here: 66.2 us
  blocking collectives  32.3 us (48%)
  waiting for transfers between devices  10.9 us (16%)
  starting transfers between devices  8.49 us (13%)
  Pallas kernels  6.62 us (10%)
  local copies, waits for them, and re-layouts  3.62 us (5%)
  other arithmetic  2.49 us (4%)
  matrix products  0.88 us (1%)
  between operations  0.83 us (1%)
    all_to_all x1, blocking collectives, shards(): spread = lax.all_to_all(halves, CHIPS, 2, 2, tiled=True)  32.3 us
    pallas_call x1, Pallas kernels, slot_products(): pl.pallas_call(slot_kernel, grid_spec=grid_spec, out_shape=jax.ShapeDtype...  6.62 us
    ppermute x1, waiting for transfers between devices, shards(): before = lax.ppermute(amplitudes, TILE, up)  5.69 us
    ppermute x3, starting transfers between devices, exchange_rows(): lax.ppermute(mirrored, 'row', [(i, (i + shift) % size) for i in range(siz...  4.63 us
    ppermute x3, waiting for transfers between devices, exchange_rows(): lax.ppermute(mirrored, 'row', [(i, (i + shift) % size) for i in range(siz...  4.58 us
    ppermute x1, starting transfers between devices, shards(): both_cores = totals + lax.ppermute(totals, 'c', [(0, 1), (1, 0)])  2.12 us
    ppermute x1, starting transfers between devices, shards(): after = lax.ppermute(amplitudes, TILE, down)  1.74 us
  transfers between devices with their start and end apart: 6, of which 4 were waited for; matrix products, arithmetic and copies ran while one was open for 4% of the time, Pallas kernels for 0%

profile of v15, /device:TPU:32, one launch (start us, length us, event | category | flops | bytes accessed | tf_op | source)
XLA Modules:
  0.0 66.2 jit_solution(6226107283842360558)
XLA Ops:
  0.0 1.7 %collective-permute-start.1 = (f32[9,64,256]{2,1,0:T(8,128)}, f32[9,64,256]{2,1,0:T(8,128)S(1)}, u32[]{:S(2)}, u32[]{:S(2)}) collective-permute-start(f32[9,64,256]{2,1,0:T(8,128)} %own_ref.1), channel_id=1, source_target_pairs={{4,0},{8,4},{12,8},{16,12},{20,16},{24,20},{28,24},{32,28},{36,32}... | collective-permute-start | bytes 1769480 | tf_op jit(solution)/shard_map/ppermute | solution.py:150
  2.4 0.7 %fusion.6 = s32[64]{0:T(128)S(1)} fusion(s32[1,64]{1,0:T(1,128)} %param.9, s32[]{:T(128)S(6)} %add.81), kind=kLoop, calls=%fused_computation.26 | loop fusion | flops 1728 | bytes 516 | tf_op jit(solution)/shard_map/add | solution.py:162
  3.1 0.7 %pad_add_fusion.index_ref = s32[128]{0:T(128)S(1)} fusion(s32[64]{0:T(128)} %bitcast.50, s32[64]{0:T(128)S(1)} %fusion.6), kind=kLoop, calls=%fused_computation.30 | loop fusion | flops 128 | bytes 1024 | tf_op jit(solution)/shard_map/concatenate | solution.py:162
  3.8 5.7 %collective-permute-done.before_ref = f32[9,64,256]{2,1,0:T(8,128)S(1)} collective-permute-done((f32[9,64,256]{2,1,0:T(8,128)}, f32[9,64,256]{2,1,0:T(8,128)S(1)}, u32[]{:S(2)}, u32[]{:S(2)}) %collective-permute-start) | collective-permute-done | bytes 589856 | tf_op jit(solution)/shard_map/ppermute | solution.py:149
  9.5 1.1 %copy-done = f32[9,64,256]{2,1,0:T(8,128)S(1)} copy-done((f32[9,64,256]{2,1,0:T(8,128)S(1)}, f32[9,64,256]{2,1,0:T(8,128)}, u32[]{:S(2)}) %copy-start) | copy-done | bytes 589848
  10.6 6.6 %shard_map.64 = f32[18,128,64]{2,1,0:T(8,128)S(1)} custom-call(s32[128]{0:T(128)S(1)} %pad_add_fusion.index_ref, s32[1]{0:T(128)} %bitcast.44.live_ref, f32[9,64,256]{2,1,0:T(8,128)S(1)} %collective-permute-done.before_ref, f32[9,64,256]{2,1,0:T(8,128)S(1)} %copy-done, f32[9,64,256]{2,1,0:T(8,128)S(1)} %collective-permute-done.1.after_ref, ...), custom_call_target="tpu_custom_call" | custom-call | flops 1610612736 | bytes 10747904 | tf_op jit(solution)/shard_map/pallas_call | solution.py:109
  17.2 0.3 copy.33
  17.6 2.1 %collective-permute-start.2 = (f32[18,128,64]{1,2,0:T(8,128)S(1)}, f32[18,128,64]{1,2,0:T(8,128)S(1)}, u32[]{:S(2)}, u32[]{:S(2)}) collective-permute-start(f32[18,128,64]{1,2,0:T(8,128)S(1)} %copy.33), channel_id=1, source_target_pairs={{0,4},{4,0},{1,5},{5,1},{2,6},{6,2},{3,7},{7,3},{8,12},{12,8},{9,1... | collective-permute-start | bytes 1769480 | tf_op jit(solution)/shard_map/ppermute | solution.py:178
  19.7 0.2 select_reduce_fusion
  19.9 0.7 %gather_fusion = s32[32]{0:T(128)S(1)} fusion(s32[64]{0:T(128)S(1)} %select_reduce_fusion, s32[1024]{0:T(1024)S(1)} %pad_clamp_fusion), kind=kCustom, calls=%fused_computation | custom fusion | bytes 384 | tf_op jit(solution)/shard_map/gather | solution.py:154
  20.7 0.6 collective-permute-done.2
  21.3 0.4 copy.34
  21.7 0.9 %fusion = f32[18,128,64]{1,2,0:T(8,128)S(1)} fusion(f32[18,128,64]{2,1,0:T(8,128)S(1)} %shard_map.64, f32[18,128,64]{2,1,0:T(8,128)S(1)} %copy.34, s32[64]{0:T(128)S(1)} %pad_add_fusion.1), kind=kOutput, calls=%fused_computation.1 | convolution fusion | flops 113397760 | bytes 1769728 | tf_op jit(solution)/shard_map/qp,ebp->eqb/dot_general | solution.py:171
  22.6 0.5 copy.36
  23.1 32.3 %all_to_all.5 = f32[18,2,32,128]{3,1,0,2:T(2,128)S(1)} all-to-all(f32[18,2,32,128]{3,1,0,2:T(2,128)S(1)} %copy.36), channel_id=1, replica_groups=mesh['x'=4,'z'=8,'c'=2,'row'=4] {'x','z'}, dimensions={2} | all-to-all | bytes 1179648 | tf_op jit(solution)/shard_map/all_to_all | solution.py:181
  55.4 0.2 reduce_sum.19
  55.6 0.1 reshape_broadcast_in_dim_squeeze.7
  55.7 0.1 reshape.43
  55.8 2.9 %collective-permute-start.3 = (f32[1,24,96]{2,1,0:T(8,128)S(1)}, f32[1,24,96]{2,1,0:T(8,128)S(1)}, u32[]{:S(2)}, u32[]{:S(2)}) collective-permute-start(f32[1,24,96]{2,1,0:T(8,128)S(1)} %reshape.43), channel_id=1, source_target_pairs={{0,3},{1,0},{2,1},{3,2},{4,7},{5,4},{6,5},{7,6},{8,11},{9,8},{10,9... | collective-permute-start | bytes 27656 | tf_op jit(solution)/shard_map/ppermute | solution.py:129
  58.7 1.7 %collective-permute-start.4 = (f32[1,24,96]{2,1,0:T(8,128)S(1)}, f32[1,24,96]{2,1,0:T(8,128)S(1)}, u32[]{:S(2)}, u32[]{:S(2)}) collective-permute-start(f32[1,24,96]{2,1,0:T(8,128)S(1)} %reshape.43), channel_id=1, source_target_pairs={{0,2},{1,3},{2,0},{3,1},{4,6},{5,7},{6,4},{7,5},{8,10},{9,11},{10,... | collective-permute-start | bytes 27656 | tf_op jit(solution)/shard_map/ppermute | solution.py:129
  60.5 0.1 reshape_broadcast_in_dim_squeeze.6
  60.8 3.2 %collective-permute-done.4 = f32[1,24,96]{2,1,0:T(8,128)S(1)} collective-permute-done((f32[1,24,96]{2,1,0:T(8,128)S(1)}, f32[1,24,96]{2,1,0:T(8,128)S(1)}, u32[]{:S(2)}, u32[]{:S(2)}) %collective-permute-start.4) | collective-permute-done | bytes 9248 | tf_op jit(solution)/shard_map/ppermute | solution.py:129
  63.9 1.4 %collective-permute-done.5 = f32[1,24,96]{2,1,0:T(8,128)S(1)} collective-permute-done((f32[1,24,96]{2,1,0:T(8,128)S(1)}, f32[1,24,96]{2,1,0:T(8,128)S(1)}, u32[]{:S(2)}, u32[]{:S(2)}) %collective-permute-start.5) | collective-permute-done | bytes 9248 | tf_op jit(solution)/shard_map/ppermute | solution.py:129
  65.5 0.6 bitcast_add_fusion
  (27 shorter events, 0.5 us)
Async XLA Ops:
  0.0 9.5 %collective-permute-start = (f32[9,64,256]{2,1,0:T(8,128)}, f32[9,64,256]{2,1,0:T(8,128)S(1)}, u32[]{:S(2)}, u32[]{:S(2)}) collective-permute-start(f32[9,64,256]{2,1,0:T(8,128)} %own_ref.1), channel_id=1, source_target_pairs={{0,4},{4,8},{8,12},{12,16},{16,20},{20,24},{24,28},{28,32},{32,36}... | collective-permute-start | bytes 1769480 | tf_op jit(solution)/shard_map/ppermute | solution.py:149
  0.0 9.5 %collective-permute-start.1 = (f32[9,64,256]{2,1,0:T(8,128)}, f32[9,64,256]{2,1,0:T(8,128)S(1)}, u32[]{:S(2)}, u32[]{:S(2)}) collective-permute-start(f32[9,64,256]{2,1,0:T(8,128)} %own_ref.1), channel_id=1, source_target_pairs={{4,0},{8,4},{12,8},{16,12},{20,16},{24,20},{28,24},{32,28},{36,32}... | collective-permute-start | bytes 1769480 | tf_op jit(solution)/shard_map/ppermute | solution.py:150
  9.5 1.1 %copy-start = (f32[9,64,256]{2,1,0:T(8,128)S(1)}, f32[9,64,256]{2,1,0:T(8,128)}, u32[]{:S(2)}) copy-start(f32[9,64,256]{2,1,0:T(8,128)} %own_ref.1) | copy-start | bytes 1769476
  17.2 2.5 %copy-start.1 = (s32[64,2]{0,1:T(2,128)S(1)}, s32[64,2]{0,1:T(2,128)}, u32[]{:S(2)}) copy-start(s32[64,2]{0,1:T(2,128)} %param.11) | copy-start | bytes 1540
  17.6 3.7 %collective-permute-start.2 = (f32[18,128,64]{1,2,0:T(8,128)S(1)}, f32[18,128,64]{1,2,0:T(8,128)S(1)}, u32[]{:S(2)}, u32[]{:S(2)}) collective-permute-start(f32[18,128,64]{1,2,0:T(8,128)S(1)} %copy.33), channel_id=1, source_target_pairs={{0,4},{4,0},{1,5},{5,1},{2,6},{6,2},{3,7},{7,3},{8,12},{12,8},{9,1... | collective-permute-start | bytes 1769480 | tf_op jit(solution)/shard_map/ppermute | solution.py:178
  55.8 4.9 %collective-permute-start.3 = (f32[1,24,96]{2,1,0:T(8,128)S(1)}, f32[1,24,96]{2,1,0:T(8,128)S(1)}, u32[]{:S(2)}, u32[]{:S(2)}) collective-permute-start(f32[1,24,96]{2,1,0:T(8,128)S(1)} %reshape.43), channel_id=1, source_target_pairs={{0,3},{1,0},{2,1},{3,2},{4,7},{5,4},{6,5},{7,6},{8,11},{9,8},{10,9... | collective-permute-start | bytes 27656 | tf_op jit(solution)/shard_map/ppermute | solution.py:129
  58.7 5.2 %collective-permute-start.4 = (f32[1,24,96]{2,1,0:T(8,128)S(1)}, f32[1,24,96]{2,1,0:T(8,128)S(1)}, u32[]{:S(2)}, u32[]{:S(2)}) collective-permute-start(f32[1,24,96]{2,1,0:T(8,128)S(1)} %reshape.43), channel_id=1, source_target_pairs={{0,2},{1,3},{2,0},{3,1},{4,6},{5,7},{6,4},{7,5},{8,10},{9,11},{10,... | collective-permute-start | bytes 27656 | tf_op jit(solution)/shard_map/ppermute | solution.py:129
  60.5 4.9 %collective-permute-start.5 = (f32[1,24,96]{2,1,0:T(8,128)S(1)}, f32[1,24,96]{2,1,0:T(8,128)S(1)}, u32[]{:S(2)}, u32[]{:S(2)}) collective-permute-start(f32[1,24,96]{2,1,0:T(8,128)S(1)} %reshape.43), channel_id=1, source_target_pairs={{0,1},{1,2},{2,3},{3,0},{4,5},{5,6},{6,7},{7,4},{8,9},{9,10},{10,1... | collective-permute-start | bytes 27656 | tf_op jit(solution)/shard_map/ppermute | solution.py:129

commit v16 on v15

--- a/solution.py
+++ b/solution.py
@@ -10,7 +10,7 @@
 TS = 16
 ATS = 8
 SLAB = 96
-GROUP = 32
+GROUP = 8
 CHIPS = ("x", "z")
 TILE = ("x", "z", "c")
 

time: 66.7 us -> 68 us (1.019)
  Pallas kernels: 6.62 us -> 4.4 us
  starting transfers between devices: 8.49 us -> 10.7 us
  blocking collectives: 32.3 us -> 34.5 us
    pallas_call x1, Pallas kernels: 6.62 us -> 4.4 us  [slot_products(): pl.pallas_call(slot_kernel, grid_spec=grid_spec, out_shape=jax.ShapeDtype...]
    all_to_all x1, blocking collectives: 32.3 us -> 34.5 us  [shards(): spread = lax.all_to_all(halves, CHIPS, 2, 2, tiled=True)]
    ppermute x1, starting transfers between devices: 2.12 us -> 3.29 us  [shards(): both_cores = totals + lax.ppermute(totals, 'c', [(0, 1), (1, 0)])]
    ppermute x3, starting transfers between devices: 4.63 us -> 5.64 us  [exchange_rows(): lax.ppermute(mirrored, 'row', [(i, (i + shift) % size) for i in range(siz...]
where the time goes in v16:
time: 68 us; the launch traced here: 67.7 us
  blocking collectives  34.5 us (51%)
  starting transfers between devices  10.7 us (16%)
  waiting for transfers between devices  10.3 us (15%)
  Pallas kernels  4.4 us (6%)
  local copies, waits for them, and re-layouts  3.62 us (5%)
  other arithmetic  2.49 us (4%)
  matrix products  0.88 us (1%)
  between operations  0.83 us (1%)
    all_to_all x1, blocking collectives, shards(): spread = lax.all_to_all(halves, CHIPS, 2, 2, tiled=True)  34.5 us
    ppermute x1, waiting for transfers between devices, shards(): before = lax.ppermute(amplitudes, TILE, up)  5.69 us
    ppermute x3, starting transfers between devices, exchange_rows(): lax.ppermute(mirrored, 'row', [(i, (i + shift) % size) for i in range(siz...  5.64 us
    pallas_call x1, Pallas kernels, slot_products(): pl.pallas_call(slot_kernel, grid_spec=grid_spec, out_shape=jax.ShapeDtype...  4.4 us
    ppermute x3, waiting for transfers between devices, exchange_rows(): lax.ppermute(mirrored, 'row', [(i, (i + shift) % size) for i in range(siz...  3.95 us
    ppermute x1, starting transfers between devices, shards(): both_cores = totals + lax.ppermute(totals, 'c', [(0, 1), (1, 0)])  3.29 us
    ppermute x1, starting transfers between devices, shards(): after = lax.ppermute(amplitudes, TILE, down)  1.74 us
  transfers between devices with their start and end apart: 6, of which 4 were waited for; matrix products, arithmetic and copies ran while one was open for 4% of the time, Pallas kernels for 0%

profile of v16, /device:TPU:32, one launch (start us, length us, event | category | flops | bytes accessed | tf_op | source)
XLA Modules:
  0.0 67.7 jit_solution(18072869372063269481)
XLA Ops:
  0.0 1.7 %collective-permute-start.1 = (f32[9,64,256]{2,1,0:T(8,128)}, f32[9,64,256]{2,1,0:T(8,128)S(1)}, u32[]{:S(2)}, u32[]{:S(2)}) collective-permute-start(f32[9,64,256]{2,1,0:T(8,128)} %own_ref.1), channel_id=1, source_target_pairs={{4,0},{8,4},{12,8},{16,12},{20,16},{24,20},{28,24},{32,28},{36,32}... | collective-permute-start | bytes 1769480 | tf_op jit(solution)/shard_map/ppermute | solution.py:150
  2.4 0.7 %fusion.6 = s32[64]{0:T(128)S(1)} fusion(s32[1,64]{1,0:T(1,128)} %param.9, s32[]{:T(128)S(6)} %add.81), kind=kLoop, calls=%fused_computation.26 | loop fusion | flops 1728 | bytes 516 | tf_op jit(solution)/shard_map/add | solution.py:162
  3.1 0.7 %pad_add_fusion.index_ref = s32[128]{0:T(128)S(1)} fusion(s32[64]{0:T(128)} %bitcast.50, s32[64]{0:T(128)S(1)} %fusion.6), kind=kLoop, calls=%fused_computation.30 | loop fusion | flops 128 | bytes 1024 | tf_op jit(solution)/shard_map/concatenate | solution.py:162
  3.8 5.7 %collective-permute-done.before_ref = f32[9,64,256]{2,1,0:T(8,128)S(1)} collective-permute-done((f32[9,64,256]{2,1,0:T(8,128)}, f32[9,64,256]{2,1,0:T(8,128)S(1)}, u32[]{:S(2)}, u32[]{:S(2)}) %collective-permute-start) | collective-permute-done | bytes 589856 | tf_op jit(solution)/shard_map/ppermute | solution.py:149
  9.5 1.1 %copy-done = f32[9,64,256]{2,1,0:T(8,128)S(1)} copy-done((f32[9,64,256]{2,1,0:T(8,128)S(1)}, f32[9,64,256]{2,1,0:T(8,128)}, u32[]{:S(2)}) %copy-start) | copy-done | bytes 589848
  10.6 4.4 %shard_map.64 = f32[18,128,64]{2,1,0:T(8,128)S(1)} custom-call(s32[128]{0:T(128)S(1)} %pad_add_fusion.index_ref, s32[1]{0:T(128)} %bitcast.44.live_ref, f32[9,64,256]{2,1,0:T(8,128)S(1)} %collective-permute-done.before_ref, f32[9,64,256]{2,1,0:T(8,128)S(1)} %copy-done, f32[9,64,256]{2,1,0:T(8,128)S(1)} %collective-permute-done.1.after_ref, ...), custom_call_target="tpu_custom_call" | custom-call | flops 1610612736 | bytes 10747904 | tf_op jit(solution)/shard_map/pallas_call | solution.py:109
  15.0 0.3 copy.33
  15.4 3.3 %collective-permute-start.2 = (f32[18,128,64]{1,2,0:T(8,128)S(1)}, f32[18,128,64]{1,2,0:T(8,128)S(1)}, u32[]{:S(2)}, u32[]{:S(2)}) collective-permute-start(f32[18,128,64]{1,2,0:T(8,128)S(1)} %copy.33), channel_id=1, source_target_pairs={{0,4},{4,0},{1,5},{5,1},{2,6},{6,2},{3,7},{7,3},{8,12},{12,8},{9,1... | collective-permute-start | bytes 1769480 | tf_op jit(solution)/shard_map/ppermute | solution.py:178
  18.7 0.2 select_reduce_fusion
  18.9 0.7 %gather_fusion = s32[32]{0:T(128)S(1)} fusion(s32[64]{0:T(128)S(1)} %select_reduce_fusion, s32[1024]{0:T(1024)S(1)} %pad_clamp_fusion), kind=kCustom, calls=%fused_computation | custom fusion | bytes 384 | tf_op jit(solution)/shard_map/gather | solution.py:154
  19.6 0.6 collective-permute-done.2
  20.3 0.4 copy.34
  20.7 0.9 %fusion = f32[18,128,64]{1,2,0:T(8,128)S(1)} fusion(f32[18,128,64]{2,1,0:T(8,128)S(1)} %shard_map.64, f32[18,128,64]{2,1,0:T(8,128)S(1)} %copy.34, s32[64]{0:T(128)S(1)} %pad_add_fusion.1), kind=kOutput, calls=%fused_computation.1 | convolution fusion | flops 113397760 | bytes 1769728 | tf_op jit(solution)/shard_map/qp,ebp->eqb/dot_general | solution.py:171
  21.5 0.5 copy.36
  22.0 34.5 %all_to_all.5 = f32[18,2,32,128]{3,1,0,2:T(2,128)S(1)} all-to-all(f32[18,2,32,128]{3,1,0,2:T(2,128)S(1)} %copy.36), channel_id=1, replica_groups=mesh['x'=4,'z'=8,'c'=2,'row'=4] {'x','z'}, dimensions={2} | all-to-all | bytes 1179648 | tf_op jit(solution)/shard_map/all_to_all | solution.py:181
  56.5 0.2 reduce_sum.19
  56.7 0.1 reshape_broadcast_in_dim_squeeze.7
  56.9 1.8 %collective-permute-start.3 = (f32[1,24,96]{2,1,0:T(8,128)S(1)}, f32[1,24,96]{2,1,0:T(8,128)S(1)}, u32[]{:S(2)}, u32[]{:S(2)}) collective-permute-start(f32[1,24,96]{2,1,0:T(8,128)S(1)} %reshape.43), channel_id=1, source_target_pairs={{0,3},{1,0},{2,1},{3,2},{4,7},{5,4},{6,5},{7,6},{8,11},{9,8},{10,9... | collective-permute-start | bytes 27656 | tf_op jit(solution)/shard_map/ppermute | solution.py:129
  58.7 3.2 %collective-permute-start.4 = (f32[1,24,96]{2,1,0:T(8,128)S(1)}, f32[1,24,96]{2,1,0:T(8,128)S(1)}, u32[]{:S(2)}, u32[]{:S(2)}) collective-permute-start(f32[1,24,96]{2,1,0:T(8,128)S(1)} %reshape.43), channel_id=1, source_target_pairs={{0,2},{1,3},{2,0},{3,1},{4,6},{5,7},{6,4},{7,5},{8,10},{9,11},{10,... | collective-permute-start | bytes 27656 | tf_op jit(solution)/shard_map/ppermute | solution.py:129
  61.9 0.6 collective-permute-start.5
  62.7 0.1 reshape_broadcast_in_dim_squeeze.6
  62.9 1.0 %collective-permute-done.4 = f32[1,24,96]{2,1,0:T(8,128)S(1)} collective-permute-done((f32[1,24,96]{2,1,0:T(8,128)S(1)}, f32[1,24,96]{2,1,0:T(8,128)S(1)}, u32[]{:S(2)}, u32[]{:S(2)}) %collective-permute-start.4) | collective-permute-done | bytes 9248 | tf_op jit(solution)/shard_map/ppermute | solution.py:129
  63.9 2.9 %collective-permute-done.5 = f32[1,24,96]{2,1,0:T(8,128)S(1)} collective-permute-done((f32[1,24,96]{2,1,0:T(8,128)S(1)}, f32[1,24,96]{2,1,0:T(8,128)S(1)}, u32[]{:S(2)}, u32[]{:S(2)}) %collective-permute-start.5) | collective-permute-done | bytes 9248 | tf_op jit(solution)/shard_map/ppermute | solution.py:129
  67.0 0.6 bitcast_add_fusion
  (27 shorter events, 0.6 us)
Async XLA Ops:
  0.0 9.5 %collective-permute-start = (f32[9,64,256]{2,1,0:T(8,128)}, f32[9,64,256]{2,1,0:T(8,128)S(1)}, u32[]{:S(2)}, u32[]{:S(2)}) collective-permute-start(f32[9,64,256]{2,1,0:T(8,128)} %own_ref.1), channel_id=1, source_target_pairs={{0,4},{4,8},{8,12},{12,16},{16,20},{20,24},{24,28},{28,32},{32,36}... | collective-permute-start | bytes 1769480 | tf_op jit(solution)/shard_map/ppermute | solution.py:149
  0.0 9.5 %collective-permute-start.1 = (f32[9,64,256]{2,1,0:T(8,128)}, f32[9,64,256]{2,1,0:T(8,128)S(1)}, u32[]{:S(2)}, u32[]{:S(2)}) collective-permute-start(f32[9,64,256]{2,1,0:T(8,128)} %own_ref.1), channel_id=1, source_target_pairs={{4,0},{8,4},{12,8},{16,12},{20,16},{24,20},{28,24},{32,28},{36,32}... | collective-permute-start | bytes 1769480 | tf_op jit(solution)/shard_map/ppermute | solution.py:150
  9.5 1.1 %copy-start = (f32[9,64,256]{2,1,0:T(8,128)S(1)}, f32[9,64,256]{2,1,0:T(8,128)}, u32[]{:S(2)}) copy-start(f32[9,64,256]{2,1,0:T(8,128)} %own_ref.1) | copy-start | bytes 1769476
  15.0 3.7 %copy-start.1 = (s32[64,2]{0,1:T(2,128)S(1)}, s32[64,2]{0,1:T(2,128)}, u32[]{:S(2)}) copy-start(s32[64,2]{0,1:T(2,128)} %param.11) | copy-start | bytes 1540
  15.4 4.9 %collective-permute-start.2 = (f32[18,128,64]{1,2,0:T(8,128)S(1)}, f32[18,128,64]{1,2,0:T(8,128)S(1)}, u32[]{:S(2)}, u32[]{:S(2)}) collective-permute-start(f32[18,128,64]{1,2,0:T(8,128)S(1)} %copy.33), channel_id=1, source_target_pairs={{0,4},{4,0},{1,5},{5,1},{2,6},{6,2},{3,7},{7,3},{8,12},{12,8},{9,1... | collective-permute-start | bytes 1769480 | tf_op jit(solution)/shard_map/ppermute | solution.py:178
  56.9 5.9 %collective-permute-start.3 = (f32[1,24,96]{2,1,0:T(8,128)S(1)}, f32[1,24,96]{2,1,0:T(8,128)S(1)}, u32[]{:S(2)}, u32[]{:S(2)}) collective-permute-start(f32[1,24,96]{2,1,0:T(8,128)S(1)} %reshape.43), channel_id=1, source_target_pairs={{0,3},{1,0},{2,1},{3,2},{4,7},{5,4},{6,5},{7,6},{8,11},{9,8},{10,9... | collective-permute-start | bytes 27656 | tf_op jit(solution)/shard_map/ppermute | solution.py:129
  58.7 5.2 %collective-permute-start.4 = (f32[1,24,96]{2,1,0:T(8,128)S(1)}, f32[1,24,96]{2,1,0:T(8,128)S(1)}, u32[]{:S(2)}, u32[]{:S(2)}) collective-permute-start(f32[1,24,96]{2,1,0:T(8,128)S(1)} %reshape.43), channel_id=1, source_target_pairs={{0,2},{1,3},{2,0},{3,1},{4,6},{5,7},{6,4},{7,5},{8,10},{9,11},{10,... | collective-permute-start | bytes 27656 | tf_op jit(solution)/shard_map/ppermute | solution.py:129
  61.9 4.9 %collective-permute-start.5 = (f32[1,24,96]{2,1,0:T(8,128)S(1)}, f32[1,24,96]{2,1,0:T(8,128)S(1)}, u32[]{:S(2)}, u32[]{:S(2)}) collective-permute-start(f32[1,24,96]{2,1,0:T(8,128)S(1)} %reshape.43), channel_id=1, source_target_pairs={{0,1},{1,2},{2,3},{3,0},{4,5},{5,6},{6,7},{7,4},{8,9},{9,10},{10,1... | collective-permute-start | bytes 27656 | tf_op jit(solution)/shard_map/ppermute | solution.py:129
